TPU v7x, 32 devices: a whole 2x2x4 slice. The times are simulated.
32 devices in a mesh: row: 8 (over z, y), col: 4 (over x, core).
Axes of the slice: x: 2, y: 2, z: 4, core: 2. Of those that a mesh axis runs over, the one named last changes fastest.
Arguments:
- gram: float32 [16384, 16384], P('row', 'col'), may hold values from -1 to 17, as said below
Outputs:
- factored: float32 [16384, 16384], P('row', 'col')
Inputs may be any that keep to these rules, and one draw needn't show every extreme that they name: gram holds a symmetric positive definite matrix in the block-cyclic order of the steps.
All inputs are finite; a program needn't handle non-finite values.
Results may differ from a plain program's by a relative error of at most 0.0001.
Values sent between devices are 32-bit elements; how exact they have to be, the bound alone decides.
No kernel may reach another device: no remote copies, remote signals or barrier semaphores. Data moves between devices by JAX's collectives and lax.ppermute only.
A program may use at most 192 MiB of HBM per device.

v0:
```python
import jax
import jax.numpy as jnp
from jax import lax
from jax.sharding import PartitionSpec as P

NB = 512
STEPS = 2


def broadcast(value, axis, source):
    kept = jnp.where(lax.axis_index(axis) == source, value, 0).astype(value.dtype)
    return lax.psum(kept, axis)


def from_partner(block, axis, apart):
    count = lax.axis_size(axis)
    route = []
    for low in range(count):
        high = low | 1 << apart
        if high != low and high < count:
            route += [(low, high), (high, low)]
    return lax.ppermute(block, axis, route)


def global_index(count, block, grid, position):
    ladder = jnp.arange(count, dtype=jnp.int32)
    return (ladder // block * grid + position) * block + ladder % block


def times_transposed(left, right):
    return lax.dot_general(
        left,
        right,
        (((1,), (1,)), ((), ())),
        precision=lax.Precision.HIGHEST,
        preferred_element_type=jnp.float32,
    )


def local(gram):
    grid_rows = lax.axis_size("row")
    grid_cols = lax.axis_size("col")
    row_id = lax.axis_index("row")
    col_id = lax.axis_index("col")
    rblock = NB * grid_cols // grid_rows
    per_class = grid_rows // grid_cols
    local_rows = gram.shape[0]
    local_cols = gram.shape[1]
    blocks = local_rows // rblock
    grows = global_index(local_rows, rblock, grid_rows, row_id)
    gcols = global_index(local_cols, NB, grid_cols, col_id)
    member = row_id % per_class
    row_class = row_id // per_class
    identity = jnp.eye(NB, dtype=jnp.float32)

    def factor_panel(matrix, panel_index):
        owner_col = panel_index % grid_cols
        local_block = panel_index // grid_cols
        end_row = panel_index * NB + NB
        column = matrix[:, local_block * NB : (local_block + 1) * NB]
        square = column[local_block * rblock : (local_block + 1) * rblock]
        is_owner = col_id == owner_col
        in_class = row_class == owner_col
        select = (jnp.arange(per_class, dtype=jnp.int32) == member).astype(jnp.float32)
        weight = jnp.where(is_owner & in_class, 1.0, 0.0).astype(jnp.float32)
        placed = (select[:, None, None] * square[None]).reshape(NB, NB) * weight
        diagonal = lax.psum(placed, "row")
        diagonal = jnp.where(is_owner, diagonal, identity)
        low_factor = jnp.linalg.cholesky(diagonal)
        inverse = jax.scipy.linalg.solve_triangular(low_factor, identity, lower=True)
        solved = times_transposed(column, inverse)
        trailing = jnp.where((grows >= end_row)[:, None], solved, 0.0)
        rows_diag = lax.dynamic_slice_in_dim(low_factor, member * rblock, rblock, 0)
        previous = trailing[local_block * rblock : (local_block + 1) * rblock]
        patched = jnp.where(in_class, rows_diag, previous)
        factored = trailing.at[local_block * rblock : (local_block + 1) * rblock].set(patched)
        new_column = jnp.where(is_owner, factored, column)
        matrix = matrix.at[:, local_block * NB : (local_block + 1) * NB].set(new_column)
        return (matrix, trailing)

    matrix = gram
    for panel_index in range(STEPS):
        matrix, trailing = factor_panel(matrix, panel_index)
        spread_owner_col = panel_index % grid_cols
        spread_rows_all = broadcast(trailing, "col", spread_owner_col)
        pieces = spread_rows_all.reshape(grid_cols, blocks // grid_cols * rblock, NB)
        shift_bits = per_class.bit_length() - 1
        for bit_level in reversed(range(grid_cols.bit_length() - 1)):
            halfway = pieces.shape[0] // 2
            own_bit = row_class >> bit_level & 1
            wanted = col_id >> bit_level & 1
            upper = own_bit == 1
            retained = jnp.where(upper, pieces[halfway:], pieces[:halfway])
            outgoing = jnp.where(upper, pieces[:halfway], pieces[halfway:])
            received = from_partner(outgoing, "row", shift_bits + bit_level)
            pieces = jnp.where(own_bit == wanted, retained, received)
        gathered = lax.all_gather(pieces[0], "row", axis=0, tiled=True)
        spread_columns = gathered.reshape(grid_cols, per_class, blocks // grid_cols, rblock, NB)
        spread_columns = jnp.transpose(spread_columns, (0, 2, 1, 3, 4)).reshape(local_cols, NB)
        first_row = panel_index * NB
        apply_end_row = first_row + NB
        current = matrix
        updated = current - times_transposed(spread_rows_all, spread_columns)
        panel_rows = (grows >= first_row) & (grows < apply_end_row)
        beyond = gcols >= apply_end_row
        updated = jnp.where(panel_rows[:, None] & beyond[None, :], 0.0, updated)
        matrix = matrix.at[:, 0:local_cols].set(updated)
    matrix, trailing = factor_panel(matrix, STEPS)
    return matrix


def solution(mesh):
    placed = (P("row", "col"),)
    return jax.shard_map(
        local, mesh=mesh, in_specs=placed, out_specs=P("row", "col"), check_vma=False
    )
```

profile of v0, /device:TPU:25, one launch (start us, length us, event | category | flops | bytes accessed | tf_op | source)
XLA Modules:
  0.0 1540.0 jit_solution(489001765417519902)
XLA Ops:
  6.5 23.0 %copy.106 = f32[2048,4096]{1,0:T(8,128)} copy(f32[2048,4096]{1,0:T(8,128)} %param.24) | data formatting | bytes 67108864
  32.8 77.2 %all-reduce.7.cloned.1.call-done = f32[512,512]{0,1:T(8,128)} async-done(((f32[512,512]{0,1:T(8,128)}), f32[512,512]{0,1:T(8,128)}) %all-reduce.7.cloned.1.call-update) | async-done | bytes 1048592 | tf_op jit(solution)/shard_map/psum | solution.py:67
  112.9 11.7 cholesky.374
  135.3 11.7 cholesky.393
  157.7 11.7 cholesky.414
  179.8 11.7 cholesky.431
  206.2 39.3 %custom-call.34 = f32[4,128,128]{1,2,0:T(8,128)S(1)} custom-call(f32[4,128,128]{2,1,0:T(8,128)S(1)} %get-tuple-element.139), custom_call_target="InvertDiagBlocksLowerTriangular" | custom-call | tf_op jit(solution)/shard_map/jit(_solve_triangular)/triangular_solve | solution.py:70
  250.3 10.6 broadcast_select_fusion.1
  261.0 87.4 %all-reduce.9.cloned.1.call-done = f32[2048,512]{1,0:T(8,128)} async-done(((f32[2048,512]{1,0:T(8,128)}), f32[2048,512]{1,0:T(8,128)}) %all-reduce.9.cloned.1.call-update) | async-done | bytes 4194320 | tf_op jit(solution)/shard_map/psum | solution.py:12
  353.5 93.3 %collective-permute-done = f32[2,512,512]{2,1,0:T(8,128)S(1)} collective-permute-done((f32[2,512,512]{2,1,0:T(8,128)}, f32[2,512,512]{2,1,0:T(8,128)S(1)}, u32[]{:S(2)}, u32[]{:S(2)}) %collective-permute-start) | collective-permute-done | bytes 2097184 | tf_op jit(solution)/shard_map/ppermute | solution.py:22
  451.5 24.5 %collective-permute-done.1 = f32[1,512,512]{2,1,0:T(8,128)} collective-permute-done((f32[1,512,512]{2,1,0:T(8,128)}, f32[1,512,512]{2,1,0:T(8,128)}, u32[]{:S(2)}, u32[]{:S(2)}) %collective-permute-start.1) | collective-permute-done | bytes 1048608 | tf_op jit(solution)/shard_map/ppermute | solution.py:22
  486.5 116.0 %all-gather.5.cloned.1.call-done = f32[1,4096,512]{2,1,0:T(8,128)} async-done(((f32[1,512,512]{2,1,0:T(8,128)}), f32[1,4096,512]{2,1,0:T(8,128)}) %all-gather.5.cloned.1.call-update) | async-done | bytes 8388624 | tf_op jit(solution)/shard_map/all_gather | solution.py:97
  607.2 60.7 %subtract_select_fusion.1 = f32[2048,4096]{1,0:T(8,128)} fusion(f32[2048,4096]{1,0:T(8,128)} %fusion, pred[4096]{0:T(1024)(128)(4,1)S(1)} %broadcast_compare_fusion.1, pred[2048]{0:T(1024)(128)(4,1)S(1)} %get-tuple-element.222, f32[2048,512]{1,0:T(8,128)S(1)} %copy-done, f32[4096,512]{1,0:T(8,128)S(1)} %bitcast.177), kind=kOutput, calls=%fused_computation.7 | convolution fusion | flops 51564773376 | bytes 79697920 | tf_op jit(solution)/shard_map/dot_general | solution.py:31
  671.0 76.1 %all-reduce.11.cloned.1.call-done = f32[512,512]{0,1:T(8,128)} async-done(((f32[512,512]{0,1:T(8,128)}), f32[512,512]{0,1:T(8,128)}) %all-reduce.11.cloned.1.call-update) | async-done | bytes 1048592 | tf_op jit(solution)/shard_map/psum | solution.py:67
  751.4 11.7 cholesky.446
  773.8 11.7 cholesky.465
  796.2 11.7 cholesky.486
  818.4 11.7 cholesky.503
  845.6 39.3 %custom-call.38 = f32[4,128,128]{1,2,0:T(8,128)S(1)} custom-call(f32[4,128,128]{2,1,0:T(8,128)S(1)} %get-tuple-element.140), custom_call_target="InvertDiagBlocksLowerTriangular" | custom-call | tf_op jit(solution)/shard_map/jit(_solve_triangular)/triangular_solve | solution.py:70
  889.7 10.6 broadcast_select_fusion
  900.5 85.5 %all-reduce.13.cloned.1.call-done = f32[2048,512]{1,0:T(8,128)} async-done(((f32[2048,512]{1,0:T(8,128)}), f32[2048,512]{1,0:T(8,128)}) %all-reduce.13.cloned.1.call-update) | async-done | bytes 4194320 | tf_op jit(solution)/shard_map/psum | solution.py:12
  989.1 93.1 %collective-permute-done.2 = f32[2,512,512]{2,1,0:T(8,128)S(1)} collective-permute-done((f32[2,512,512]{2,1,0:T(8,128)S(1)}, f32[2,512,512]{2,1,0:T(8,128)S(1)}, u32[]{:S(2)}, u32[]{:S(2)}) %collective-permute-start.2) | collective-permute-done | bytes 2097184 | tf_op jit(solution)/shard_map/ppermute | solution.py:22
  1083.1 24.2 %collective-permute-done.3 = f32[1,512,512]{2,1,0:T(8,128)S(1)} collective-permute-done((f32[1,512,512]{2,1,0:T(8,128)S(1)}, f32[1,512,512]{2,1,0:T(8,128)S(1)}, u32[]{:S(2)}, u32[]{:S(2)}) %collective-permute-start.3) | collective-permute-done | bytes 1048608 | tf_op jit(solution)/shard_map/ppermute | solution.py:22
  1117.9 114.7 %all-gather.7.cloned.1.call-done = f32[1,4096,512]{2,1,0:T(8,128)} async-done(((f32[1,512,512]{2,1,0:T(8,128)}), f32[1,4096,512]{2,1,0:T(8,128)}) %all-gather.7.cloned.1.call-update) | async-done | bytes 8388624 | tf_op jit(solution)/shard_map/all_gather | solution.py:97
  1237.2 60.9 %subtract_select_fusion = f32[2048,4096]{1,0:T(8,128)} fusion(f32[2048,4096]{1,0:T(8,128)} %fusion.1, pred[4096]{0:T(1024)(128)(4,1)S(1)} %broadcast_compare_fusion, pred[2048]{0:T(1024)(128)(4,1)S(1)} %compare_and_fusion.1, f32[2048,512]{1,0:T(8,128)S(1)} %copy-done.1, f32[4096,512]{1,0:T(8,128)S(1)} %bitcast.178), kind=kOutput, calls=%fused_computation.6 | convolution fusion | flops 51564773376 | bytes 79697920 | tf_op jit(solution)/shard_map/dot_general | solution.py:31
  1301.1 76.3 %all-reduce.15.cloned.1.call-done = f32[512,512]{0,1:T(8,128)} async-done(((f32[512,512]{0,1:T(8,128)}), f32[512,512]{0,1:T(8,128)}) %all-reduce.15.cloned.1.call-update) | async-done | bytes 1048592 | tf_op jit(solution)/shard_map/psum | solution.py:67
  1380.3 11.7 cholesky.518
  1402.7 11.7 cholesky.537
  1414.5 10.2 custom-call.40
  1425.4 11.7 cholesky.558
  1447.5 11.9 cholesky.575
  1474.1 39.3 %custom-call.42 = f32[4,128,128]{1,2,0:T(8,128)S(1)} custom-call(f32[4,128,128]{2,1,0:T(8,128)S(1)} %get-tuple-element.141), custom_call_target="InvertDiagBlocksLowerTriangular" | custom-call | tf_op jit(solution)/shard_map/jit(_solve_triangular)/triangular_solve | solution.py:70
  (215 shorter events, 239.0 us)
Async XLA Ops:
  6.5 103.4 %all-reduce.7.cloned.1.call-start = ((), (), s32[]{:S(2)}) async-start(), calls=%async_computation | async-start | bytes 2097152 | tf_op jit(solution)/shard_map/psum | solution.py:67
  32.6 315.9 %all-reduce.9.cloned.1.call-start = ((), (), s32[]{:S(2)}) async-start(), calls=%async_computation.1 | async-start | bytes 8388608 | tf_op jit(solution)/shard_map/psum | solution.py:12
  109.9 1.5 copy-start.2
  261.0 341.6 %all-gather.5.cloned.1.call-start = ((), (), s32[]{:S(2)}) async-start(), calls=%async_computation.5 | async-start | bytes 9437184 | tf_op jit(solution)/shard_map/all_gather | solution.py:97
  353.3 93.6 %collective-permute-start = (f32[2,512,512]{2,1,0:T(8,128)}, f32[2,512,512]{2,1,0:T(8,128)S(1)}, u32[]{:S(2)}, u32[]{:S(2)}) collective-permute-start(f32[2,512,512]{2,1,0:T(8,128)} %bitcast.13), channel_id=1, source_target_pairs={{0,16},{16,0},{4,20},{20,4},{8,24},{24,8},{12,28},{28,12},{1,17},{... | collective-permute-start | bytes 6291464 | tf_op jit(solution)/shard_map/ppermute | solution.py:22
  446.8 1.3 copy-start.7
  451.5 24.5 %collective-permute-start.1 = (f32[1,512,512]{2,1,0:T(8,128)}, f32[1,512,512]{2,1,0:T(8,128)}, u32[]{:S(2)}, u32[]{:S(2)}) collective-permute-start(f32[1,512,512]{2,1,0:T(8,128)} %slice_select_fusion.5), channel_id=1, source_target_pairs={{0,8},{8,0},{4,12},{12,4},{16,24},{24,16},{20,28},{28,20},{1,9},{9... | collective-permute-start | bytes 3145736 | tf_op jit(solution)/shard_map/ppermute | solution.py:22
  477.4 269.7 %all-reduce.11.cloned.1.call-start = ((), (), s32[]{:S(2)}) async-start(), calls=%async_computation.2 | async-start | bytes 2097152 | tf_op jit(solution)/shard_map/psum | solution.py:67
  602.6 4.6 copy-start
  670.8 315.2 %all-reduce.13.cloned.1.call-start = ((), (), s32[]{:S(2)}) async-start(), calls=%async_computation.3 | async-start | bytes 8388608 | tf_op jit(solution)/shard_map/psum | solution.py:12
  747.1 2.8 copy-start.3
  900.3 332.3 %all-gather.7.cloned.1.call-start = ((), (), s32[]{:S(2)}) async-start(), calls=%async_computation.6 | async-start | bytes 9437184 | tf_op jit(solution)/shard_map/all_gather | solution.py:97
  988.8 93.4 %collective-permute-start.2 = (f32[2,512,512]{2,1,0:T(8,128)S(1)}, f32[2,512,512]{2,1,0:T(8,128)S(1)}, u32[]{:S(2)}, u32[]{:S(2)}) collective-permute-start(f32[2,512,512]{2,1,0:T(8,128)S(1)} %bitcast.189), channel_id=1, source_target_pairs={{0,16},{16,0},{4,20},{20,4},{8,24},{24,8},{12,28},{28,12},{1,17},{... | collective-permute-start | bytes 6291464 | tf_op jit(solution)/shard_map/ppermute | solution.py:22
  1082.7 26.0 %copy-start.5 = (f32[512,512]{1,0:T(8,128)S(1)}, f32[512,512]{1,0:T(8,128)}, u32[]{:S(2)}) copy-start(f32[512,512]{1,0:T(8,128)} %get-tuple-element.169) | copy-start | bytes 3145732
  1083.0 24.3 %collective-permute-start.3 = (f32[1,512,512]{2,1,0:T(8,128)S(1)}, f32[1,512,512]{2,1,0:T(8,128)S(1)}, u32[]{:S(2)}, u32[]{:S(2)}) collective-permute-start(f32[1,512,512]{2,1,0:T(8,128)S(1)} %slice_select_fusion.4), channel_id=1, source_target_pairs={{0,8},{8,0},{4,12},{12,4},{16,24},{24,16},{20,28},{28,20},{1,9},{9... | collective-permute-start | bytes 3145736 | tf_op jit(solution)/shard_map/ppermute | solution.py:22
  1108.7 268.7 %all-reduce.15.cloned.1.call-start = ((), (), s32[]{:S(2)}) async-start(), calls=%async_computation.4 | async-start | bytes 2097152 | tf_op jit(solution)/shard_map/psum | solution.py:67
  1232.6 4.6 copy-start.1
  1377.4 1.5 copy-start.4
  1518.2 8.7 copy-start.6
Sparse Core Ops, SparseCore 0:
  32.7 77.1 all-reduce.6
  261.1 87.3 all-reduce.8
  477.5 124.9 all-gather.4
  670.9 76.1 all-reduce.10
  900.4 85.5 all-reduce.12
  1108.8 123.7 all-gather.6
  1301.2 76.1 all-reduce.14
where the time goes:
time: 1550 us; the launch traced here: 1540 us
  waiting for transfers between devices  869 us (56%)
  other arithmetic  408 us (26%)
  matrix products  171 us (11%)
  local copies, waits for them, and re-layouts  67.9 us (4%)
  between operations  22.3 us (1%)
    another operation x44, other arithmetic, factor_panel(): low_factor = jnp.linalg.cholesky(diagonal)  238 us
    ppermute x4, waiting for transfers between devices, from_partner(): return lax.ppermute(block, axis, route)  235 us
    all_gather x2, waiting for transfers between devices, local(): gathered = lax.all_gather(pieces[0], 'row', axis=0, tiled=True)  231 us
    psum x3, waiting for transfers between devices, factor_panel(): diagonal = lax.psum(placed, 'row')  230 us
    psum x2, waiting for transfers between devices, broadcast(): return lax.psum(kept, axis)  173 us
    dot_general x5, matrix products, times_transposed(): lax.dot_general(left, right, (((1,), (1,)), ((), ())), precision=lax.Prec...  152 us
    another operation x7, other arithmetic, factor_panel(): jax.scipy.linalg.solve_triangular(low_factor, identity, lower=True)  122 us
  transfers between devices with their start and end apart: 11, of which 11 were waited for; matrix products, arithmetic and copies ran while one was open for 1% of the time, Pallas kernels for 0%

commit v1 on v0

v1 whole, which is shorter than its diff:
```python
import jax
import jax.numpy as jnp
from jax import lax
from jax.sharding import PartitionSpec as P

NB = 512
STEPS = 2


def from_partner(block, axis, apart):
    count = lax.axis_size(axis)
    route = []
    for low in range(count):
        high = low | 1 << apart
        if high != low and high < count:
            route += [(low, high), (high, low)]
    return lax.ppermute(block, axis, route)


def global_index(count, block, grid, position):
    ladder = jnp.arange(count, dtype=jnp.int32)
    return (ladder // block * grid + position) * block + ladder % block


def times_transposed(left, right):
    return lax.dot_general(
        left,
        right,
        (((1,), (1,)), ((), ())),
        precision=lax.Precision.HIGHEST,
        preferred_element_type=jnp.float32,
    )


def bcast_col(value, owner, col_id, grid_cols):
    held = value
    have = [owner]
    bit = 1
    while bit < grid_cols:
        route = [(h, h ^ bit) for h in have if (h ^ bit) < grid_cols]
        got = lax.ppermute(held, "col", route)
        targets = [t for _, t in route]
        is_target = jnp.zeros((), bool)
        for t in targets:
            is_target = is_target | (col_id == t)
        held = jnp.where(is_target, got, held)
        have = have + targets
        bit <<= 1
    return held


def local(gram):
    grid_rows = lax.axis_size("row")
    grid_cols = lax.axis_size("col")
    row_id = lax.axis_index("row")
    col_id = lax.axis_index("col")
    rblock = NB * grid_cols // grid_rows
    per_class = grid_rows // grid_cols
    panels = STEPS + 1
    assert panels <= grid_cols and panels * per_class <= grid_rows
    local_rows = gram.shape[0]
    local_cols = gram.shape[1]
    blocks = local_rows // rblock
    grows = global_index(local_rows, rblock, grid_rows, row_id)
    gcols = global_index(local_cols, NB, grid_cols, col_id)
    row_class = row_id // per_class
    identity = jnp.eye(NB, dtype=jnp.float32)

    tile = gram[0:rblock, 0:NB]
    colblk = lax.all_gather(tile, "row", axis=0, tiled=True)
    colblk = colblk[: panels * NB].reshape(panels, NB, NB)
    send_a = jnp.where(col_id == 0, colblk[0], colblk[1])
    recv_a = lax.ppermute(send_a, "col", [(0, 1), (1, 2)])
    recv_b = lax.ppermute(colblk[0:2], "col", [(0, 2)])

    def pick(options, default):
        out = default
        for col, val in options:
            out = jnp.where(col_id == col, val, out)
        return out

    g00 = pick([(0, colblk[0]), (1, recv_a), (2, recv_b[0])], identity)
    g10 = pick([(1, colblk[0].T), (2, recv_b[1])], jnp.zeros_like(identity))
    g11 = pick([(1, colblk[1]), (2, recv_a)], identity)
    g20 = pick([(2, colblk[0].T)], jnp.zeros_like(identity))
    g21 = pick([(2, colblk[1].T)], jnp.zeros_like(identity))
    g22 = pick([(2, colblk[2])], identity)

    def factor(diag):
        low_factor = jnp.linalg.cholesky(diag)
        inverse = jax.scipy.linalg.solve_triangular(low_factor, identity, lower=True)
        return low_factor, inverse

    panel_in = gram[:, 0:NB]

    def panel_rows(updated, low_factor, inverse, panel_index):
        end_row = panel_index * NB + NB
        solved = times_transposed(updated, inverse)
        trailing = jnp.where((grows >= end_row)[:, None], solved, 0.0)
        first = panel_index * per_class
        member = jnp.clip(row_id - first, 0, per_class - 1)
        rows_diag = lax.dynamic_slice_in_dim(low_factor, member * rblock, rblock, 0)
        in_panel = (row_id >= first) & (row_id < first + per_class)
        patched = jnp.where(in_panel, rows_diag, trailing[0:rblock])
        column = trailing.at[0:rblock].set(patched)
        return trailing, column

    def spread_columns_of(spread_rows_all):
        pieces = spread_rows_all.reshape(grid_cols, blocks // grid_cols * rblock, NB)
        shift_bits = per_class.bit_length() - 1
        for bit_level in reversed(range(grid_cols.bit_length() - 1)):
            halfway = pieces.shape[0] // 2
            own_bit = row_class >> bit_level & 1
            wanted = col_id >> bit_level & 1
            upper = own_bit == 1
            retained = jnp.where(upper, pieces[halfway:], pieces[:halfway])
            outgoing = jnp.where(upper, pieces[:halfway], pieces[halfway:])
            received = from_partner(outgoing, "row", shift_bits + bit_level)
            pieces = jnp.where(own_bit == wanted, retained, received)
        gathered = lax.all_gather(pieces[0], "row", axis=0, tiled=True)
        spread = gathered.reshape(grid_cols, per_class, blocks // grid_cols, rblock, NB)
        return jnp.transpose(spread, (0, 2, 1, 3, 4)).reshape(local_cols, NB)

    l0, i0 = factor(g00)
    l0_b1 = times_transposed(g10, i0)
    l0_b2 = times_transposed(g20, i0)
    trail0, column0 = panel_rows(panel_in, l0, i0, 0)
    rows0 = bcast_col(trail0, 0, col_id, grid_cols)
    cols0 = spread_columns_of(rows0)

    l1, i1 = factor(g11 - times_transposed(l0_b1, l0_b1))
    l1_b2 = times_transposed(g21 - times_transposed(l0_b2, l0_b1), i1)
    upd1 = panel_in - times_transposed(rows0, l0_b1)
    trail1, column1 = panel_rows(upd1, l1, i1, 1)
    rows1 = bcast_col(trail1, 1, col_id, grid_cols)
    cols1 = spread_columns_of(rows1)

    d2 = g22 - times_transposed(l0_b2, l0_b2) - times_transposed(l1_b2, l1_b2)
    l2, i2 = factor(d2)
    upd2 = panel_in - times_transposed(rows0, l0_b2) - times_transposed(rows1, l1_b2)
    _, column2 = panel_rows(upd2, l2, i2, 2)

    left = jnp.concatenate([rows0, rows1], axis=1)
    right = jnp.concatenate([cols0, cols1], axis=1)
    updated = gram - times_transposed(left, right)
    in_steps = grows < STEPS * NB
    panel_end = (grows // NB + 1) * NB
    zero = in_steps[:, None] & (gcols[None, :] >= panel_end[:, None])
    updated = jnp.where(zero, 0.0, updated)
    own_column = pick([(0, column0), (1, column1), (2, column2)], updated[:, 0:NB])
    updated = updated.at[:, 0:NB].set(own_column)
    return updated


def solution(mesh):
    placed = (P("row", "col"),)
    return jax.shard_map(
        local, mesh=mesh, in_specs=placed, out_specs=P("row", "col"), check_vma=False
    )
```

time: 1550 us -> 1140 us (0.74)
  waiting for transfers between devices: 869 us -> 367 us
  matrix products: 171 us -> 238 us
  starting transfers between devices: 1.62 us -> 17.5 us
    psum x5 -> x0, waiting for transfers between devices: 403 us -> none  [the longest x3 230 us: factor_panel(): diagonal = lax.psum(placed, 'row')]
    all_gather x2 -> x3, waiting for transfers between devices: 231 us -> 73.2 us  [the longest x1 73.2 us: local(): colblk = lax.all_gather(tile, 'row', axis=0, tiled=True)]
    ppermute x0 -> x6, waiting for transfers between devices: none -> 128 us  [the longest x4 105 us: bcast_col(): got = lax.ppermute(held, 'col', route)]
    ppermute x4, waiting for transfers between devices: 235 us -> 165 us  [from_partner(): return lax.ppermute(block, axis, route)]
    dot_general x5 -> x14, matrix products: 152 us -> 196 us  [times_transposed(): lax.dot_general(left, right, (((1,), (1,)), ((), ())), precision=lax.Prec...]
    another operation x39, matrix products: 19.8 us -> 42.2 us  [the longest x21 23.5 us: factor(): jax.scipy.linalg.solve_triangular(low_factor, identity, lower=True)]
    unnamed x22 -> x62, local copies, waits for them, and re-layouts: 24.6 us -> 5.57 us
    ppermute x0 -> x6, starting transfers between devices: none -> 15.8 us  [the longest x4 10.8 us: bcast_col(): got = lax.ppermute(held, 'col', route)]
  transfers between devices with their start and end apart: 11 -> 13, of which waited for: 11 -> 9; matrix products, arithmetic and copies ran while one was open for 1% -> 36% of each run, Pallas kernels for 0% -> 0%
where the time goes in v1:
time: 1140 us; the launch traced here: 1120 us
  other arithmetic  408 us (36%)
  waiting for transfers between devices  367 us (32%)
  matrix products  238 us (21%)
  local copies, waits for them, and re-layouts  69.5 us (6%)
  between operations  22.3 us (2%)
  starting transfers between devices  17.5 us (2%)
    another operation x44, other arithmetic, factor(): low_factor = jnp.linalg.cholesky(diag)  240 us
    dot_general x14, matrix products, times_transposed(): lax.dot_general(left, right, (((1,), (1,)), ((), ())), precision=lax.Prec...  196 us
    ppermute x4, waiting for transfers between devices, from_partner(): return lax.ppermute(block, axis, route)  165 us
    another operation x7, other arithmetic, factor(): jax.scipy.linalg.solve_triangular(low_factor, identity, lower=True)  124 us
    ppermute x4, waiting for transfers between devices, bcast_col(): got = lax.ppermute(held, 'col', route)  105 us
    all_gather x1, waiting for transfers between devices, local(): colblk = lax.all_gather(tile, 'row', axis=0, tiled=True)  73.2 us
    another operation x40, local copies, waits for them, and re-layouts, factor(): jax.scipy.linalg.solve_triangular(low_factor, identity, lower=True)  31.2 us
    another operation x21, matrix products, factor(): jax.scipy.linalg.solve_triangular(low_factor, identity, lower=True)  23.5 us
  transfers between devices with their start and end apart: 13, of which 9 were waited for; matrix products, arithmetic and copies ran while one was open for 36% of the time, Pallas kernels for 0%

profile of v1, /device:TPU:25, one launch (start us, length us, event | category | flops | bytes accessed | tf_op | source)
XLA Modules:
  0.0 1123.1 jit_solution(9803564116441316535)
XLA Ops:
  8.5 73.2 %all-gather.6.cloned.1.call-done = f32[2048,512]{1,0:T(8,128)} async-done(((f32[256,512]{1,0:T(8,128)}), f32[2048,512]{1,0:T(8,128)}) %all-gather.6.cloned.1.call-update) | async-done | bytes 4194320 | tf_op jit(solution)/shard_map/all_gather | solution.py:70
  97.5 22.9 %collective-permute-done.1 = f32[512,512]{0,1:T(8,128)} collective-permute-done((f32[512,512]{0,1:T(8,128)}, f32[512,512]{0,1:T(8,128)}, u32[]{:S(2)}, u32[]{:S(2)}) %collective-permute-start.1) | collective-permute-done | bytes 1048608 | tf_op jit(solution)/shard_map/ppermute | solution.py:73
  123.8 11.7 %cholesky.374 = f32[128,128]{1,0:T(8,128)S(1)} custom-call(f32[128,128]{1,0:T(8,128)S(1)} %cholesky.586), custom_call_target="Cholesky" | custom-call | tf_op jit(solution)/shard_map/jit(cholesky)/cholesky | solution.py:90
  148.0 11.7 %cholesky.393 = f32[128,128]{1,0:T(8,128)S(1)} custom-call(f32[128,128]{1,0:T(8,128)S(1)} %cholesky.590), custom_call_target="Cholesky" | custom-call | tf_op jit(solution)/shard_map/jit(cholesky)/cholesky | solution.py:90
  159.8 10.1 custom-call.32
  171.5 11.7 %cholesky.414 = f32[128,128]{1,0:T(8,128)S(1)} custom-call(f32[128,128]{1,0:T(8,128)S(1)} %cholesky.595), custom_call_target="Cholesky" | custom-call | tf_op jit(solution)/shard_map/jit(cholesky)/cholesky | solution.py:90
  195.1 11.9 %cholesky.431 = f32[128,128]{1,0:T(8,128)S(1)} custom-call(f32[128,128]{1,0:T(8,128)S(1)} %convolution_subtract_fusion.20), custom_call_target="Cholesky" | custom-call | tf_op jit(solution)/shard_map/jit(cholesky)/cholesky | solution.py:90
  219.8 39.3 %custom-call.34 = f32[4,128,128]{1,2,0:T(8,128)S(1)} custom-call(f32[4,128,128]{2,1,0:T(8,128)S(1)} %get-tuple-element.75), custom_call_target="InvertDiagBlocksLowerTriangular" | custom-call | tf_op jit(solution)/shard_map/jit(_solve_triangular)/triangular_solve | solution.py:91
  276.2 10.3 collective-permute-done.2
  305.3 11.7 %cholesky.446 = f32[128,128]{1,0:T(8,128)S(1)} custom-call(f32[128,128]{1,0:T(8,128)S(1)} %cholesky.599), custom_call_target="Cholesky" | custom-call | tf_op jit(solution)/shard_map/jit(cholesky)/cholesky | solution.py:90
  317.1 9.9 custom-call.35
  329.6 11.7 %cholesky.465 = f32[128,128]{1,0:T(8,128)S(1)} custom-call(f32[128,128]{1,0:T(8,128)S(1)} %cholesky.603), custom_call_target="Cholesky" | custom-call | tf_op jit(solution)/shard_map/jit(cholesky)/cholesky | solution.py:90
  352.8 11.7 %cholesky.486 = f32[128,128]{1,0:T(8,128)S(1)} custom-call(f32[128,128]{1,0:T(8,128)S(1)} %cholesky.608), custom_call_target="Cholesky" | custom-call | tf_op jit(solution)/shard_map/jit(cholesky)/cholesky | solution.py:90
  364.5 10.0 custom-call.37
  376.0 11.7 %cholesky.503 = f32[128,128]{1,0:T(8,128)S(1)} custom-call(f32[128,128]{1,0:T(8,128)S(1)} %convolution_subtract_fusion.19), custom_call_target="Cholesky" | custom-call | tf_op jit(solution)/shard_map/jit(cholesky)/cholesky | solution.py:90
  402.7 12.4 %while.11 = (s32[]{:T(128)}, f32[512,512]{1,0:T(8,128)}, s32[4,2]{0,1:T(2,128)S(1)}, f32[4,128,128]{2,1,0:T(8,128)S(1)}, s32[]{:T(128)}) while((s32[]{:T(128)}, f32[512,512]{1,0:T(8,128)}, s32[4,2]{0,1:T(2,128)S(1)}, f32[4,128,128]{2,1,0:T(8,128)S(1)}, s32[]{:T(128)}) %tuple.111), condition=%wide.while_cond.4.clone, body=%wide.while_body.4.clone.sunk | while | flops 2 | bytes 131189 | solution.py:91
  415.1 39.3 %custom-call.38 = f32[4,128,128]{1,2,0:T(8,128)S(1)} custom-call(f32[4,128,128]{2,1,0:T(8,128)S(1)} %get-tuple-element.76), custom_call_target="InvertDiagBlocksLowerTriangular" | custom-call | tf_op jit(solution)/shard_map/jit(_solve_triangular)/triangular_solve | solution.py:91
  459.0 35.4 %collective-permute-done.6 = f32[2,512,512]{2,1,0:T(8,128)} collective-permute-done((f32[2,512,512]{2,1,0:T(8,128)}, f32[2,512,512]{2,1,0:T(8,128)}, u32[]{:S(2)}, u32[]{:S(2)}) %collective-permute-start.6) | collective-permute-done | bytes 2097184 | tf_op jit(solution)/shard_map/ppermute | solution.py:17
  509.8 10.8 collective-permute-done.7
  522.0 10.7 fusion.17
  548.2 88.5 %collective-permute-done.5 = f32[2048,512]{1,0:T(8,128)S(1)} collective-permute-done((f32[2048,512]{1,0:T(8,128)S(1)}, f32[2048,512]{1,0:T(8,128)S(1)}, u32[]{:S(2)}, u32[]{:S(2)}) %collective-permute-start.5) | collective-permute-done | bytes 4194336 | tf_op jit(solution)/shard_map/ppermute | solution.py:41
  639.6 94.8 %collective-permute-done.8 = f32[2,512,512]{2,1,0:T(8,128)S(1)} collective-permute-done((f32[2,512,512]{2,1,0:T(8,128)S(1)}, f32[2,512,512]{2,1,0:T(8,128)S(1)}, u32[]{:S(2)}, u32[]{:S(2)}) %collective-permute-start.8) | collective-permute-done | bytes 2097184 | tf_op jit(solution)/shard_map/ppermute | solution.py:17
  735.3 24.3 %collective-permute-done.9 = f32[1,512,512]{2,1,0:T(8,128)S(1)} collective-permute-done((f32[1,512,512]{2,1,0:T(8,128)S(1)}, f32[1,512,512]{2,1,0:T(8,128)S(1)}, u32[]{:S(2)}, u32[]{:S(2)}) %collective-permute-start.9) | collective-permute-done | bytes 1048608 | tf_op jit(solution)/shard_map/ppermute | solution.py:17
  785.8 11.7 %cholesky.518 = f32[128,128]{1,0:T(8,128)S(1)} custom-call(f32[128,128]{1,0:T(8,128)S(1)} %cholesky.612), custom_call_target="Cholesky" | custom-call | tf_op jit(solution)/shard_map/jit(cholesky)/cholesky | solution.py:90
  811.7 11.7 %cholesky.537 = f32[128,128]{1,0:T(8,128)S(1)} custom-call(f32[128,128]{1,0:T(8,128)S(1)} %cholesky.616), custom_call_target="Cholesky" | custom-call | tf_op jit(solution)/shard_map/jit(cholesky)/cholesky | solution.py:90
  824.0 10.0 custom-call.40
  836.3 11.7 %cholesky.558 = f32[128,128]{1,0:T(8,128)S(1)} custom-call(f32[128,128]{1,0:T(8,128)S(1)} %cholesky.621), custom_call_target="Cholesky" | custom-call | tf_op jit(solution)/shard_map/jit(cholesky)/cholesky | solution.py:90
  860.8 12.1 %cholesky.575 = f32[128,128]{1,0:T(8,128)S(1)} custom-call(f32[128,128]{1,0:T(8,128)S(1)} %convolution_subtract_fusion.18), custom_call_target="Cholesky" | custom-call | tf_op jit(solution)/shard_map/jit(cholesky)/cholesky | solution.py:90
  881.8 11.7 %while.12 = (s32[]{:T(128)}, f32[512,512]{1,0:T(8,128)}, s32[4,2]{0,1:T(2,128)S(1)}, f32[4,128,128]{2,1,0:T(8,128)S(1)}, s32[]{:T(128)}) while((s32[]{:T(128)}, f32[512,512]{1,0:T(8,128)}, s32[4,2]{0,1:T(2,128)S(1)}, f32[4,128,128]{2,1,0:T(8,128)S(1)}, s32[]{:T(128)}) %tuple.112), condition=%wide.while_cond.4.clone.1, body=%wide.while_body.4.clone.1.sunk | while | flops 2 | bytes 131189 | solution.py:91
  894.2 40.1 %custom-call.42 = f32[4,128,128]{1,2,0:T(8,128)S(1)} custom-call(f32[4,128,128]{2,1,0:T(8,128)} %copy-done.30), custom_call_target="InvertDiagBlocksLowerTriangular" | custom-call | tf_op jit(solution)/shard_map/jit(_solve_triangular)/triangular_solve | solution.py:91
  960.9 10.1 fusion.20
  988.9 119.0 %subtract_select_fusion = f32[2048,4096]{1,0:T(8,128)} fusion(f32[2048,4096]{1,0:T(8,128)} %param.12, f32[4096,512]{1,0:T(8,128)} %bitcast.194, f32[4096,512]{1,0:T(8,128)} %bitcast.193, s32[4096]{0:T(1024)S(1)} %fusion.147, s32[2048]{0:T(1024)S(1)} %fusion.161, pred[2048]{0:T(1024)(128)(4,1)S(1)} %broadcast_compare_fusion.3, f32[2048,512]{1,0:T(8,128)} %copy-done.4, ...), kind=kOutput, calls=%fused_computation.6 | convolution fusion | flops 103119060992 | bytes 92301312 | tf_op jit(solution)/shard_map/dot_general | solution.py:26
  (261 shorter events, 308.0 us)
Async XLA Ops:
  6.5 75.2 %all-gather.6.cloned.1.call-start = ((), (), s32[]{:S(2)}) async-start(), calls=%async_computation | async-start | bytes 4718592 | tf_op jit(solution)/shard_map/all_gather | solution.py:70
  8.4 964.4 %all-gather.8.cloned.1.call-start = ((), (), s32[]{:S(2)}) async-start(), calls=%async_computation.1 | async-start | bytes 9437184 | tf_op jit(solution)/shard_map/all_gather | solution.py:120
  85.1 35.3 %collective-permute-start = (f32[2,512,512]{1,2,0:T(8,128)}, f32[2,512,512]{1,2,0:T(8,128)}, u32[]{:S(2)}, u32[]{:S(2)}) collective-permute-start(f32[2,512,512]{1,2,0:T(8,128)} %copy.40), channel_id=1, source_target_pairs={{0,2},{4,6},{8,10},{12,14},{16,18},{20,22},{24,26},{28,30}} | collective-permute-start | bytes 6291464 | tf_op jit(solution)/shard_map/ppermute | solution.py:74
  94.0 26.3 %collective-permute-start.1 = (f32[512,512]{0,1:T(8,128)}, f32[512,512]{0,1:T(8,128)}, u32[]{:S(2)}, u32[]{:S(2)}) collective-permute-start(f32[512,512]{0,1:T(8,128)} %copy.41), channel_id=1, source_target_pairs={{0,1},{1,2},{4,5},{5,6},{8,9},{9,10},{12,13},{13,14},{16,17},{17,1... | collective-permute-start | bytes 3145736 | tf_op jit(solution)/shard_map/ppermute | solution.py:73
  219.8 39.8 %copy-start.19 = (f32[512,512]{1,0:T(8,128)}, f32[512,512]{1,0:T(8,128)S(1)}, u32[]{:S(2)}) copy-start(f32[512,512]{1,0:T(8,128)S(1)} %get-tuple-element.309) | copy-start | bytes 3145732
  259.5 35.0 %copy-start.7 = (f32[128,512]{1,0:T(8,128)}, f32[128,512]{1,0:T(8,128)S(1)}, u32[]{:S(2)}) copy-start(f32[128,512]{1,0:T(8,128)S(1)} %fusion.88) | copy-start | bytes 786436
  260.6 34.0 %copy-start.11 = (f32[128,512]{1,0:T(8,128)}, f32[128,512]{1,0:T(8,128)S(1)}, u32[]{:S(2)}) copy-start(f32[128,512]{1,0:T(8,128)S(1)} %fusion.126) | copy-start | bytes 786436
  263.0 31.5 %copy-start.18 = (f32[128,512]{1,0:T(8,128)}, f32[128,512]{1,0:T(8,128)S(1)}, u32[]{:S(2)}) copy-start(f32[128,512]{1,0:T(8,128)S(1)} %fusion.124) | copy-start | bytes 786436
  265.9 28.6 %copy-start.28 = (f32[128,512]{1,0:T(8,128)}, f32[128,512]{1,0:T(8,128)S(1)}, u32[]{:S(2)}) copy-start(f32[128,512]{1,0:T(8,128)S(1)} %fusion.123) | copy-start | bytes 786436
  274.7 14.9 %copy-start.6 = (f32[2048,512]{1,0:T(8,128)}, f32[2048,512]{1,0:T(8,128)S(1)}, u32[]{:S(2)}) copy-start(f32[2048,512]{1,0:T(8,128)S(1)} %select_bitcast_fusion) | copy-start | bytes 12582916
  274.7 18.6 %copy-start.13 = (f32[512,512]{1,0:T(8,128)S(1)}, f32[512,512]{1,0:T(8,128)}, u32[]{:S(2)}) copy-start(f32[512,512]{1,0:T(8,128)} %get-tuple-element.116) | copy-start | bytes 3145732
  274.7 11.8 %collective-permute-start.2 = (f32[2048,512]{1,0:T(8,128)S(1)}, f32[2048,512]{1,0:T(8,128)S(1)}, u32[]{:S(2)}, u32[]{:S(2)}) collective-permute-start(f32[2048,512]{1,0:T(8,128)S(1)} %select_bitcast_fusion), channel_id=1, source_target_pairs={{0,1},{4,5},{8,9},{12,13},{16,17},{20,21},{24,25},{28,29}} | collective-permute-start | bytes 12582920 | tf_op jit(solution)/shard_map/ppermute | solution.py:41
  289.5 105.2 %collective-permute-start.3 = (f32[2048,512]{1,0:T(8,128)}, f32[2048,512]{1,0:T(8,128)}, u32[]{:S(2)}, u32[]{:S(2)}) collective-permute-start(f32[2048,512]{1,0:T(8,128)} %broadcast_select_fusion.1), channel_id=1, source_target_pairs={{0,2},{1,3},{4,6},{5,7},{8,10},{9,11},{12,14},{13,15},{16,18},{17,... | collective-permute-start | bytes 12582920 | tf_op jit(solution)/shard_map/ppermute | solution.py:41
  401.2 93.2 %collective-permute-start.6 = (f32[2,512,512]{2,1,0:T(8,128)}, f32[2,512,512]{2,1,0:T(8,128)}, u32[]{:S(2)}, u32[]{:S(2)}) collective-permute-start(f32[2,512,512]{2,1,0:T(8,128)} %bitcast.28), channel_id=1, source_target_pairs={{0,16},{16,0},{4,20},{20,4},{8,24},{24,8},{12,28},{28,12},{1,17},{... | collective-permute-start | bytes 6291464 | tf_op jit(solution)/shard_map/ppermute | solution.py:17
  454.4 42.4 %copy-start.29 = (f32[4,128,128]{1,2,0:T(8,128)}, f32[4,128,128]{1,2,0:T(8,128)S(1)}, u32[]{:S(2)}) copy-start(f32[4,128,128]{1,2,0:T(8,128)S(1)} %custom-call.38) | copy-start | bytes 786436
  454.4 40.0 %copy-start.8 = (f32[1024,512]{1,0:T(8,128)S(1)}, f32[1024,512]{1,0:T(8,128)}, u32[]{:S(2)}) copy-start(f32[1024,512]{1,0:T(8,128)} %get-tuple-element.119) | copy-start | bytes 6291460
  457.0 64.9 %copy-start.9 = (f32[128,512]{1,0:T(8,128)}, f32[128,512]{1,0:T(8,128)S(1)}, u32[]{:S(2)}) copy-start(f32[128,512]{1,0:T(8,128)S(1)} %fusion.120) | copy-start | bytes 786436
  496.8 23.8 %collective-permute-start.7 = (f32[1,512,512]{2,1,0:T(8,128)S(1)}, f32[1,512,512]{2,1,0:T(8,128)S(1)}, u32[]{:S(2)}, u32[]{:S(2)}) collective-permute-start(f32[1,512,512]{2,1,0:T(8,128)S(1)} %slice_select_fusion.5), channel_id=1, source_target_pairs={{0,8},{8,0},{4,12},{12,4},{16,24},{24,16},{20,28},{28,20},{1,9},{9... | collective-permute-start | bytes 3145736 | tf_op jit(solution)/shard_map/ppermute | solution.py:17
  497.3 24.7 %copy-start.15 = (f32[128,512]{1,0:T(8,128)}, f32[128,512]{1,0:T(8,128)S(1)}, u32[]{:S(2)}) copy-start(f32[128,512]{1,0:T(8,128)S(1)} %fusion.118) | copy-start | bytes 786436
  501.4 20.5 %copy-start.23 = (f32[128,512]{1,0:T(8,128)}, f32[128,512]{1,0:T(8,128)S(1)}, u32[]{:S(2)}) copy-start(f32[128,512]{1,0:T(8,128)S(1)} %fusion.117) | copy-start | bytes 786436
  521.9 458.9 %all-gather.10.cloned.1.call-start = ((), (), s32[]{:S(2)}) async-start(), calls=%async_computation.2 | async-start | bytes 9437184 | tf_op jit(solution)/shard_map/all_gather | solution.py:120
  532.7 10.7 collective-permute-start.4
  546.6 90.0 %collective-permute-start.5 = (f32[2048,512]{1,0:T(8,128)S(1)}, f32[2048,512]{1,0:T(8,128)S(1)}, u32[]{:S(2)}, u32[]{:S(2)}) collective-permute-start(f32[2048,512]{1,0:T(8,128)S(1)} %broadcast_select_fusion), channel_id=1, source_target_pairs={{1,3},{0,2},{5,7},{4,6},{9,11},{8,10},{13,15},{12,14},{17,19},{16,... | collective-permute-start | bytes 12582920 | tf_op jit(solution)/shard_map/ppermute | solution.py:41
  639.6 94.8 %collective-permute-start.8 = (f32[2,512,512]{2,1,0:T(8,128)S(1)}, f32[2,512,512]{2,1,0:T(8,128)S(1)}, u32[]{:S(2)}, u32[]{:S(2)}) collective-permute-start(f32[2,512,512]{2,1,0:T(8,128)S(1)} %bitcast.197), channel_id=1, source_target_pairs={{0,16},{16,0},{4,20},{20,4},{8,24},{24,8},{12,28},{28,12},{1,17},{... | collective-permute-start | bytes 6291464 | tf_op jit(solution)/shard_map/ppermute | solution.py:17
  735.0 27.0 %copy-start.12 = (f32[512,512]{1,0:T(8,128)S(1)}, f32[512,512]{1,0:T(8,128)}, u32[]{:S(2)}) copy-start(f32[512,512]{1,0:T(8,128)} %get-tuple-element.114) | copy-start | bytes 3145732
  735.2 24.4 %collective-permute-start.9 = (f32[1,512,512]{2,1,0:T(8,128)S(1)}, f32[1,512,512]{2,1,0:T(8,128)S(1)}, u32[]{:S(2)}, u32[]{:S(2)}) collective-permute-start(f32[1,512,512]{2,1,0:T(8,128)S(1)} %slice_select_fusion.4), channel_id=1, source_target_pairs={{0,8},{8,0},{4,12},{12,4},{16,24},{24,16},{20,28},{28,20},{1,9},{9... | collective-permute-start | bytes 3145736 | tf_op jit(solution)/shard_map/ppermute | solution.py:17
  763.3 8.4 copy-start.10
  763.3 8.4 copy-start.16
  763.3 8.4 copy-start.24
  934.3 9.7 copy-start.2
  944.0 9.3 copy-start.5
  960.9 10.1 copy-start.27
  (13 other events, 50.5 us)
Sparse Core Ops, SparseCore 0:
  9.5 72.1 all-gather.5
  522.0 169.6 all-gather.7
  761.1 123.1 all-gather.9

commit v2 on v1

--- a/solution.py
+++ b/solution.py
@@ -7,27 +7,17 @@
 STEPS = 2
 
 
-def from_partner(block, axis, apart):
-    count = lax.axis_size(axis)
-    route = []
-    for low in range(count):
-        high = low | 1 << apart
-        if high != low and high < count:
-            route += [(low, high), (high, low)]
-    return lax.ppermute(block, axis, route)
-
-
 def global_index(count, block, grid, position):
     ladder = jnp.arange(count, dtype=jnp.int32)
     return (ladder // block * grid + position) * block + ladder % block
 
 
-def times_transposed(left, right):
+def times_transposed(left, right, precision=lax.Precision.HIGHEST):
     return lax.dot_general(
         left,
         right,
         (((1,), (1,)), ((), ())),
-        precision=lax.Precision.HIGHEST,
+        precision=precision,
         preferred_element_type=jnp.float32,
     )
 
@@ -105,19 +95,19 @@
         column = trailing.at[0:rblock].set(patched)
         return trailing, column
 
-    def spread_columns_of(spread_rows_all):
-        pieces = spread_rows_all.reshape(grid_cols, blocks // grid_cols * rblock, NB)
-        shift_bits = per_class.bit_length() - 1
-        for bit_level in reversed(range(grid_cols.bit_length() - 1)):
-            halfway = pieces.shape[0] // 2
-            own_bit = row_class >> bit_level & 1
-            wanted = col_id >> bit_level & 1
-            upper = own_bit == 1
-            retained = jnp.where(upper, pieces[halfway:], pieces[:halfway])
-            outgoing = jnp.where(upper, pieces[:halfway], pieces[halfway:])
-            received = from_partner(outgoing, "row", shift_bits + bit_level)
-            pieces = jnp.where(own_bit == wanted, retained, received)
-        gathered = lax.all_gather(pieces[0], "row", axis=0, tiled=True)
+    def spread_columns_of(trail, owner):
+        span = blocks // grid_cols * rblock
+        pieces = trail.reshape(grid_cols, span, NB)
+        got = pieces[0]
+        for piece in range(grid_cols):
+            route = []
+            for source_row in range(grid_rows):
+                target_row = piece * per_class + source_row % per_class
+                target_col = source_row // per_class
+                route.append((source_row * grid_cols + owner, target_row * grid_cols + target_col))
+            received = lax.ppermute(pieces[piece], ("row", "col"), route)
+            got = jnp.where(row_id // per_class == piece, received, got)
+        gathered = lax.all_gather(got, "row", axis=0, tiled=True)
         spread = gathered.reshape(grid_cols, per_class, blocks // grid_cols, rblock, NB)
         return jnp.transpose(spread, (0, 2, 1, 3, 4)).reshape(local_cols, NB)
 
@@ -126,14 +116,14 @@
     l0_b2 = times_transposed(g20, i0)
     trail0, column0 = panel_rows(panel_in, l0, i0, 0)
     rows0 = bcast_col(trail0, 0, col_id, grid_cols)
-    cols0 = spread_columns_of(rows0)
+    cols0 = spread_columns_of(trail0, 0)
 
     l1, i1 = factor(g11 - times_transposed(l0_b1, l0_b1))
     l1_b2 = times_transposed(g21 - times_transposed(l0_b2, l0_b1), i1)
     upd1 = panel_in - times_transposed(rows0, l0_b1)
     trail1, column1 = panel_rows(upd1, l1, i1, 1)
     rows1 = bcast_col(trail1, 1, col_id, grid_cols)
-    cols1 = spread_columns_of(rows1)
+    cols1 = spread_columns_of(trail1, 1)
 
     d2 = g22 - times_transposed(l0_b2, l0_b2) - times_transposed(l1_b2, l1_b2)
     l2, i2 = factor(d2)
@@ -142,7 +132,7 @@
 
     left = jnp.concatenate([rows0, rows1], axis=1)
     right = jnp.concatenate([cols0, cols1], axis=1)
-    updated = gram - times_transposed(left, right)
+    updated = gram - times_transposed(left, right, lax.Precision.HIGH)
     in_steps = grows < STEPS * NB
     panel_end = (grows // NB + 1) * NB
     zero = in_steps[:, None] & (gcols[None, :] >= panel_end[:, None])

time: 1140 us -> 935 us (0.82)
  waiting for transfers between devices: 367 us -> 192 us
  matrix products: 238 us -> 190 us
  starting transfers between devices: 17.5 us -> 30.1 us
    ppermute x4, waiting for transfers between devices: 105 us -> 5.54 us  [bcast_col(): got = lax.ppermute(held, 'col', route)]
    ppermute x4 -> x8, waiting for transfers between devices: 165 us -> 89.8 us  [spread_columns_of(): received = lax.ppermute(pieces[piece], ('row', 'col'), route)]
    dot_general x14, matrix products: 196 us -> 144 us  [times_transposed(): lax.dot_general(left, right, (((1,), (1,)), ((), ())), precision=precisio...]
    transpose x2 -> x0, local copies, waits for them, and re-layouts: 16.1 us -> none  [spread_columns_of(): return jnp.transpose(spread, (0, 2, 1, 3, 4)).reshape(local_cols, NB)]
    reshape x0 -> x2, local copies, waits for them, and re-layouts: none -> 15.9 us  [spread_columns_of(): gathered.reshape(grid_cols, per_class, blocks // grid_cols, rblock, NB)]
  transfers between devices with their start and end apart: 13 -> 17, of which waited for: 9 -> 8; matrix products, arithmetic and copies ran while one was open for 36% -> 46% of each run, Pallas kernels for 0% -> 0%
where the time goes in v2:
time: 935 us; the launch traced here: 918 us
  other arithmetic  411 us (44%)
  waiting for transfers between devices  192 us (21%)
  matrix products  190 us (20%)
  local copies, waits for them, and re-layouts  73 us (8%)
  starting transfers between devices  30.1 us (3%)
  between operations  22.1 us (2%)
    another operation x44, other arithmetic, factor(): low_factor = jnp.linalg.cholesky(diag)  240 us
    dot_general x14, matrix products, times_transposed(): lax.dot_general(left, right, (((1,), (1,)), ((), ())), precision=precisio...  144 us
    another operation x7, other arithmetic, factor(): jax.scipy.linalg.solve_triangular(low_factor, identity, lower=True)  125 us
    ppermute x8, waiting for transfers between devices, spread_columns_of(): received = lax.ppermute(pieces[piece], ('row', 'col'), route)  89.8 us
    all_gather x1, waiting for transfers between devices, local(): colblk = lax.all_gather(tile, 'row', axis=0, tiled=True)  73.2 us
    another operation x40, local copies, waits for them, and re-layouts, factor(): jax.scipy.linalg.solve_triangular(low_factor, identity, lower=True)  30.4 us
    another operation x21, matrix products, factor(): jax.scipy.linalg.solve_triangular(low_factor, identity, lower=True)  27.1 us
    ppermute x1, waiting for transfers between devices, local(): recv_a = lax.ppermute(send_a, 'col', [(0, 1), (1, 2)])  22.9 us
  transfers between devices with their start and end apart: 17, of which 8 were waited for; matrix products, arithmetic and copies ran while one was open for 46% of the time, Pallas kernels for 0%

profile of v2, /device:TPU:25, one launch (start us, length us, event | category | flops | bytes accessed | tf_op | source)
XLA Modules:
  0.0 918.1 jit_solution(5237050791947873356)
XLA Ops:
  8.5 73.2 %all-gather.4.cloned.1.call-done = f32[2048,512]{1,0:T(8,128)} async-done(((f32[256,512]{1,0:T(8,128)}), f32[2048,512]{1,0:T(8,128)}) %all-gather.4.cloned.1.call-update) | async-done | bytes 4194320 | tf_op jit(solution)/shard_map/all_gather | solution.py:60
  97.5 22.9 %collective-permute-done.1 = f32[512,512]{0,1:T(8,128)} collective-permute-done((f32[512,512]{0,1:T(8,128)}, f32[512,512]{0,1:T(8,128)}, u32[]{:S(2)}, u32[]{:S(2)}) %collective-permute-start.1) | collective-permute-done | bytes 1048608 | tf_op jit(solution)/shard_map/ppermute | solution.py:63
  123.8 11.7 %cholesky.374 = f32[128,128]{1,0:T(8,128)S(1)} custom-call(f32[128,128]{1,0:T(8,128)S(1)} %cholesky.586), custom_call_target="Cholesky" | custom-call | tf_op jit(solution)/shard_map/jit(cholesky)/cholesky | solution.py:80
  135.6 9.8 %custom-call.31 = f32[1,128,128]{1,2,0:T(8,128)S(1)} custom-call(f32[1,128,128]{2,1,0:T(8,128)S(1)} %get-tuple-element.155), custom_call_target="InvertDiagBlocksLowerTriangular" | custom-call | tf_op jit(solution)/shard_map/jit(cholesky)/cholesky | solution.py:80
  148.0 11.7 %cholesky.393 = f32[128,128]{1,0:T(8,128)S(1)} custom-call(f32[128,128]{1,0:T(8,128)S(1)} %cholesky.590), custom_call_target="Cholesky" | custom-call | tf_op jit(solution)/shard_map/jit(cholesky)/cholesky | solution.py:80
  159.8 9.9 %custom-call.32 = f32[1,128,128]{1,2,0:T(8,128)S(1)} custom-call(f32[1,128,128]{2,1,0:T(8,128)S(1)} %get-tuple-element.152), custom_call_target="InvertDiagBlocksLowerTriangular" | custom-call | tf_op jit(solution)/shard_map/jit(cholesky)/cholesky | solution.py:80
  171.3 11.7 %cholesky.414 = f32[128,128]{1,0:T(8,128)S(1)} custom-call(f32[128,128]{1,0:T(8,128)S(1)} %cholesky.595), custom_call_target="Cholesky" | custom-call | tf_op jit(solution)/shard_map/jit(cholesky)/cholesky | solution.py:80
  195.0 12.1 %cholesky.431 = f32[128,128]{1,0:T(8,128)S(1)} custom-call(f32[128,128]{1,0:T(8,128)S(1)} %convolution_subtract_fusion.20), custom_call_target="Cholesky" | custom-call | tf_op jit(solution)/shard_map/jit(cholesky)/cholesky | solution.py:80
  220.5 39.3 %custom-call.34 = f32[4,128,128]{1,2,0:T(8,128)S(1)} custom-call(f32[4,128,128]{2,1,0:T(8,128)S(1)} %get-tuple-element.75), custom_call_target="InvertDiagBlocksLowerTriangular" | custom-call | tf_op jit(solution)/shard_map/jit(_solve_triangular)/triangular_solve | solution.py:81
  266.7 10.0 %select_bitcast_fusion = f32[2048,512]{1,0:T(8,128)} fusion(f32[2048,4096]{1,0:T(8,128)} %param.12, pred[2048]{0:T(1024)(128)(4,1)S(1)} %broadcast_compare_fusion.1, f32[128,512]{1,0:T(8,128)S(1)} %fusion.123, f32[128,512]{1,0:T(8,128)S(1)} %fusion.124, f32[128,512]{1,0:T(8,128)S(1)} %fusion.126, f32[128,512]{1,0:T(8,128)S(1)} %fusion.88), kind=kOutput, calls=%fused_computation.19 | convolution fusion | flops 6444285952 | bytes 9439232 | tf_op jit(solution)/shard_map/dot_general | solution.py:16
  287.5 50.6 %collective-permute-done.6 = f32[512,512]{1,0:T(8,128)} collective-permute-done((f32[512,512]{1,0:T(8,128)}, f32[512,512]{1,0:T(8,128)}, u32[]{:S(2)}, u32[]{:S(2)}) %collective-permute-start.6) | collective-permute-done | bytes 1048608 | tf_op jit(solution)/shard_map/ppermute | solution.py:108
  355.0 11.7 %cholesky.446 = f32[128,128]{1,0:T(8,128)S(1)} custom-call(f32[128,128]{1,0:T(8,128)S(1)} %cholesky.599), custom_call_target="Cholesky" | custom-call | tf_op jit(solution)/shard_map/jit(cholesky)/cholesky | solution.py:80
  366.7 10.0 %custom-call.35 = f32[1,128,128]{1,2,0:T(8,128)S(1)} custom-call(f32[1,128,128]{2,1,0:T(8,128)S(1)} %get-tuple-element.145), custom_call_target="InvertDiagBlocksLowerTriangular" | custom-call | tf_op jit(solution)/shard_map/jit(cholesky)/cholesky | solution.py:80
  379.4 11.7 %cholesky.465 = f32[128,128]{1,0:T(8,128)S(1)} custom-call(f32[128,128]{1,0:T(8,128)S(1)} %cholesky.603), custom_call_target="Cholesky" | custom-call | tf_op jit(solution)/shard_map/jit(cholesky)/cholesky | solution.py:80
  391.1 9.8 %custom-call.36 = f32[1,128,128]{1,2,0:T(8,128)S(1)} custom-call(f32[1,128,128]{2,1,0:T(8,128)S(1)} %get-tuple-element.142), custom_call_target="InvertDiagBlocksLowerTriangular" | custom-call | tf_op jit(solution)/shard_map/jit(cholesky)/cholesky | solution.py:80
  402.5 11.7 %cholesky.486 = f32[128,128]{1,0:T(8,128)S(1)} custom-call(f32[128,128]{1,0:T(8,128)S(1)} %cholesky.608), custom_call_target="Cholesky" | custom-call | tf_op jit(solution)/shard_map/jit(cholesky)/cholesky | solution.py:80
  414.3 10.2 %custom-call.37 = f32[1,128,128]{1,2,0:T(8,128)S(1)} custom-call(f32[1,128,128]{2,1,0:T(8,128)S(1)} %get-tuple-element.139), custom_call_target="InvertDiagBlocksLowerTriangular" | custom-call | tf_op jit(solution)/shard_map/jit(cholesky)/cholesky | solution.py:80
  434.4 11.7 %cholesky.503 = f32[128,128]{1,0:T(8,128)S(1)} custom-call(f32[128,128]{1,0:T(8,128)S(1)} %convolution_subtract_fusion.19), custom_call_target="Cholesky" | custom-call | tf_op jit(solution)/shard_map/jit(cholesky)/cholesky | solution.py:80
  453.2 11.6 %while.11 = (s32[]{:T(128)}, f32[512,512]{1,0:T(8,128)}, s32[4,2]{0,1:T(2,128)S(1)}, f32[4,128,128]{2,1,0:T(8,128)S(1)}, s32[]{:T(128)}) while((s32[]{:T(128)}, f32[512,512]{1,0:T(8,128)}, s32[4,2]{0,1:T(2,128)S(1)}, f32[4,128,128]{2,1,0:T(8,128)S(1)}, s32[]{:T(128)}) %tuple.115), condition=%wide.while_cond.4.clone, body=%wide.while_body.4.clone.sunk | while | flops 2 | bytes 131189 | solution.py:81
  464.8 39.5 %custom-call.38 = f32[4,128,128]{1,2,0:T(8,128)S(1)} custom-call(f32[4,128,128]{2,1,0:T(8,128)S(1)} %get-tuple-element.76), custom_call_target="InvertDiagBlocksLowerTriangular" | custom-call | tf_op jit(solution)/shard_map/jit(_solve_triangular)/triangular_solve | solution.py:81
  528.7 9.9 %fusion.17 = f32[2048,512]{1,0:T(8,128)} fusion(f32[2048,512]{1,0:T(8,128)S(1)} %fusion.186, f32[2048,4096]{1,0:T(8,128)} %param.12, pred[2048]{0:T(1024)(128)(4,1)S(1)} %broadcast_compare_fusion.2, f32[128,512]{1,0:T(8,128)S(1)} %fusion.117, f32[128,512]{1,0:T(8,128)S(1)} %fusion.118, f32[128,512]{1,0:T(8,128)S(1)} %fusion.120, f32[128,512]{1,0:T(8,128)S(1)} %fusion.86), kind=kOutput, calls=%fused_computation.24 | convolution fusion | flops 6445334528 | bytes 13633536 | tf_op jit(solution)/shard_map/dot_general | solution.py:16
  554.5 11.2 %collective-permute-done.12 = f32[512,512]{1,0:T(8,128)S(1)} collective-permute-done((f32[512,512]{1,0:T(8,128)S(1)}, f32[512,512]{1,0:T(8,128)S(1)}, u32[]{:S(2)}, u32[]{:S(2)}) %collective-permute-start.12) | collective-permute-done | bytes 1048608 | tf_op jit(solution)/shard_map/ppermute | solution.py:108
  565.7 11.2 %collective-permute-done.11 = f32[512,512]{1,0:T(8,128)S(1)} collective-permute-done((f32[512,512]{1,0:T(8,128)S(1)}, f32[512,512]{1,0:T(8,128)S(1)}, u32[]{:S(2)}, u32[]{:S(2)}) %collective-permute-start.11) | collective-permute-done | bytes 1048608 | tf_op jit(solution)/shard_map/ppermute | solution.py:108
  577.0 10.0 %collective-permute-done.10 = f32[512,512]{1,0:T(8,128)S(1)} collective-permute-done((f32[512,512]{1,0:T(8,128)S(1)}, f32[512,512]{1,0:T(8,128)S(1)}, u32[]{:S(2)}, u32[]{:S(2)}) %collective-permute-start.10) | collective-permute-done | bytes 1048608 | tf_op jit(solution)/shard_map/ppermute | solution.py:108
  617.5 11.9 %cholesky.518 = f32[128,128]{1,0:T(8,128)S(1)} custom-call(f32[128,128]{1,0:T(8,128)S(1)} %cholesky.612), custom_call_target="Cholesky" | custom-call | tf_op jit(solution)/shard_map/jit(cholesky)/cholesky | solution.py:80
  643.7 11.7 %cholesky.537 = f32[128,128]{1,0:T(8,128)S(1)} custom-call(f32[128,128]{1,0:T(8,128)S(1)} %cholesky.616), custom_call_target="Cholesky" | custom-call | tf_op jit(solution)/shard_map/jit(cholesky)/cholesky | solution.py:80
  668.2 11.9 %cholesky.558 = f32[128,128]{1,0:T(8,128)S(1)} custom-call(f32[128,128]{1,0:T(8,128)S(1)} %cholesky.621), custom_call_target="Cholesky" | custom-call | tf_op jit(solution)/shard_map/jit(cholesky)/cholesky | solution.py:80
  692.8 11.7 %cholesky.575 = f32[128,128]{1,0:T(8,128)S(1)} custom-call(f32[128,128]{1,0:T(8,128)S(1)} %convolution_subtract_fusion.18), custom_call_target="Cholesky" | custom-call | tf_op jit(solution)/shard_map/jit(cholesky)/cholesky | solution.py:80
  722.0 10.7 %while.12 = (s32[]{:T(128)}, f32[512,512]{1,0:T(8,128)}, s32[4,2]{0,1:T(2,128)S(1)}, f32[4,128,128]{2,1,0:T(8,128)S(1)}, s32[]{:T(128)}) while((s32[]{:T(128)}, f32[512,512]{1,0:T(8,128)}, s32[4,2]{0,1:T(2,128)S(1)}, f32[4,128,128]{2,1,0:T(8,128)S(1)}, s32[]{:T(128)}) %tuple.116), condition=%wide.while_cond.4.clone.1, body=%wide.while_body.4.clone.1.sunk | while | flops 2 | bytes 131189 | solution.py:81
  732.7 39.9 %custom-call.42 = f32[4,128,128]{1,2,0:T(8,128)} custom-call(f32[4,128,128]{2,1,0:T(8,128)S(1)} %get-tuple-element.77), custom_call_target="InvertDiagBlocksLowerTriangular" | custom-call | tf_op jit(solution)/shard_map/jit(_solve_triangular)/triangular_solve | solution.py:81
  815.6 10.3 %fusion.20 = f32[2048,512]{1,0:T(8,128)} fusion(f32[2048,512]{1,0:T(8,128)S(1)} %fusion.188, f32[2048,512]{1,0:T(8,128)S(1)} %copy-done.2, f32[2048,4096]{1,0:T(8,128)} %param.12, pred[2048]{0:T(1024)(128)(4,1)S(1)} %broadcast_compare_fusion, f32[128,512]{1,0:T(8,128)S(1)} %copy-done.29, f32[128,512]{1,0:T(8,128)S(1)} %copy-done.22, ...), kind=kOutput, calls=%fused_computation.25 | convolution fusion | flops 6446383104 | bytes 17827840 | tf_op jit(solution)/shard_map/dot_general | solution.py:16
  835.8 67.4 %subtract_select_fusion = f32[2048,4096]{1,0:T(8,128)} fusion(f32[2048,4096]{1,0:T(8,128)} %param.12, f32[4096,512]{1,0:T(8,128)} %bitcast.190, f32[4096,512]{1,0:T(8,128)} %bitcast.189, s32[4096]{0:T(1024)S(1)} %fusion.147, s32[2048]{0:T(1024)S(1)} %fusion.161, pred[2048]{0:T(1024)(128)(4,1)S(1)} %broadcast_compare_fusion.3, f32[2048,512]{1,0:T(8,128)} %copy-done.3, ...), kind=kOutput, calls=%fused_computation.6 | convolution fusion | flops 51579453440 | bytes 92301312 | tf_op jit(solution)/shard_map/dot_general | solution.py:16
  (265 shorter events, 317.5 us)
Async XLA Ops:
  6.5 75.2 %all-gather.4.cloned.1.call-start = ((), (), s32[]{:S(2)}) async-start(), calls=%async_computation | async-start | bytes 4718592 | tf_op jit(solution)/shard_map/all_gather | solution.py:60
  8.4 788.5 %all-gather.6.cloned.1.call-start = ((), (), s32[]{:S(2)}) async-start(), calls=%async_computation.1 | async-start | bytes 9437184 | tf_op jit(solution)/shard_map/all_gather | solution.py:110
  85.1 35.3 %collective-permute-start = (f32[2,512,512]{1,2,0:T(8,128)}, f32[2,512,512]{1,2,0:T(8,128)}, u32[]{:S(2)}, u32[]{:S(2)}) collective-permute-start(f32[2,512,512]{1,2,0:T(8,128)} %copy.22), channel_id=1, source_target_pairs={{0,2},{4,6},{8,10},{12,14},{16,18},{20,22},{24,26},{28,30}} | collective-permute-start | bytes 6291464 | tf_op jit(solution)/shard_map/ppermute | solution.py:64
  94.1 26.3 %collective-permute-start.1 = (f32[512,512]{0,1:T(8,128)}, f32[512,512]{0,1:T(8,128)}, u32[]{:S(2)}, u32[]{:S(2)}) collective-permute-start(f32[512,512]{0,1:T(8,128)} %copy.23), channel_id=1, source_target_pairs={{0,1},{1,2},{4,5},{5,6},{8,9},{9,10},{12,13},{13,14},{16,17},{17,1... | collective-permute-start | bytes 3145736 | tf_op jit(solution)/shard_map/ppermute | solution.py:63
  220.5 39.8 %copy-start.17 = (f32[512,512]{1,0:T(8,128)}, f32[512,512]{1,0:T(8,128)S(1)}, u32[]{:S(2)}) copy-start(f32[512,512]{1,0:T(8,128)S(1)} %get-tuple-element.307) | copy-start | bytes 3145732
  260.3 83.8 %copy-start.4 = (f32[128,512]{1,0:T(8,128)}, f32[128,512]{1,0:T(8,128)S(1)}, u32[]{:S(2)}) copy-start(f32[128,512]{1,0:T(8,128)S(1)} %fusion.88) | copy-start | bytes 786436
  261.4 82.8 %copy-start.7 = (f32[128,512]{1,0:T(8,128)}, f32[128,512]{1,0:T(8,128)S(1)}, u32[]{:S(2)}) copy-start(f32[128,512]{1,0:T(8,128)S(1)} %fusion.126) | copy-start | bytes 786436
  263.8 80.4 %copy-start.16 = (f32[128,512]{1,0:T(8,128)}, f32[128,512]{1,0:T(8,128)S(1)}, u32[]{:S(2)}) copy-start(f32[128,512]{1,0:T(8,128)S(1)} %fusion.124) | copy-start | bytes 786436
  266.7 77.5 %copy-start.28 = (f32[128,512]{1,0:T(8,128)}, f32[128,512]{1,0:T(8,128)S(1)}, u32[]{:S(2)}) copy-start(f32[128,512]{1,0:T(8,128)S(1)} %fusion.123) | copy-start | bytes 786436
  281.0 61.8 %copy-start.11 = (f32[512,512]{1,0:T(8,128)S(1)}, f32[512,512]{1,0:T(8,128)}, u32[]{:S(2)}) copy-start(f32[512,512]{1,0:T(8,128)} %get-tuple-element.116) | copy-start | bytes 3145732
  281.1 6.4 collective-permute-start.9
  282.8 4.6 collective-permute-start.8
  284.5 3.0 collective-permute-start.7
  286.1 52.0 %collective-permute-start.6 = (f32[512,512]{1,0:T(8,128)}, f32[512,512]{1,0:T(8,128)}, u32[]{:S(2)}, u32[]{:S(2)}) collective-permute-start(f32[512,512]{1,0:T(8,128)} %get-tuple-element.121), channel_id=1, source_target_pairs={{0,24},{4,28},{8,25},{12,29},{16,26},{20,30},{24,27},{28,31}} | collective-permute-start | bytes 3145736 | tf_op jit(solution)/shard_map/ppermute | solution.py:108
  341.3 486.5 %all-gather.8.cloned.1.call-start = ((), (), s32[]{:S(2)}) async-start(), calls=%async_computation.2 | async-start | bytes 9437184 | tf_op jit(solution)/shard_map/all_gather | solution.py:110
  341.3 83.3 %collective-permute-start.2 = (f32[2048,512]{1,0:T(8,128)}, f32[2048,512]{1,0:T(8,128)}, u32[]{:S(2)}, u32[]{:S(2)}) collective-permute-start(f32[2048,512]{1,0:T(8,128)} %select_bitcast_fusion), channel_id=1, source_target_pairs={{0,1},{4,5},{8,9},{12,13},{16,17},{20,21},{24,25},{28,29}} | collective-permute-start | bytes 12582920 | tf_op jit(solution)/shard_map/ppermute | solution.py:31
  429.9 88.4 %collective-permute-start.3 = (f32[2048,512]{1,0:T(8,128)}, f32[2048,512]{1,0:T(8,128)}, u32[]{:S(2)}, u32[]{:S(2)}) collective-permute-start(f32[2048,512]{1,0:T(8,128)} %broadcast_select_fusion.1), channel_id=1, source_target_pairs={{0,2},{1,3},{4,6},{5,7},{8,10},{9,11},{12,14},{13,15},{16,18},{17,... | collective-permute-start | bytes 12582920 | tf_op jit(solution)/shard_map/ppermute | solution.py:31
  506.6 22.1 %copy-start.5 = (f32[128,512]{1,0:T(8,128)}, f32[128,512]{1,0:T(8,128)S(1)}, u32[]{:S(2)}) copy-start(f32[128,512]{1,0:T(8,128)S(1)} %fusion.120) | copy-start | bytes 786436
  509.0 19.7 %copy-start.13 = (f32[128,512]{1,0:T(8,128)}, f32[128,512]{1,0:T(8,128)S(1)}, u32[]{:S(2)}) copy-start(f32[128,512]{1,0:T(8,128)S(1)} %fusion.118) | copy-start | bytes 786436
  512.8 15.9 %copy-start.23 = (f32[128,512]{1,0:T(8,128)}, f32[128,512]{1,0:T(8,128)S(1)}, u32[]{:S(2)}) copy-start(f32[128,512]{1,0:T(8,128)S(1)} %fusion.117) | copy-start | bytes 786436
  541.3 49.2 %copy-start.10 = (f32[512,512]{1,0:T(8,128)S(1)}, f32[512,512]{1,0:T(8,128)}, u32[]{:S(2)}) copy-start(f32[512,512]{1,0:T(8,128)} %get-tuple-element.114) | copy-start | bytes 3145732
  541.3 13.2 %collective-permute-start.13 = (f32[512,512]{1,0:T(8,128)S(1)}, f32[512,512]{1,0:T(8,128)S(1)}, u32[]{:S(2)}, u32[]{:S(2)}) collective-permute-start(f32[512,512]{1,0:T(8,128)S(1)} %get-tuple-element.122), channel_id=1, source_target_pairs={{1,0},{5,4},{9,1},{13,5},{17,2},{21,6},{25,3},{29,7}} | collective-permute-start | bytes 3145736 | tf_op jit(solution)/shard_map/ppermute | solution.py:108
  542.8 22.9 %collective-permute-start.12 = (f32[512,512]{1,0:T(8,128)S(1)}, f32[512,512]{1,0:T(8,128)S(1)}, u32[]{:S(2)}, u32[]{:S(2)}) collective-permute-start(f32[512,512]{1,0:T(8,128)S(1)} %get-tuple-element.123), channel_id=1, source_target_pairs={{1,8},{5,12},{9,9},{13,13},{17,10},{21,14},{25,11},{29,15}} | collective-permute-start | bytes 3145736 | tf_op jit(solution)/shard_map/ppermute | solution.py:108
  544.2 32.8 %collective-permute-start.11 = (f32[512,512]{1,0:T(8,128)S(1)}, f32[512,512]{1,0:T(8,128)S(1)}, u32[]{:S(2)}, u32[]{:S(2)}) collective-permute-start(f32[512,512]{1,0:T(8,128)S(1)} %get-tuple-element.124), channel_id=1, source_target_pairs={{1,16},{5,20},{9,17},{13,21},{17,18},{21,22},{25,19},{29,23}} | collective-permute-start | bytes 3145736 | tf_op jit(solution)/shard_map/ppermute | solution.py:108
  545.5 41.4 %collective-permute-start.10 = (f32[512,512]{1,0:T(8,128)S(1)}, f32[512,512]{1,0:T(8,128)S(1)}, u32[]{:S(2)}, u32[]{:S(2)}) collective-permute-start(f32[512,512]{1,0:T(8,128)S(1)} %get-tuple-element.125), channel_id=1, source_target_pairs={{1,24},{5,28},{9,25},{13,29},{17,26},{21,30},{25,27},{29,31}} | collective-permute-start | bytes 3145736 | tf_op jit(solution)/shard_map/ppermute | solution.py:108
  591.8 12.0 %copy-start.6 = (f32[128,512]{1,0:T(8,128)S(1)}, f32[128,512]{1,0:T(8,128)}, u32[]{:S(2)}) copy-start(f32[128,512]{1,0:T(8,128)} %copy-done.5) | copy-start | bytes 786436
  591.8 12.0 %copy-start.14 = (f32[128,512]{1,0:T(8,128)S(1)}, f32[128,512]{1,0:T(8,128)}, u32[]{:S(2)}) copy-start(f32[128,512]{1,0:T(8,128)} %copy-done.13) | copy-start | bytes 786436
  591.9 12.0 %copy-start.24 = (f32[128,512]{1,0:T(8,128)S(1)}, f32[128,512]{1,0:T(8,128)}, u32[]{:S(2)}) copy-start(f32[128,512]{1,0:T(8,128)} %copy-done.23) | copy-start | bytes 786436
  596.9 113.3 %collective-permute-start.4 = (f32[2048,512]{1,0:T(8,128)}, f32[2048,512]{1,0:T(8,128)}, u32[]{:S(2)}, u32[]{:S(2)}) collective-permute-start(f32[2048,512]{1,0:T(8,128)} %fusion.17), channel_id=1, source_target_pairs={{1,0},{5,4},{9,8},{13,12},{17,16},{21,20},{25,24},{29,28}} | collective-permute-start | bytes 12582920 | tf_op jit(solution)/shard_map/ppermute | solution.py:31
  715.4 89.5 %collective-permute-start.5 = (f32[2048,512]{1,0:T(8,128)}, f32[2048,512]{1,0:T(8,128)}, u32[]{:S(2)}, u32[]{:S(2)}) collective-permute-start(f32[2048,512]{1,0:T(8,128)} %broadcast_select_fusion), channel_id=1, source_target_pairs={{1,3},{0,2},{5,7},{4,6},{9,11},{8,10},{13,15},{12,14},{17,19},{16,... | collective-permute-start | bytes 12582920 | tf_op jit(solution)/shard_map/ppermute | solution.py:31
  772.6 12.0 %copy-start.25 = (f32[512,512]{1,0:T(8,128)S(1)}, f32[512,512]{1,0:T(8,128)}, u32[]{:S(2)}) copy-start(f32[512,512]{1,0:T(8,128)} %get-tuple-element.107) | copy-start | bytes 3145732
  772.6 14.0 %copy-start.1 = (f32[2048,512]{1,0:T(8,128)S(1)}, f32[2048,512]{1,0:T(8,128)}, u32[]{:S(2)}) copy-start(f32[2048,512]{1,0:T(8,128)} %copy-done) | copy-start | bytes 12582916
  (17 other events, 97.6 us)
Sparse Core Ops, SparseCore 0:
  9.5 72.1 all-gather.3
  341.4 121.0 all-gather.5
  589.9 121.4 all-gather.7

commit v3 on v2

--- a/solution.py
+++ b/solution.py
@@ -5,6 +5,7 @@
 
 NB = 512
 STEPS = 2
+SUB = 128
 
 
 def global_index(count, block, grid, position):
@@ -77,9 +78,45 @@
     g22 = pick([(2, colblk[2])], identity)
 
     def factor(diag):
-        low_factor = jnp.linalg.cholesky(diag)
-        inverse = jax.scipy.linalg.solve_triangular(low_factor, identity, lower=True)
-        return low_factor, inverse
+        sym = (diag + diag.T) * 0.5
+        side = SUB
+        count = NB // side
+        eye_sub = jnp.eye(side, dtype=jnp.float32)
+        diag_factors = []
+        diag_inverses = []
+        below_blocks = []
+        rest = sym
+        for step in range(count):
+            lead = rest[0:side, 0:side]
+            low = jnp.linalg.cholesky(lead)
+            inv = jax.scipy.linalg.solve_triangular(low, eye_sub, lower=True)
+            diag_factors.append(low)
+            diag_inverses.append(inv)
+            if step + 1 < count:
+                below = times_transposed(rest[side:, 0:side], inv)
+                below_blocks.append(below)
+                rest = rest[side:, side:] - times_transposed(below, below)
+        low_factor = jnp.zeros((NB, NB), jnp.float32)
+        for step in range(count):
+            at = step * side
+            low_factor = low_factor.at[at : at + side, at : at + side].set(diag_factors[step])
+            if step + 1 < count:
+                low_factor = low_factor.at[at + side :, at : at + side].set(below_blocks[step])
+
+        def invert(first, size):
+            if size == side:
+                return diag_inverses[first // side]
+            half = size // 2
+            top = invert(first, half)
+            bottom = invert(first + half, half)
+            corner = low_factor[first + half : first + size, first : first + half]
+            mixed = -jnp.dot(bottom, jnp.dot(corner, top, precision=lax.Precision.HIGHEST),
+                             precision=lax.Precision.HIGHEST)
+            upper = jnp.concatenate([top, jnp.zeros((half, half), jnp.float32)], axis=1)
+            lower = jnp.concatenate([mixed, bottom], axis=1)
+            return jnp.concatenate([upper, lower], axis=0)
+
+        return low_factor, invert(0, NB)
 
     panel_in = gram[:, 0:NB]
 

time: 935 us -> 839 us (0.90)
  the two profiles are of different devices: /device:TPU:25 before, /device:TPU:26 now
where the time goes in v3:
time: 839 us; the launch traced here: 827 us
  other arithmetic  336 us (40%)
  waiting for transfers between devices  242 us (29%)
  matrix products  169 us (20%)
  local copies, waits for them, and re-layouts  45.4 us (5%)
  starting transfers between devices  19.8 us (2%)
  between operations  15.1 us (2%)
    dot_general x32, matrix products, times_transposed(): lax.dot_general(left, right, (((1,), (1,)), ((), ())), precision=precisio...  157 us
    another operation x36, other arithmetic, factor(): low = jnp.linalg.cholesky(lead)  153 us
    another operation x21, other arithmetic, factor(): inv = jax.scipy.linalg.solve_triangular(low, eye_sub, lower=True)  126 us
    ppermute x4, waiting for transfers between devices, bcast_col(): got = lax.ppermute(held, 'col', route)  79.3 us
    all_gather x1, waiting for transfers between devices, local(): colblk = lax.all_gather(tile, 'row', axis=0, tiled=True)  73.3 us
    ppermute x8, waiting for transfers between devices, spread_columns_of(): received = lax.ppermute(pieces[piece], ('row', 'col'), route)  57.1 us
    ppermute x1, waiting for transfers between devices, local(): recv_a = lax.ppermute(send_a, 'col', [(0, 1), (1, 2)])  24.8 us
    select_n x4, other arithmetic, bcast_col(): held = jnp.where(is_target, got, held)  16.9 us
  transfers between devices with their start and end apart: 17, of which 7 were waited for; matrix products, arithmetic and copies ran while one was open for 41% of the time, Pallas kernels for 0%

profile of v3, /device:TPU:26, one launch (start us, length us, event | category | flops | bytes accessed | tf_op | source)
XLA Modules:
  0.0 827.1 jit_solution(3861957509615405452)
XLA Ops:
  8.5 73.3 %all-gather.4.cloned.1.call-done = f32[2048,512]{1,0:T(8,128)} async-done(((f32[256,512]{1,0:T(8,128)}), f32[2048,512]{1,0:T(8,128)}) %all-gather.4.cloned.1.call-update) | async-done | bytes 4194320 | tf_op jit(solution)/shard_map/all_gather | solution.py:61
  92.8 24.8 %collective-permute-done.1 = f32[512,512]{0,1:T(8,128)S(1)} collective-permute-done((f32[512,512]{0,1:T(8,128)}, f32[512,512]{0,1:T(8,128)S(1)}, u32[]{:S(2)}, u32[]{:S(2)}) %collective-permute-start.1) | collective-permute-done | bytes 1048608 | tf_op jit(solution)/shard_map/ppermute | solution.py:64
  129.2 11.7 %cholesky.194 = f32[128,128]{1,0:T(8,128)S(1)} custom-call(f32[128,128]{1,0:T(8,128)S(1)} %fusion.151), custom_call_target="Cholesky" | custom-call | tf_op jit(solution)/shard_map/jit(cholesky)/cholesky | solution.py:91
  142.1 9.8 %custom-call.16 = f32[1,128,128]{1,2,0:T(8,128)S(1)} custom-call(f32[1,128,128]{2,1,0:T(8,128)S(1)} %get-tuple-element.311), custom_call_target="InvertDiagBlocksLowerTriangular" | custom-call | tf_op jit(solution)/shard_map/jit(_solve_triangular)/triangular_solve | solution.py:92
  155.6 12.0 %cholesky.205 = f32[128,128]{1,0:T(8,128)S(1)} custom-call(f32[128,128]{1,0:T(8,128)S(1)} %fusion.149), custom_call_target="Cholesky" | custom-call | tf_op jit(solution)/shard_map/jit(cholesky)/cholesky | solution.py:91
  169.0 9.8 %custom-call.17 = f32[1,128,128]{1,2,0:T(8,128)S(1)} custom-call(f32[1,128,128]{2,1,0:T(8,128)S(1)} %get-tuple-element.340), custom_call_target="InvertDiagBlocksLowerTriangular" | custom-call | tf_op jit(solution)/shard_map/jit(_solve_triangular)/triangular_solve | solution.py:92
  180.1 11.7 %cholesky.216 = f32[128,128]{1,0:T(8,128)S(1)} custom-call(f32[128,128]{1,0:T(8,128)S(1)} %fusion.147), custom_call_target="Cholesky" | custom-call | tf_op jit(solution)/shard_map/jit(cholesky)/cholesky | solution.py:91
  193.1 9.8 %custom-call.18 = f32[1,128,128]{1,2,0:T(8,128)S(1)} custom-call(f32[1,128,128]{2,1,0:T(8,128)S(1)} %get-tuple-element.337), custom_call_target="InvertDiagBlocksLowerTriangular" | custom-call | tf_op jit(solution)/shard_map/jit(_solve_triangular)/triangular_solve | solution.py:92
  203.9 11.9 %cholesky.227 = f32[128,128]{1,0:T(8,128)S(1)} custom-call(f32[128,128]{1,0:T(8,128)S(1)} %fusion.145), custom_call_target="Cholesky" | custom-call | tf_op jit(solution)/shard_map/jit(cholesky)/cholesky | solution.py:91
  218.3 9.8 %custom-call.19 = f32[1,128,128]{1,2,0:T(8,128)S(1)} custom-call(f32[1,128,128]{2,1,0:T(8,128)S(1)} %get-tuple-element.335), custom_call_target="InvertDiagBlocksLowerTriangular" | custom-call | tf_op jit(solution)/shard_map/jit(_solve_triangular)/triangular_solve | solution.py:92
  246.5 18.9 %collective-permute-done.6 = f32[512,512]{1,0:T(8,128)} collective-permute-done((f32[512,512]{1,0:T(8,128)}, f32[512,512]{1,0:T(8,128)}, u32[]{:S(2)}, u32[]{:S(2)}) %collective-permute-start.6) | collective-permute-done | bytes 1048608 | tf_op jit(solution)/shard_map/ppermute | solution.py:145
  281.8 11.7 %cholesky.238 = f32[128,128]{1,0:T(8,128)S(1)} custom-call(f32[128,128]{1,0:T(8,128)S(1)} %fusion.143), custom_call_target="Cholesky" | custom-call | tf_op jit(solution)/shard_map/jit(cholesky)/cholesky | solution.py:91
  294.9 10.2 %custom-call.20 = f32[1,128,128]{1,2,0:T(8,128)S(1)} custom-call(f32[1,128,128]{2,1,0:T(8,128)S(1)} %get-tuple-element.309), custom_call_target="InvertDiagBlocksLowerTriangular" | custom-call | tf_op jit(solution)/shard_map/jit(_solve_triangular)/triangular_solve | solution.py:92
  308.8 11.7 %cholesky.249 = f32[128,128]{1,0:T(8,128)S(1)} custom-call(f32[128,128]{1,0:T(8,128)S(1)} %fusion.141), custom_call_target="Cholesky" | custom-call | tf_op jit(solution)/shard_map/jit(cholesky)/cholesky | solution.py:91
  321.8 9.8 %custom-call.21 = f32[1,128,128]{1,2,0:T(8,128)S(1)} custom-call(f32[1,128,128]{2,1,0:T(8,128)S(1)} %get-tuple-element.334), custom_call_target="InvertDiagBlocksLowerTriangular" | custom-call | tf_op jit(solution)/shard_map/jit(_solve_triangular)/triangular_solve | solution.py:92
  340.2 11.7 %cholesky.260 = f32[128,128]{1,0:T(8,128)S(1)} custom-call(f32[128,128]{1,0:T(8,128)S(1)} %fusion.139), custom_call_target="Cholesky" | custom-call | tf_op jit(solution)/shard_map/jit(cholesky)/cholesky | solution.py:91
  353.3 9.8 %custom-call.22 = f32[1,128,128]{1,2,0:T(8,128)S(1)} custom-call(f32[1,128,128]{2,1,0:T(8,128)S(1)} %get-tuple-element.331), custom_call_target="InvertDiagBlocksLowerTriangular" | custom-call | tf_op jit(solution)/shard_map/jit(_solve_triangular)/triangular_solve | solution.py:92
  364.1 11.7 %cholesky.271 = f32[128,128]{1,0:T(8,128)S(1)} custom-call(f32[128,128]{1,0:T(8,128)S(1)} %fusion.137), custom_call_target="Cholesky" | custom-call | tf_op jit(solution)/shard_map/jit(cholesky)/cholesky | solution.py:91
  377.1 10.0 %custom-call.23 = f32[1,128,128]{1,2,0:T(8,128)S(1)} custom-call(f32[1,128,128]{2,1,0:T(8,128)S(1)} %get-tuple-element.329), custom_call_target="InvertDiagBlocksLowerTriangular" | custom-call | tf_op jit(solution)/shard_map/jit(_solve_triangular)/triangular_solve | solution.py:92
  391.0 65.8 %collective-permute-done.3 = f32[2048,512]{1,0:T(8,128)} collective-permute-done((f32[2048,512]{1,0:T(8,128)}, f32[2048,512]{1,0:T(8,128)}, u32[]{:S(2)}, u32[]{:S(2)}) %collective-permute-start.3) | collective-permute-done | bytes 4194336 | tf_op jit(solution)/shard_map/ppermute | solution.py:32
  466.9 10.4 %fusion.17 = f32[2048,512]{1,0:T(8,128)} fusion(f32[2048,512]{1,0:T(8,128)S(1)} %fusion.209, f32[2048,4096]{1,0:T(8,128)} %param.54, pred[2048]{0:T(1024)(128)(4,1)S(1)} %broadcast_compare_fusion.2, f32[256,256]{1,0:T(8,128)S(1)} %select_maximum_fusion.7, f32[128,128]{1,0:T(8,128)S(1)} %copy.88, f32[128,128]{1,0:T(8,128)S(1)} %convolution_negate_fusion.5, ...), kind=kOutput, calls=%fused_computation.18 | convolution fusion | flops 6446120960 | bytes 13371392 | tf_op jit(solution)/shard_map/dot_general | solution.py:17
  483.6 38.1 %collective-permute-done.10 = f32[512,512]{1,0:T(8,128)S(1)} collective-permute-done((f32[512,512]{1,0:T(8,128)S(1)}, f32[512,512]{1,0:T(8,128)S(1)}, u32[]{:S(2)}, u32[]{:S(2)}) %collective-permute-start.10) | collective-permute-done | bytes 1048608 | tf_op jit(solution)/shard_map/ppermute | solution.py:145
  551.1 11.7 %cholesky.282 = f32[128,128]{1,0:T(8,128)S(1)} custom-call(f32[128,128]{1,0:T(8,128)S(1)} %fusion.135), custom_call_target="Cholesky" | custom-call | tf_op jit(solution)/shard_map/jit(cholesky)/cholesky | solution.py:91
  564.3 10.0 %custom-call.24 = f32[1,128,128]{1,2,0:T(8,128)S(1)} custom-call(f32[1,128,128]{2,1,0:T(8,128)S(1)} %get-tuple-element.307), custom_call_target="InvertDiagBlocksLowerTriangular" | custom-call | tf_op jit(solution)/shard_map/jit(_solve_triangular)/triangular_solve | solution.py:92
  579.8 11.7 %cholesky.293 = f32[128,128]{1,0:T(8,128)S(1)} custom-call(f32[128,128]{1,0:T(8,128)S(1)} %fusion.133), custom_call_target="Cholesky" | custom-call | tf_op jit(solution)/shard_map/jit(cholesky)/cholesky | solution.py:91
  592.9 9.8 %custom-call.25 = f32[1,128,128]{1,2,0:T(8,128)S(1)} custom-call(f32[1,128,128]{2,1,0:T(8,128)S(1)} %get-tuple-element.328), custom_call_target="InvertDiagBlocksLowerTriangular" | custom-call | tf_op jit(solution)/shard_map/jit(_solve_triangular)/triangular_solve | solution.py:92
  610.1 13.6 %cholesky.304 = f32[128,128]{1,0:T(8,128)} custom-call(f32[128,128]{1,0:T(8,128)} %fusion.131), custom_call_target="Cholesky" | custom-call | tf_op jit(solution)/shard_map/jit(cholesky)/cholesky | solution.py:91
  647.1 12.5 %cholesky.315 = f32[128,128]{1,0:T(8,128)S(1)} custom-call(f32[128,128]{1,0:T(8,128)} %fusion.129), custom_call_target="Cholesky" | custom-call | tf_op jit(solution)/shard_map/jit(cholesky)/cholesky | solution.py:91
  661.5 10.6 %custom-call.27 = f32[1,128,128]{1,2,0:T(8,128)S(1)} custom-call(f32[1,128,128]{2,1,0:T(8,128)} %get-tuple-element.323), custom_call_target="InvertDiagBlocksLowerTriangular" | custom-call | tf_op jit(solution)/shard_map/jit(_solve_triangular)/triangular_solve | solution.py:92
  700.5 13.5 %collective-permute-done.5 = f32[2048,512]{1,0:T(8,128)} collective-permute-done((f32[2048,512]{1,0:T(8,128)}, f32[2048,512]{1,0:T(8,128)}, u32[]{:S(2)}, u32[]{:S(2)}) %collective-permute-start.5) | collective-permute-done | bytes 4194336 | tf_op jit(solution)/shard_map/ppermute | solution.py:32
  724.6 10.2 %fusion.20 = f32[2048,512]{1,0:T(8,128)} fusion(f32[2048,512]{1,0:T(8,128)S(1)} %fusion.212, f32[2048,512]{1,0:T(8,128)S(1)} %copy-done.3, f32[2048,4096]{1,0:T(8,128)} %param.54, pred[2048]{0:T(1024)(128)(4,1)S(1)} %copy-done.32, f32[256,256]{1,0:T(8,128)S(1)} %copy-done.21, f32[128,128]{1,0:T(8,128)S(1)} %copy.108, ...), kind=kOutput, calls=%fused_computation.19 | convolution fusion | flops 6447169536 | bytes 17565696 | tf_op jit(solution)/shard_map/dot_general | solution.py:17
  744.7 67.3 %subtract_select_fusion = f32[2048,4096]{1,0:T(8,128)} fusion(f32[2048,4096]{1,0:T(8,128)} %param.54, f32[4096,512]{1,0:T(8,128)} %bitcast.212, f32[4096,512]{1,0:T(8,128)} %bitcast.211, s32[4096]{0:T(1024)S(1)} %fusion.171, s32[2048]{0:T(1024)S(1)} %copy-done.33, pred[2048]{0:T(1024)(128)(4,1)S(1)} %copy-done.34, f32[2048,512]{1,0:T(8,128)} %copy-done.4, ...), kind=kOutput, calls=%fused_computation | convolution fusion | flops 51579453440 | bytes 92301312 | tf_op jit(solution)/shard_map/dot_general | solution.py:17
  (287 shorter events, 236.5 us)
Async XLA Ops:
  6.5 75.2 %all-gather.4.cloned.1.call-start = ((), (), s32[]{:S(2)}) async-start(), calls=%async_computation | async-start | bytes 4718592 | tf_op jit(solution)/shard_map/all_gather | solution.py:61
  8.4 684.1 %all-gather.6.cloned.1.call-start = ((), (), s32[]{:S(2)}) async-start(), calls=%async_computation.1 | async-start | bytes 9437184 | tf_op jit(solution)/shard_map/all_gather | solution.py:147
  85.2 39.5 %collective-permute-start = (f32[2,512,512]{1,2,0:T(8,128)}, f32[2,512,512]{1,2,0:T(8,128)}, u32[]{:S(2)}, u32[]{:S(2)}) collective-permute-start(f32[2,512,512]{1,2,0:T(8,128)} %copy.54), channel_id=1, source_target_pairs={{0,2},{4,6},{8,10},{12,14},{16,18},{20,22},{24,26},{28,30}} | collective-permute-start | bytes 6291464 | tf_op jit(solution)/shard_map/ppermute | solution.py:65
  90.1 27.5 %collective-permute-start.1 = (f32[512,512]{0,1:T(8,128)}, f32[512,512]{0,1:T(8,128)S(1)}, u32[]{:S(2)}, u32[]{:S(2)}) collective-permute-start(f32[512,512]{0,1:T(8,128)} %broadcast_select_fusion.4), channel_id=1, source_target_pairs={{0,1},{1,2},{4,5},{5,6},{8,9},{9,10},{12,13},{13,14},{16,17},{17,1... | collective-permute-start | bytes 3145736 | tf_op jit(solution)/shard_map/ppermute | solution.py:64
  117.6 9.6 %copy-start.7 = (f32[512,512]{0,1:T(8,128)}, f32[512,512]{0,1:T(8,128)S(1)}, u32[]{:S(2)}) copy-start(f32[512,512]{0,1:T(8,128)S(1)} %collective-permute-done.1) | copy-start | bytes 3145732
  217.2 20.7 %copy-start.14 = (f32[512,512]{1,0:T(8,128)}, f32[512,512]{1,0:T(8,128)S(1)}, u32[]{:S(2)}) copy-start(f32[512,512]{1,0:T(8,128)S(1)} %get-tuple-element.336) | copy-start | bytes 3145732
  217.9 54.0 %copy-start.24 = (f32[256,256]{1,0:T(8,128)}, f32[256,256]{1,0:T(8,128)S(1)}, u32[]{:S(2)}) copy-start(f32[256,256]{1,0:T(8,128)S(1)} %select_maximum_fusion.8) | copy-start | bytes 786436
  228.5 43.4 %copy-start.27 = (f32[128,128]{1,0:T(8,128)}, f32[128,128]{1,0:T(8,128)S(1)}, u32[]{:S(2)}) copy-start(f32[128,128]{1,0:T(8,128)S(1)} %copy.70) | copy-start | bytes 196612
  229.2 42.7 %copy-start.22 = (f32[256,256]{1,0:T(8,128)}, f32[256,256]{1,0:T(8,128)S(1)}, u32[]{:S(2)}) copy-start(f32[256,256]{1,0:T(8,128)S(1)} %convolution_negate_fusion.2) | copy-start | bytes 786436
  240.2 31.3 %copy-start.8 = (f32[512,512]{0,1:T(8,128)S(1)}, f32[512,512]{0,1:T(8,128)}, u32[]{:S(2)}) copy-start(f32[512,512]{0,1:T(8,128)} %copy-done.7) | copy-start | bytes 3145732
  241.2 5.3 collective-permute-start.9
  241.9 4.6 collective-permute-start.8
  243.6 3.0 collective-permute-start.7
  245.2 20.2 %collective-permute-start.6 = (f32[512,512]{1,0:T(8,128)}, f32[512,512]{1,0:T(8,128)}, u32[]{:S(2)}, u32[]{:S(2)}) collective-permute-start(f32[512,512]{1,0:T(8,128)} %get-tuple-element.316), channel_id=1, source_target_pairs={{0,24},{4,28},{8,25},{12,29},{16,26},{20,30},{24,27},{28,31}} | collective-permute-start | bytes 3145736 | tf_op jit(solution)/shard_map/ppermute | solution.py:145
  268.6 468.1 %all-gather.8.cloned.1.call-start = ((), (), s32[]{:S(2)}) async-start(), calls=%async_computation.2 | async-start | bytes 9437184 | tf_op jit(solution)/shard_map/all_gather | solution.py:147
  268.6 64.0 %collective-permute-start.2 = (f32[2048,512]{1,0:T(8,128)}, f32[2048,512]{1,0:T(8,128)}, u32[]{:S(2)}, u32[]{:S(2)}) collective-permute-start(f32[2048,512]{1,0:T(8,128)} %copy-done.2), channel_id=1, source_target_pairs={{0,1},{4,5},{8,9},{12,13},{16,17},{20,21},{24,25},{28,29}} | collective-permute-start | bytes 12582920 | tf_op jit(solution)/shard_map/ppermute | solution.py:32
  337.9 118.9 %collective-permute-start.3 = (f32[2048,512]{1,0:T(8,128)}, f32[2048,512]{1,0:T(8,128)}, u32[]{:S(2)}, u32[]{:S(2)}) collective-permute-start(f32[2048,512]{1,0:T(8,128)} %broadcast_select_fusion.1), channel_id=1, source_target_pairs={{0,2},{1,3},{4,6},{5,7},{8,10},{9,11},{12,14},{13,15},{16,18},{17,... | collective-permute-start | bytes 12582920 | tf_op jit(solution)/shard_map/ppermute | solution.py:32
  377.1 82.9 %copy-start.12 = (f32[512,512]{1,0:T(8,128)}, f32[512,512]{1,0:T(8,128)S(1)}, u32[]{:S(2)}) copy-start(f32[512,512]{1,0:T(8,128)S(1)} %get-tuple-element.330) | copy-start | bytes 3145732
  387.5 79.4 %copy-start.29 = (f32[128,128]{1,0:T(8,128)}, f32[128,128]{1,0:T(8,128)S(1)}, u32[]{:S(2)}) copy-start(f32[128,128]{1,0:T(8,128)S(1)} %copy.88) | copy-start | bytes 196612
  388.9 78.1 %copy-start.19 = (f32[256,256]{1,0:T(8,128)}, f32[256,256]{1,0:T(8,128)S(1)}, u32[]{:S(2)}) copy-start(f32[256,256]{1,0:T(8,128)S(1)} %select_maximum_fusion.7) | copy-start | bytes 786436
  391.0 75.9 %copy-start.16 = (f32[256,256]{1,0:T(8,128)}, f32[256,256]{1,0:T(8,128)S(1)}, u32[]{:S(2)}) copy-start(f32[256,256]{1,0:T(8,128)S(1)} %convolution_negate_fusion.1) | copy-start | bytes 786436
  479.9 47.2 %copy-start.23 = (f32[256,256]{1,0:T(8,128)S(1)}, f32[256,256]{1,0:T(8,128)}, u32[]{:S(2)}) copy-start(f32[256,256]{1,0:T(8,128)} %copy-done.22) | copy-start | bytes 786436
  479.9 47.2 %copy-start.25 = (f32[256,256]{1,0:T(8,128)S(1)}, f32[256,256]{1,0:T(8,128)}, u32[]{:S(2)}) copy-start(f32[256,256]{1,0:T(8,128)} %copy-done.24) | copy-start | bytes 786436
  479.9 47.2 %copy-start.28 = (f32[128,128]{1,0:T(8,128)S(1)}, f32[128,128]{1,0:T(8,128)}, u32[]{:S(2)}) copy-start(f32[128,128]{1,0:T(8,128)} %copy-done.27) | copy-start | bytes 196612
  479.9 3.6 collective-permute-start.13
  480.8 2.8 collective-permute-start.12
  481.6 2.1 collective-permute-start.11
  482.3 39.5 %collective-permute-start.10 = (f32[512,512]{1,0:T(8,128)S(1)}, f32[512,512]{1,0:T(8,128)S(1)}, u32[]{:S(2)}, u32[]{:S(2)}) collective-permute-start(f32[512,512]{1,0:T(8,128)S(1)} %get-tuple-element.320), channel_id=1, source_target_pairs={{1,24},{5,28},{9,25},{13,29},{17,26},{21,30},{25,27},{29,31}} | collective-permute-start | bytes 3145736 | tf_op jit(solution)/shard_map/ppermute | solution.py:145
  535.6 89.7 %collective-permute-start.4 = (f32[2048,512]{1,0:T(8,128)}, f32[2048,512]{1,0:T(8,128)}, u32[]{:S(2)}, u32[]{:S(2)}) collective-permute-start(f32[2048,512]{1,0:T(8,128)} %fusion.17), channel_id=1, source_target_pairs={{1,0},{5,4},{9,8},{13,12},{17,16},{21,20},{25,24},{29,28}} | collective-permute-start | bytes 12582920 | tf_op jit(solution)/shard_map/ppermute | solution.py:32
  606.4 24.2 %copy-start.26 = (f32[256,256]{0,1:T(8,128)}, f32[256,256]{0,1:T(8,128)S(1)}, u32[]{:S(2)}) copy-start(f32[256,256]{0,1:T(8,128)S(1)} %convolution_subtract_fusion.5) | copy-start | bytes 786436
  630.5 83.4 %collective-permute-start.5 = (f32[2048,512]{1,0:T(8,128)}, f32[2048,512]{1,0:T(8,128)}, u32[]{:S(2)}, u32[]{:S(2)}) collective-permute-start(f32[2048,512]{1,0:T(8,128)} %broadcast_select_fusion), channel_id=1, source_target_pairs={{1,3},{0,2},{5,7},{4,6},{9,11},{8,10},{13,15},{12,14},{17,19},{16,... | collective-permute-start | bytes 12582920 | tf_op jit(solution)/shard_map/ppermute | solution.py:32
  682.1 8.4 %copy-start.13 = (f32[512,512]{1,0:T(8,128)S(1)}, f32[512,512]{1,0:T(8,128)}, u32[]{:S(2)}) copy-start(f32[512,512]{1,0:T(8,128)} %copy-done.12) | copy-start | bytes 3145732
  (21 other events, 117.1 us)
Sparse Core Ops, SparseCore 0:
  9.5 72.2 all-gather.3
  268.7 148.7 all-gather.5
  524.8 122.8 all-gather.7

commit v4 on v3

--- a/solution.py
+++ b/solution.py
@@ -25,22 +25,14 @@
 
 def bcast_col(value, owner, col_id, grid_cols):
     held = value
-    have = [owner]
-    bit = 1
-    while bit < grid_cols:
-        route = [(h, h ^ bit) for h in have if (h ^ bit) < grid_cols]
-        got = lax.ppermute(held, "col", route)
-        targets = [t for _, t in route]
-        is_target = jnp.zeros((), bool)
-        for t in targets:
-            is_target = is_target | (col_id == t)
-        held = jnp.where(is_target, got, held)
-        have = have + targets
-        bit <<= 1
+    for target in range(grid_cols):
+        if target != owner:
+            got = lax.ppermute(value, "col", [(owner, target)])
+            held = jnp.where(col_id == target, got, held)
     return held
 
 
-def local(gram):
+def local_body(gram):
     grid_rows = lax.axis_size("row")
     grid_cols = lax.axis_size("col")
     row_id = lax.axis_index("row")
@@ -54,7 +46,6 @@
     blocks = local_rows // rblock
     grows = global_index(local_rows, rblock, grid_rows, row_id)
     gcols = global_index(local_cols, NB, grid_cols, col_id)
-    row_class = row_id // per_class
     identity = jnp.eye(NB, dtype=jnp.float32)
 
     tile = gram[0:rblock, 0:NB]
@@ -182,5 +173,5 @@
 def solution(mesh):
     placed = (P("row", "col"),)
     return jax.shard_map(
-        local, mesh=mesh, in_specs=placed, out_specs=P("row", "col"), check_vma=False
+        local_body, mesh=mesh, in_specs=placed, out_specs=P("row", "col"), check_vma=False
     )

time: 839 us -> 818 us (0.975)
  the two profiles are of different devices: /device:TPU:26 before, /device:TPU:25 now
where the time goes in v4:
time: 818 us; the launch traced here: 804 us
  other arithmetic  327 us (40%)
  waiting for transfers between devices  217 us (27%)
  matrix products  169 us (21%)
  local copies, waits for them, and re-layouts  41.7 us (5%)
  starting transfers between devices  33.8 us (4%)
  between operations  15 us (2%)
    dot_general x32, matrix products, times_transposed(): lax.dot_general(left, right, (((1,), (1,)), ((), ())), precision=precisio...  155 us
    another operation x36, other arithmetic, factor(): low = jnp.linalg.cholesky(lead)  154 us
    another operation x21, other arithmetic, factor(): inv = jax.scipy.linalg.solve_triangular(low, eye_sub, lower=True)  127 us
    ppermute x8, waiting for transfers between devices, spread_columns_of(): received = lax.ppermute(pieces[piece], ('row', 'col'), route)  99.9 us
    all_gather x1, waiting for transfers between devices, local_body(): colblk = lax.all_gather(tile, 'row', axis=0, tiled=True)  73.2 us
    ppermute x6, waiting for transfers between devices, bcast_col(): got = lax.ppermute(value, 'col', [(owner, target)])  22.4 us
    ppermute x1, waiting for transfers between devices, local_body(): recv_a = lax.ppermute(send_a, 'col', [(0, 1), (1, 2)])  21.8 us
    ppermute x6, starting transfers between devices, bcast_col(): got = lax.ppermute(value, 'col', [(owner, target)])  17.2 us
  transfers between devices with their start and end apart: 19, of which 8 were waited for; matrix products, arithmetic and copies ran while one was open for 41% of the time, Pallas kernels for 0%

profile of v4, /device:TPU:25, one launch (start us, length us, event | category | flops | bytes accessed | tf_op | source)
XLA Modules:
  0.0 804.0 jit_solution(9736744443764458938)
XLA Ops:
  8.5 73.2 %all-gather.4.cloned.1.call-done = f32[2048,512]{1,0:T(8,128)} async-done(((f32[256,512]{1,0:T(8,128)}), f32[2048,512]{1,0:T(8,128)}) %all-gather.4.cloned.1.call-update) | async-done | bytes 4194320 | tf_op jit(solution)/shard_map/all_gather | solution.py:52
  95.2 21.8 %collective-permute-done.1 = f32[512,512]{0,1:T(8,128)S(1)} collective-permute-done((f32[512,512]{0,1:T(8,128)}, f32[512,512]{0,1:T(8,128)S(1)}, u32[]{:S(2)}, u32[]{:S(2)}) %collective-permute-start.1) | collective-permute-done | bytes 1048608 | tf_op jit(solution)/shard_map/ppermute | solution.py:55
  121.9 11.7 %cholesky.194 = f32[128,128]{1,0:T(8,128)S(1)} custom-call(f32[128,128]{1,0:T(8,128)S(1)} %fusion.151), custom_call_target="Cholesky" | custom-call | tf_op jit(solution)/shard_map/jit(cholesky)/cholesky | solution.py:82
  135.1 9.8 %custom-call.16 = f32[1,128,128]{1,2,0:T(8,128)S(1)} custom-call(f32[1,128,128]{2,1,0:T(8,128)S(1)} %get-tuple-element.311), custom_call_target="InvertDiagBlocksLowerTriangular" | custom-call | tf_op jit(solution)/shard_map/jit(_solve_triangular)/triangular_solve | solution.py:83
  148.6 11.8 %cholesky.205 = f32[128,128]{1,0:T(8,128)S(1)} custom-call(f32[128,128]{1,0:T(8,128)S(1)} %fusion.149), custom_call_target="Cholesky" | custom-call | tf_op jit(solution)/shard_map/jit(cholesky)/cholesky | solution.py:82
  161.7 9.8 %custom-call.17 = f32[1,128,128]{1,2,0:T(8,128)S(1)} custom-call(f32[1,128,128]{2,1,0:T(8,128)S(1)} %get-tuple-element.340), custom_call_target="InvertDiagBlocksLowerTriangular" | custom-call | tf_op jit(solution)/shard_map/jit(_solve_triangular)/triangular_solve | solution.py:83
  172.8 11.7 %cholesky.216 = f32[128,128]{1,0:T(8,128)S(1)} custom-call(f32[128,128]{1,0:T(8,128)S(1)} %fusion.147), custom_call_target="Cholesky" | custom-call | tf_op jit(solution)/shard_map/jit(cholesky)/cholesky | solution.py:82
  185.9 9.8 %custom-call.18 = f32[1,128,128]{1,2,0:T(8,128)S(1)} custom-call(f32[1,128,128]{2,1,0:T(8,128)S(1)} %get-tuple-element.337), custom_call_target="InvertDiagBlocksLowerTriangular" | custom-call | tf_op jit(solution)/shard_map/jit(_solve_triangular)/triangular_solve | solution.py:83
  196.7 11.9 %cholesky.227 = f32[128,128]{1,0:T(8,128)S(1)} custom-call(f32[128,128]{1,0:T(8,128)S(1)} %fusion.145), custom_call_target="Cholesky" | custom-call | tf_op jit(solution)/shard_map/jit(cholesky)/cholesky | solution.py:82
  211.1 9.8 %custom-call.19 = f32[1,128,128]{1,2,0:T(8,128)S(1)} custom-call(f32[1,128,128]{2,1,0:T(8,128)S(1)} %get-tuple-element.335), custom_call_target="InvertDiagBlocksLowerTriangular" | custom-call | tf_op jit(solution)/shard_map/jit(_solve_triangular)/triangular_solve | solution.py:83
  239.3 53.6 %collective-permute-done.8 = f32[512,512]{1,0:T(8,128)} collective-permute-done((f32[512,512]{1,0:T(8,128)}, f32[512,512]{1,0:T(8,128)}, u32[]{:S(2)}, u32[]{:S(2)}) %collective-permute-start.8) | collective-permute-done | bytes 1048608 | tf_op jit(solution)/shard_map/ppermute | solution.py:136
  313.7 11.7 %cholesky.238 = f32[128,128]{1,0:T(8,128)S(1)} custom-call(f32[128,128]{1,0:T(8,128)S(1)} %fusion.143), custom_call_target="Cholesky" | custom-call | tf_op jit(solution)/shard_map/jit(cholesky)/cholesky | solution.py:82
  326.8 10.0 %custom-call.20 = f32[1,128,128]{1,2,0:T(8,128)S(1)} custom-call(f32[1,128,128]{2,1,0:T(8,128)S(1)} %get-tuple-element.309), custom_call_target="InvertDiagBlocksLowerTriangular" | custom-call | tf_op jit(solution)/shard_map/jit(_solve_triangular)/triangular_solve | solution.py:83
  340.5 11.7 %cholesky.249 = f32[128,128]{1,0:T(8,128)S(1)} custom-call(f32[128,128]{1,0:T(8,128)S(1)} %fusion.141), custom_call_target="Cholesky" | custom-call | tf_op jit(solution)/shard_map/jit(cholesky)/cholesky | solution.py:82
  353.5 9.8 %custom-call.21 = f32[1,128,128]{1,2,0:T(8,128)S(1)} custom-call(f32[1,128,128]{2,1,0:T(8,128)S(1)} %get-tuple-element.334), custom_call_target="InvertDiagBlocksLowerTriangular" | custom-call | tf_op jit(solution)/shard_map/jit(_solve_triangular)/triangular_solve | solution.py:83
  365.3 11.9 %cholesky.260 = f32[128,128]{1,0:T(8,128)S(1)} custom-call(f32[128,128]{1,0:T(8,128)S(1)} %fusion.139), custom_call_target="Cholesky" | custom-call | tf_op jit(solution)/shard_map/jit(cholesky)/cholesky | solution.py:82
  378.6 9.8 %custom-call.22 = f32[1,128,128]{1,2,0:T(8,128)S(1)} custom-call(f32[1,128,128]{2,1,0:T(8,128)S(1)} %get-tuple-element.331), custom_call_target="InvertDiagBlocksLowerTriangular" | custom-call | tf_op jit(solution)/shard_map/jit(_solve_triangular)/triangular_solve | solution.py:83
  389.4 11.7 %cholesky.271 = f32[128,128]{1,0:T(8,128)S(1)} custom-call(f32[128,128]{1,0:T(8,128)S(1)} %fusion.137), custom_call_target="Cholesky" | custom-call | tf_op jit(solution)/shard_map/jit(cholesky)/cholesky | solution.py:82
  402.6 9.8 %custom-call.23 = f32[1,128,128]{1,2,0:T(8,128)S(1)} custom-call(f32[1,128,128]{2,1,0:T(8,128)S(1)} %get-tuple-element.329), custom_call_target="InvertDiagBlocksLowerTriangular" | custom-call | tf_op jit(solution)/shard_map/jit(_solve_triangular)/triangular_solve | solution.py:83
  451.2 11.2 %collective-permute-done.14 = f32[512,512]{1,0:T(8,128)S(1)} collective-permute-done((f32[512,512]{1,0:T(8,128)S(1)}, f32[512,512]{1,0:T(8,128)S(1)}, u32[]{:S(2)}, u32[]{:S(2)}) %collective-permute-start.14) | collective-permute-done | bytes 1048608 | tf_op jit(solution)/shard_map/ppermute | solution.py:136
  462.4 11.2 %collective-permute-done.13 = f32[512,512]{1,0:T(8,128)S(1)} collective-permute-done((f32[512,512]{1,0:T(8,128)S(1)}, f32[512,512]{1,0:T(8,128)S(1)}, u32[]{:S(2)}, u32[]{:S(2)}) %collective-permute-start.13) | collective-permute-done | bytes 1048608 | tf_op jit(solution)/shard_map/ppermute | solution.py:136
  473.7 16.8 %collective-permute-done.12 = f32[512,512]{1,0:T(8,128)S(1)} collective-permute-done((f32[512,512]{1,0:T(8,128)S(1)}, f32[512,512]{1,0:T(8,128)S(1)}, u32[]{:S(2)}, u32[]{:S(2)}) %collective-permute-start.12) | collective-permute-done | bytes 1048608 | tf_op jit(solution)/shard_map/ppermute | solution.py:136
  516.2 11.7 %cholesky.282 = f32[128,128]{1,0:T(8,128)S(1)} custom-call(f32[128,128]{1,0:T(8,128)S(1)} %fusion.135), custom_call_target="Cholesky" | custom-call | tf_op jit(solution)/shard_map/jit(cholesky)/cholesky | solution.py:82
  529.3 9.8 %custom-call.24 = f32[1,128,128]{1,2,0:T(8,128)S(1)} custom-call(f32[1,128,128]{2,1,0:T(8,128)S(1)} %get-tuple-element.307), custom_call_target="InvertDiagBlocksLowerTriangular" | custom-call | tf_op jit(solution)/shard_map/jit(_solve_triangular)/triangular_solve | solution.py:83
  544.4 11.9 %cholesky.293 = f32[128,128]{1,0:T(8,128)S(1)} custom-call(f32[128,128]{1,0:T(8,128)S(1)} %fusion.133), custom_call_target="Cholesky" | custom-call | tf_op jit(solution)/shard_map/jit(cholesky)/cholesky | solution.py:82
  574.1 13.2 %cholesky.304 = f32[128,128]{1,0:T(8,128)} custom-call(f32[128,128]{1,0:T(8,128)} %fusion.131), custom_call_target="Cholesky" | custom-call | tf_op jit(solution)/shard_map/jit(cholesky)/cholesky | solution.py:82
  602.8 11.3 %custom-call.26 = f32[1,128,128]{1,2,0:T(8,128)} custom-call(f32[1,128,128]{2,1,0:T(8,128)} %get-tuple-element.325), custom_call_target="InvertDiagBlocksLowerTriangular" | custom-call | tf_op jit(solution)/shard_map/jit(_solve_triangular)/triangular_solve | solution.py:83
  618.2 12.5 %cholesky.315 = f32[128,128]{1,0:T(8,128)S(1)} custom-call(f32[128,128]{1,0:T(8,128)} %fusion.129), custom_call_target="Cholesky" | custom-call | tf_op jit(solution)/shard_map/jit(cholesky)/cholesky | solution.py:82
  632.1 10.4 %custom-call.27 = f32[1,128,128]{1,2,0:T(8,128)} custom-call(f32[1,128,128]{2,1,0:T(8,128)S(1)} %get-tuple-element.323), custom_call_target="InvertDiagBlocksLowerTriangular" | custom-call | tf_op jit(solution)/shard_map/jit(_solve_triangular)/triangular_solve | solution.py:83
  660.1 22.4 %collective-permute-done.5 = f32[2048,512]{1,0:T(8,128)} collective-permute-done((f32[2048,512]{1,0:T(8,128)}, f32[2048,512]{1,0:T(8,128)}, u32[]{:S(2)}, u32[]{:S(2)}) %collective-permute-start.5) | collective-permute-done | bytes 4194336 | tf_op jit(solution)/shard_map/ppermute | solution.py:30
  693.7 10.2 %fusion.20 = f32[2048,512]{1,0:T(8,128)} fusion(f32[2048,512]{1,0:T(8,128)S(1)} %fusion.212, f32[2048,512]{1,0:T(8,128)S(1)} %fusion.211, f32[2048,4096]{1,0:T(8,128)} %param.54, pred[2048]{0:T(1024)(128)(4,1)S(1)} %copy-done.36, f32[256,256]{1,0:T(8,128)S(1)} %copy-done.24, f32[128,128]{1,0:T(8,128)S(1)} %copy.108, ...), kind=kOutput, calls=%fused_computation.21 | convolution fusion | flops 6447169536 | bytes 17565696 | tf_op jit(solution)/shard_map/dot_general | solution.py:17
  721.7 67.3 %subtract_select_fusion = f32[2048,4096]{1,0:T(8,128)} fusion(f32[2048,4096]{1,0:T(8,128)} %param.54, f32[4096,512]{1,0:T(8,128)} %bitcast.212, f32[4096,512]{1,0:T(8,128)} %bitcast.211, s32[4096]{0:T(1024)S(1)} %fusion.171, s32[2048]{0:T(1024)S(1)} %copy-done.37, pred[2048]{0:T(1024)(128)(4,1)S(1)} %copy-done.38, f32[2048,512]{1,0:T(8,128)} %copy-done.6, ...), kind=kOutput, calls=%fused_computation | convolution fusion | flops 51579453440 | bytes 92301312 | tf_op jit(solution)/shard_map/dot_general | solution.py:17
  (297 shorter events, 247.6 us)
Async XLA Ops:
  6.5 75.2 %all-gather.4.cloned.1.call-start = ((), (), s32[]{:S(2)}) async-start(), calls=%async_computation | async-start | bytes 4718592 | tf_op jit(solution)/shard_map/all_gather | solution.py:52
  8.4 697.4 %all-gather.6.cloned.1.call-start = ((), (), s32[]{:S(2)}) async-start(), calls=%async_computation.1 | async-start | bytes 9437184 | tf_op jit(solution)/shard_map/all_gather | solution.py:138
  85.1 31.9 %collective-permute-start = (f32[2,512,512]{1,2,0:T(8,128)}, f32[2,512,512]{1,2,0:T(8,128)}, u32[]{:S(2)}, u32[]{:S(2)}) collective-permute-start(f32[2,512,512]{1,2,0:T(8,128)} %copy.54), channel_id=1, source_target_pairs={{0,2},{4,6},{8,10},{12,14},{16,18},{20,22},{24,26},{28,30}} | collective-permute-start | bytes 6291464 | tf_op jit(solution)/shard_map/ppermute | solution.py:56
  90.7 26.3 %collective-permute-start.1 = (f32[512,512]{0,1:T(8,128)}, f32[512,512]{0,1:T(8,128)S(1)}, u32[]{:S(2)}, u32[]{:S(2)}) collective-permute-start(f32[512,512]{0,1:T(8,128)} %broadcast_select_fusion), channel_id=1, source_target_pairs={{0,1},{1,2},{4,5},{5,6},{8,9},{9,10},{12,13},{13,14},{16,17},{17,1... | collective-permute-start | bytes 3145736 | tf_op jit(solution)/shard_map/ppermute | solution.py:55
  210.0 20.7 %copy-start.17 = (f32[512,512]{1,0:T(8,128)}, f32[512,512]{1,0:T(8,128)S(1)}, u32[]{:S(2)}) copy-start(f32[512,512]{1,0:T(8,128)S(1)} %get-tuple-element.336) | copy-start | bytes 3145732
  210.7 93.0 %copy-start.27 = (f32[256,256]{1,0:T(8,128)}, f32[256,256]{1,0:T(8,128)S(1)}, u32[]{:S(2)}) copy-start(f32[256,256]{1,0:T(8,128)S(1)} %select_maximum_fusion.8) | copy-start | bytes 786436
  221.3 82.5 %copy-start.31 = (f32[128,128]{1,0:T(8,128)}, f32[128,128]{1,0:T(8,128)S(1)}, u32[]{:S(2)}) copy-start(f32[128,128]{1,0:T(8,128)S(1)} %copy.70) | copy-start | bytes 196612
  222.0 81.8 %copy-start.25 = (f32[256,256]{1,0:T(8,128)}, f32[256,256]{1,0:T(8,128)S(1)}, u32[]{:S(2)}) copy-start(f32[256,256]{1,0:T(8,128)S(1)} %convolution_negate_fusion.2) | copy-start | bytes 786436
  233.0 63.2 %copy-start.10 = (f32[512,512]{0,1:T(8,128)S(1)}, f32[512,512]{0,1:T(8,128)}, u32[]{:S(2)}) copy-start(f32[512,512]{0,1:T(8,128)} %copy-done.9) | copy-start | bytes 3145732
  233.9 5.4 collective-permute-start.11
  234.6 4.7 collective-permute-start.10
  236.3 3.0 collective-permute-start.9
  238.0 54.9 %collective-permute-start.8 = (f32[512,512]{1,0:T(8,128)}, f32[512,512]{1,0:T(8,128)}, u32[]{:S(2)}, u32[]{:S(2)}) collective-permute-start(f32[512,512]{1,0:T(8,128)} %get-tuple-element.316), channel_id=1, source_target_pairs={{0,24},{4,28},{8,25},{12,29},{16,26},{20,30},{24,27},{28,31}} | collective-permute-start | bytes 3145736 | tf_op jit(solution)/shard_map/ppermute | solution.py:136
  296.1 417.7 %all-gather.8.cloned.1.call-start = ((), (), s32[]{:S(2)}) async-start(), calls=%async_computation.2 | async-start | bytes 9437184 | tf_op jit(solution)/shard_map/all_gather | solution.py:138
  296.5 119.8 %collective-permute-start.4 = (f32[2048,512]{1,0:T(8,128)}, f32[2048,512]{1,0:T(8,128)}, u32[]{:S(2)}, u32[]{:S(2)}) collective-permute-start(f32[2048,512]{1,0:T(8,128)} %copy-done.5), channel_id=1, source_target_pairs={{0,1},{4,5},{8,9},{12,13},{16,17},{20,21},{24,25},{28,29}} | collective-permute-start | bytes 12582920 | tf_op jit(solution)/shard_map/ppermute | solution.py:30
  298.1 118.2 %collective-permute-start.3 = (f32[2048,512]{1,0:T(8,128)}, f32[2048,512]{1,0:T(8,128)}, u32[]{:S(2)}, u32[]{:S(2)}) collective-permute-start(f32[2048,512]{1,0:T(8,128)} %copy-done.5), channel_id=1, source_target_pairs={{0,2},{4,6},{8,10},{12,14},{16,18},{20,22},{24,26},{28,30}} | collective-permute-start | bytes 12582920 | tf_op jit(solution)/shard_map/ppermute | solution.py:30
  300.7 115.6 %collective-permute-start.2 = (f32[2048,512]{1,0:T(8,128)}, f32[2048,512]{1,0:T(8,128)}, u32[]{:S(2)}, u32[]{:S(2)}) collective-permute-start(f32[2048,512]{1,0:T(8,128)} %copy-done.5), channel_id=1, source_target_pairs={{0,3},{4,7},{8,11},{12,15},{16,19},{20,23},{24,27},{28,31}} | collective-permute-start | bytes 12582920 | tf_op jit(solution)/shard_map/ppermute | solution.py:30
  402.6 18.6 %copy-start.14 = (f32[512,512]{1,0:T(8,128)}, f32[512,512]{1,0:T(8,128)S(1)}, u32[]{:S(2)}) copy-start(f32[512,512]{1,0:T(8,128)S(1)} %get-tuple-element.330) | copy-start | bytes 3145732
  437.4 53.1 %copy-start = (f32[2048,512]{1,0:T(8,128)}, f32[2048,512]{1,0:T(8,128)S(1)}, u32[]{:S(2)}) copy-start(f32[2048,512]{1,0:T(8,128)S(1)} %fusion.17) | copy-start | bytes 12582916
  438.0 56.7 %copy-start.26 = (f32[256,256]{1,0:T(8,128)S(1)}, f32[256,256]{1,0:T(8,128)}, u32[]{:S(2)}) copy-start(f32[256,256]{1,0:T(8,128)} %copy-done.25) | copy-start | bytes 786436
  438.0 56.7 %copy-start.28 = (f32[256,256]{1,0:T(8,128)S(1)}, f32[256,256]{1,0:T(8,128)}, u32[]{:S(2)}) copy-start(f32[256,256]{1,0:T(8,128)} %copy-done.27) | copy-start | bytes 786436
  438.0 56.7 %copy-start.32 = (f32[128,128]{1,0:T(8,128)S(1)}, f32[128,128]{1,0:T(8,128)}, u32[]{:S(2)}) copy-start(f32[128,128]{1,0:T(8,128)} %copy-done.31) | copy-start | bytes 196612
  438.0 13.2 %collective-permute-start.15 = (f32[512,512]{1,0:T(8,128)S(1)}, f32[512,512]{1,0:T(8,128)S(1)}, u32[]{:S(2)}, u32[]{:S(2)}) collective-permute-start(f32[512,512]{1,0:T(8,128)S(1)} %get-tuple-element.317), channel_id=1, source_target_pairs={{1,0},{5,4},{9,1},{13,5},{17,2},{21,6},{25,3},{29,7}} | collective-permute-start | bytes 3145736 | tf_op jit(solution)/shard_map/ppermute | solution.py:136
  439.5 22.9 %collective-permute-start.14 = (f32[512,512]{1,0:T(8,128)S(1)}, f32[512,512]{1,0:T(8,128)S(1)}, u32[]{:S(2)}, u32[]{:S(2)}) collective-permute-start(f32[512,512]{1,0:T(8,128)S(1)} %get-tuple-element.318), channel_id=1, source_target_pairs={{1,8},{5,12},{9,9},{13,13},{17,10},{21,14},{25,11},{29,15}} | collective-permute-start | bytes 3145736 | tf_op jit(solution)/shard_map/ppermute | solution.py:136
  440.9 32.8 %collective-permute-start.13 = (f32[512,512]{1,0:T(8,128)S(1)}, f32[512,512]{1,0:T(8,128)S(1)}, u32[]{:S(2)}, u32[]{:S(2)}) collective-permute-start(f32[512,512]{1,0:T(8,128)S(1)} %get-tuple-element.319), channel_id=1, source_target_pairs={{1,16},{5,20},{9,17},{13,21},{17,18},{21,22},{25,19},{29,23}} | collective-permute-start | bytes 3145736 | tf_op jit(solution)/shard_map/ppermute | solution.py:136
  442.2 48.2 %collective-permute-start.12 = (f32[512,512]{1,0:T(8,128)S(1)}, f32[512,512]{1,0:T(8,128)S(1)}, u32[]{:S(2)}, u32[]{:S(2)}) collective-permute-start(f32[512,512]{1,0:T(8,128)S(1)} %get-tuple-element.320), channel_id=1, source_target_pairs={{1,24},{5,28},{9,25},{13,29},{17,26},{21,30},{25,27},{29,31}} | collective-permute-start | bytes 3145736 | tf_op jit(solution)/shard_map/ppermute | solution.py:136
  570.3 43.7 %copy-start.29 = (f32[256,256]{0,1:T(8,128)}, f32[256,256]{0,1:T(8,128)S(1)}, u32[]{:S(2)}) copy-start(f32[256,256]{0,1:T(8,128)S(1)} %convolution_subtract_fusion.5) | copy-start | bytes 786436
  587.2 72.9 %collective-permute-start.7 = (f32[2048,512]{1,0:T(8,128)}, f32[2048,512]{1,0:T(8,128)}, u32[]{:S(2)}, u32[]{:S(2)}) collective-permute-start(f32[2048,512]{1,0:T(8,128)} %copy-done), channel_id=1, source_target_pairs={{1,0},{5,4},{9,8},{13,12},{17,16},{21,20},{25,24},{29,28}} | collective-permute-start | bytes 12582920 | tf_op jit(solution)/shard_map/ppermute | solution.py:30
  590.6 69.6 %collective-permute-start.6 = (f32[2048,512]{1,0:T(8,128)}, f32[2048,512]{1,0:T(8,128)}, u32[]{:S(2)}, u32[]{:S(2)}) collective-permute-start(f32[2048,512]{1,0:T(8,128)} %copy-done), channel_id=1, source_target_pairs={{1,2},{5,6},{9,10},{13,14},{17,18},{21,22},{25,26},{29,30}} | collective-permute-start | bytes 12582920 | tf_op jit(solution)/shard_map/ppermute | solution.py:30
  593.8 88.7 %collective-permute-start.5 = (f32[2048,512]{1,0:T(8,128)}, f32[2048,512]{1,0:T(8,128)}, u32[]{:S(2)}, u32[]{:S(2)}) collective-permute-start(f32[2048,512]{1,0:T(8,128)} %copy-done), channel_id=1, source_target_pairs={{1,3},{5,7},{9,11},{13,15},{17,19},{21,23},{25,27},{29,31}} | collective-permute-start | bytes 12582920 | tf_op jit(solution)/shard_map/ppermute | solution.py:30
  632.1 28.0 %copy-start.15 = (f32[512,512]{1,0:T(8,128)}, f32[512,512]{1,0:T(8,128)S(1)}, u32[]{:S(2)}) copy-start(f32[512,512]{1,0:T(8,128)S(1)} %get-tuple-element.324) | copy-start | bytes 3145732
  652.7 29.8 %copy-start.1 = (f32[2048,512]{1,0:T(8,128)S(1)}, f32[2048,512]{1,0:T(8,128)}, u32[]{:S(2)}) copy-start(f32[2048,512]{1,0:T(8,128)} %copy-done) | copy-start | bytes 12582916
  (27 other events, 178.3 us)
Sparse Core Ops, SparseCore 0:
  9.5 72.1 all-gather.3
  296.2 121.2 all-gather.5
  492.3 122.1 all-gather.7

commit v5 on v4

--- a/solution.py
+++ b/solution.py
@@ -158,9 +158,8 @@
     upd2 = panel_in - times_transposed(rows0, l0_b2) - times_transposed(rows1, l1_b2)
     _, column2 = panel_rows(upd2, l2, i2, 2)
 
-    left = jnp.concatenate([rows0, rows1], axis=1)
-    right = jnp.concatenate([cols0, cols1], axis=1)
-    updated = gram - times_transposed(left, right, lax.Precision.HIGH)
+    updated = gram - times_transposed(rows0, cols0, lax.Precision.HIGH)
+    updated = updated - times_transposed(rows1, cols1, lax.Precision.HIGH)
     in_steps = grows < STEPS * NB
     panel_end = (grows // NB + 1) * NB
     zero = in_steps[:, None] & (gcols[None, :] >= panel_end[:, None])

time: 818 us -> 818 us (level)
  waiting for transfers between devices: 217 us -> 232 us
  other arithmetic: 327 us -> 316 us
    ppermute x6, waiting for transfers between devices: 22.4 us -> 38.6 us  [bcast_col(): got = lax.ppermute(value, 'col', [(owner, target)])]
    dot_general x32 -> x33, matrix products: 155 us -> 160 us  [times_transposed(): lax.dot_general(left, right, (((1,), (1,)), ((), ())), precision=precisio...]
where the time goes in v5:
time: 818 us; the launch traced here: 805 us
  other arithmetic  316 us (39%)
  waiting for transfers between devices  232 us (28%)
  matrix products  169 us (21%)
  local copies, waits for them, and re-layouts  37.5 us (5%)
  starting transfers between devices  35.3 us (4%)
  between operations  15.2 us (2%)
    dot_general x33, matrix products, times_transposed(): lax.dot_general(left, right, (((1,), (1,)), ((), ())), precision=precisio...  160 us
    another operation x36, other arithmetic, factor(): low = jnp.linalg.cholesky(lead)  150 us
    another operation x21, other arithmetic, factor(): inv = jax.scipy.linalg.solve_triangular(low, eye_sub, lower=True)  124 us
    ppermute x8, waiting for transfers between devices, spread_columns_of(): received = lax.ppermute(pieces[piece], ('row', 'col'), route)  98.5 us
    all_gather x1, waiting for transfers between devices, local_body(): colblk = lax.all_gather(tile, 'row', axis=0, tiled=True)  73.2 us
    ppermute x6, waiting for transfers between devices, bcast_col(): got = lax.ppermute(value, 'col', [(owner, target)])  38.6 us
    ppermute x1, waiting for transfers between devices, local_body(): recv_a = lax.ppermute(send_a, 'col', [(0, 1), (1, 2)])  21.8 us
    ppermute x6, starting transfers between devices, bcast_col(): got = lax.ppermute(value, 'col', [(owner, target)])  17 us
  transfers between devices with their start and end apart: 19, of which 8 were waited for; matrix products, arithmetic and copies ran while one was open for 41% of the time, Pallas kernels for 0%

profile of v5, /device:TPU:25, one launch (start us, length us, event | category | flops | bytes accessed | tf_op | source)
XLA Modules:
  0.0 805.3 jit_solution(16208996995633889910)
XLA Ops:
  8.5 73.2 %all-gather.4.cloned.1.call-done = f32[2048,512]{1,0:T(8,128)} async-done(((f32[256,512]{1,0:T(8,128)}), f32[2048,512]{1,0:T(8,128)}) %all-gather.4.cloned.1.call-update) | async-done | bytes 4194320 | tf_op jit(solution)/shard_map/all_gather | solution.py:52
  95.2 21.8 %collective-permute-done.1 = f32[512,512]{0,1:T(8,128)S(1)} collective-permute-done((f32[512,512]{0,1:T(8,128)}, f32[512,512]{0,1:T(8,128)S(1)}, u32[]{:S(2)}, u32[]{:S(2)}) %collective-permute-start.1) | collective-permute-done | bytes 1048608 | tf_op jit(solution)/shard_map/ppermute | solution.py:55
  122.0 11.7 %cholesky.194 = f32[128,128]{1,0:T(8,128)S(1)} custom-call(f32[128,128]{1,0:T(8,128)S(1)} %fusion.145), custom_call_target="Cholesky" | custom-call | tf_op jit(solution)/shard_map/jit(cholesky)/cholesky | solution.py:82
  135.0 9.8 %custom-call.16 = f32[1,128,128]{1,2,0:T(8,128)S(1)} custom-call(f32[1,128,128]{2,1,0:T(8,128)S(1)} %get-tuple-element.311), custom_call_target="InvertDiagBlocksLowerTriangular" | custom-call | tf_op jit(solution)/shard_map/jit(_solve_triangular)/triangular_solve | solution.py:83
  148.5 12.0 %cholesky.205 = f32[128,128]{1,0:T(8,128)S(1)} custom-call(f32[128,128]{1,0:T(8,128)S(1)} %fusion.143), custom_call_target="Cholesky" | custom-call | tf_op jit(solution)/shard_map/jit(cholesky)/cholesky | solution.py:82
  161.8 9.8 %custom-call.17 = f32[1,128,128]{1,2,0:T(8,128)S(1)} custom-call(f32[1,128,128]{2,1,0:T(8,128)S(1)} %get-tuple-element.340), custom_call_target="InvertDiagBlocksLowerTriangular" | custom-call | tf_op jit(solution)/shard_map/jit(_solve_triangular)/triangular_solve | solution.py:83
  172.9 11.7 %cholesky.216 = f32[128,128]{1,0:T(8,128)S(1)} custom-call(f32[128,128]{1,0:T(8,128)S(1)} %fusion.141), custom_call_target="Cholesky" | custom-call | tf_op jit(solution)/shard_map/jit(cholesky)/cholesky | solution.py:82
  186.0 9.8 %custom-call.18 = f32[1,128,128]{1,2,0:T(8,128)S(1)} custom-call(f32[1,128,128]{2,1,0:T(8,128)S(1)} %get-tuple-element.337), custom_call_target="InvertDiagBlocksLowerTriangular" | custom-call | tf_op jit(solution)/shard_map/jit(_solve_triangular)/triangular_solve | solution.py:83
  196.8 11.9 %cholesky.227 = f32[128,128]{1,0:T(8,128)S(1)} custom-call(f32[128,128]{1,0:T(8,128)S(1)} %fusion.139), custom_call_target="Cholesky" | custom-call | tf_op jit(solution)/shard_map/jit(cholesky)/cholesky | solution.py:82
  211.1 9.8 %custom-call.19 = f32[1,128,128]{1,2,0:T(8,128)S(1)} custom-call(f32[1,128,128]{2,1,0:T(8,128)S(1)} %get-tuple-element.335), custom_call_target="InvertDiagBlocksLowerTriangular" | custom-call | tf_op jit(solution)/shard_map/jit(_solve_triangular)/triangular_solve | solution.py:83
  239.3 53.5 %collective-permute-done.5 = f32[512,512]{1,0:T(8,128)} collective-permute-done((f32[512,512]{1,0:T(8,128)}, f32[512,512]{1,0:T(8,128)}, u32[]{:S(2)}, u32[]{:S(2)}) %collective-permute-start.5) | collective-permute-done | bytes 1048608 | tf_op jit(solution)/shard_map/ppermute | solution.py:136
  313.5 11.7 %cholesky.238 = f32[128,128]{1,0:T(8,128)S(1)} custom-call(f32[128,128]{1,0:T(8,128)S(1)} %fusion.137), custom_call_target="Cholesky" | custom-call | tf_op jit(solution)/shard_map/jit(cholesky)/cholesky | solution.py:82
  326.6 10.2 %custom-call.20 = f32[1,128,128]{1,2,0:T(8,128)S(1)} custom-call(f32[1,128,128]{2,1,0:T(8,128)S(1)} %get-tuple-element.309), custom_call_target="InvertDiagBlocksLowerTriangular" | custom-call | tf_op jit(solution)/shard_map/jit(_solve_triangular)/triangular_solve | solution.py:83
  340.4 11.7 %cholesky.249 = f32[128,128]{1,0:T(8,128)S(1)} custom-call(f32[128,128]{1,0:T(8,128)S(1)} %fusion.135), custom_call_target="Cholesky" | custom-call | tf_op jit(solution)/shard_map/jit(cholesky)/cholesky | solution.py:82
  353.5 9.8 %custom-call.21 = f32[1,128,128]{1,2,0:T(8,128)S(1)} custom-call(f32[1,128,128]{2,1,0:T(8,128)S(1)} %get-tuple-element.334), custom_call_target="InvertDiagBlocksLowerTriangular" | custom-call | tf_op jit(solution)/shard_map/jit(_solve_triangular)/triangular_solve | solution.py:83
  365.2 11.9 %cholesky.260 = f32[128,128]{1,0:T(8,128)S(1)} custom-call(f32[128,128]{1,0:T(8,128)S(1)} %fusion.133), custom_call_target="Cholesky" | custom-call | tf_op jit(solution)/shard_map/jit(cholesky)/cholesky | solution.py:82
  378.5 9.8 %custom-call.22 = f32[1,128,128]{1,2,0:T(8,128)S(1)} custom-call(f32[1,128,128]{2,1,0:T(8,128)S(1)} %get-tuple-element.331), custom_call_target="InvertDiagBlocksLowerTriangular" | custom-call | tf_op jit(solution)/shard_map/jit(_solve_triangular)/triangular_solve | solution.py:83
  389.3 11.7 %cholesky.271 = f32[128,128]{1,0:T(8,128)S(1)} custom-call(f32[128,128]{1,0:T(8,128)S(1)} %fusion.131), custom_call_target="Cholesky" | custom-call | tf_op jit(solution)/shard_map/jit(cholesky)/cholesky | solution.py:82
  402.4 9.8 %custom-call.23 = f32[1,128,128]{1,2,0:T(8,128)S(1)} custom-call(f32[1,128,128]{2,1,0:T(8,128)S(1)} %get-tuple-element.329), custom_call_target="InvertDiagBlocksLowerTriangular" | custom-call | tf_op jit(solution)/shard_map/jit(_solve_triangular)/triangular_solve | solution.py:83
  453.8 11.2 %collective-permute-done.14 = f32[512,512]{1,0:T(8,128)} collective-permute-done((f32[512,512]{1,0:T(8,128)}, f32[512,512]{1,0:T(8,128)}, u32[]{:S(2)}, u32[]{:S(2)}) %collective-permute-start.14) | collective-permute-done | bytes 1048608 | tf_op jit(solution)/shard_map/ppermute | solution.py:136
  465.0 11.2 %collective-permute-done.13 = f32[512,512]{1,0:T(8,128)} collective-permute-done((f32[512,512]{1,0:T(8,128)}, f32[512,512]{1,0:T(8,128)}, u32[]{:S(2)}, u32[]{:S(2)}) %collective-permute-start.13) | collective-permute-done | bytes 1048608 | tf_op jit(solution)/shard_map/ppermute | solution.py:136
  476.2 17.7 %collective-permute-done.12 = f32[512,512]{1,0:T(8,128)} collective-permute-done((f32[512,512]{1,0:T(8,128)}, f32[512,512]{1,0:T(8,128)}, u32[]{:S(2)}, u32[]{:S(2)}) %collective-permute-start.12) | collective-permute-done | bytes 1048608 | tf_op jit(solution)/shard_map/ppermute | solution.py:136
  520.4 11.7 %cholesky.282 = f32[128,128]{1,0:T(8,128)S(1)} custom-call(f32[128,128]{1,0:T(8,128)S(1)} %fusion.129), custom_call_target="Cholesky" | custom-call | tf_op jit(solution)/shard_map/jit(cholesky)/cholesky | solution.py:82
  533.5 9.8 %custom-call.24 = f32[1,128,128]{1,2,0:T(8,128)S(1)} custom-call(f32[1,128,128]{2,1,0:T(8,128)S(1)} %get-tuple-element.307), custom_call_target="InvertDiagBlocksLowerTriangular" | custom-call | tf_op jit(solution)/shard_map/jit(_solve_triangular)/triangular_solve | solution.py:83
  546.9 12.1 %cholesky.293 = f32[128,128]{1,0:T(8,128)S(1)} custom-call(f32[128,128]{1,0:T(8,128)S(1)} %fusion.127), custom_call_target="Cholesky" | custom-call | tf_op jit(solution)/shard_map/jit(cholesky)/cholesky | solution.py:82
  560.4 9.8 %custom-call.25 = f32[1,128,128]{1,2,0:T(8,128)S(1)} custom-call(f32[1,128,128]{2,1,0:T(8,128)S(1)} %get-tuple-element.328), custom_call_target="InvertDiagBlocksLowerTriangular" | custom-call | tf_op jit(solution)/shard_map/jit(_solve_triangular)/triangular_solve | solution.py:83
  571.4 11.7 %cholesky.304 = f32[128,128]{1,0:T(8,128)S(1)} custom-call(f32[128,128]{1,0:T(8,128)S(1)} %fusion.125), custom_call_target="Cholesky" | custom-call | tf_op jit(solution)/shard_map/jit(cholesky)/cholesky | solution.py:82
  605.3 11.7 %cholesky.315 = f32[128,128]{1,0:T(8,128)S(1)} custom-call(f32[128,128]{1,0:T(8,128)S(1)} %fusion.123), custom_call_target="Cholesky" | custom-call | tf_op jit(solution)/shard_map/jit(cholesky)/cholesky | solution.py:82
  639.8 38.6 %collective-permute-done.9 = f32[2048,512]{1,0:T(8,128)} collective-permute-done((f32[2048,512]{1,0:T(8,128)}, f32[2048,512]{1,0:T(8,128)}, u32[]{:S(2)}, u32[]{:S(2)}) %collective-permute-start.9) | collective-permute-done | bytes 4194336 | tf_op jit(solution)/shard_map/ppermute | solution.py:30
  689.7 10.0 %fusion.14 = f32[2048,512]{1,0:T(8,128)} fusion(f32[2048,512]{1,0:T(8,128)S(1)} %fusion.206, f32[2048,512]{1,0:T(8,128)S(1)} %fusion.205, f32[2048,4096]{1,0:T(8,128)} %param.54, pred[2048]{0:T(1024)(128)(4,1)S(1)} %copy-done.32, f32[256,256]{1,0:T(8,128)S(1)} %select_maximum_fusion.6, f32[128,128]{1,0:T(8,128)S(1)} %copy.106, ...), kind=kOutput, calls=%fused_computation.15 | convolution fusion | flops 6447169536 | bytes 17565696 | tf_op jit(solution)/shard_map/dot_general | solution.py:17
  706.3 31.2 %fusion.202 = f32[2048,4096]{1,0:T(8,128)} fusion(f32[2048,512]{1,0:T(8,128)S(1)} %copy-done.5, f32[4096,512]{1,0:T(8,128)S(1)} %bitcast.216), kind=kOutput, calls=%fused_computation.331 | convolution fusion | flops 25769803776 | bytes 46137344 | tf_op jit(solution)/shard_map/dot_general | solution.py:17
  745.5 44.6 %subtract_select_fusion = f32[2048,4096]{1,0:T(8,128)} fusion(f32[2048,4096]{1,0:T(8,128)} %param.54, f32[2048,4096]{1,0:T(8,128)} %fusion.202, s32[4096]{0:T(1024)S(1)} %fusion.165, s32[2048]{0:T(1024)S(1)} %copy-done.30, pred[2048]{0:T(1024)(128)(4,1)S(1)} %copy-done.31, f32[2048,512]{1,0:T(8,128)} %copy-done.7, f32[4096,512]{1,0:T(8,128)} %bitcast.212), kind=kOutput, calls=%fused_computation | convolution fusion | flops 25811746816 | bytes 113272832 | tf_op jit(solution)/shard_map/dot_general | solution.py:17
  (286 shorter events, 237.0 us)
Async XLA Ops:
  6.5 75.2 %all-gather.4.cloned.1.call-start = ((), (), s32[]{:S(2)}) async-start(), calls=%async_computation | async-start | bytes 4718592 | tf_op jit(solution)/shard_map/all_gather | solution.py:52
  8.4 693.2 %all-gather.6.cloned.1.call-start = ((), (), s32[]{:S(2)}) async-start(), calls=%async_computation.1 | async-start | bytes 9437184 | tf_op jit(solution)/shard_map/all_gather | solution.py:138
  85.1 32.0 %collective-permute-start = (f32[2,512,512]{1,2,0:T(8,128)}, f32[2,512,512]{1,2,0:T(8,128)}, u32[]{:S(2)}, u32[]{:S(2)}) collective-permute-start(f32[2,512,512]{1,2,0:T(8,128)} %copy.53), channel_id=1, source_target_pairs={{0,2},{4,6},{8,10},{12,14},{16,18},{20,22},{24,26},{28,30}} | collective-permute-start | bytes 6291464 | tf_op jit(solution)/shard_map/ppermute | solution.py:56
  90.7 26.3 %collective-permute-start.1 = (f32[512,512]{0,1:T(8,128)}, f32[512,512]{0,1:T(8,128)S(1)}, u32[]{:S(2)}, u32[]{:S(2)}) collective-permute-start(f32[512,512]{0,1:T(8,128)} %broadcast_select_fusion), channel_id=1, source_target_pairs={{0,1},{1,2},{4,5},{5,6},{8,9},{9,10},{12,13},{13,14},{16,17},{17,1... | collective-permute-start | bytes 3145736 | tf_op jit(solution)/shard_map/ppermute | solution.py:55
  210.0 20.7 %copy-start.20 = (f32[512,512]{1,0:T(8,128)}, f32[512,512]{1,0:T(8,128)S(1)}, u32[]{:S(2)}) copy-start(f32[512,512]{1,0:T(8,128)S(1)} %get-tuple-element.336) | copy-start | bytes 3145732
  210.7 92.7 %copy-start.23 = (f32[256,256]{1,0:T(8,128)}, f32[256,256]{1,0:T(8,128)S(1)}, u32[]{:S(2)}) copy-start(f32[256,256]{1,0:T(8,128)S(1)} %select_maximum_fusion.8) | copy-start | bytes 786436
  221.3 82.2 %copy-start.26 = (f32[128,128]{1,0:T(8,128)}, f32[128,128]{1,0:T(8,128)S(1)}, u32[]{:S(2)}) copy-start(f32[128,128]{1,0:T(8,128)S(1)} %copy.69) | copy-start | bytes 196612
  221.6 81.9 %copy-start.24 = (f32[128,128]{1,0:T(8,128)}, f32[128,128]{1,0:T(8,128)S(1)}, u32[]{:S(2)}) copy-start(f32[128,128]{1,0:T(8,128)S(1)} %convolution_negate_fusion.7) | copy-start | bytes 196612
  222.0 81.5 %copy-start.21 = (f32[256,256]{1,0:T(8,128)}, f32[256,256]{1,0:T(8,128)S(1)}, u32[]{:S(2)}) copy-start(f32[256,256]{1,0:T(8,128)S(1)} %convolution_negate_fusion.2) | copy-start | bytes 786436
  233.0 63.1 %copy-start.13 = (f32[512,512]{0,1:T(8,128)S(1)}, f32[512,512]{0,1:T(8,128)}, u32[]{:S(2)}) copy-start(f32[512,512]{0,1:T(8,128)} %copy-done.12) | copy-start | bytes 3145732
  234.0 5.3 collective-permute-start.8
  234.7 4.6 collective-permute-start.7
  236.4 3.0 collective-permute-start.6
  238.0 54.9 %collective-permute-start.5 = (f32[512,512]{1,0:T(8,128)}, f32[512,512]{1,0:T(8,128)}, u32[]{:S(2)}, u32[]{:S(2)}) collective-permute-start(f32[512,512]{1,0:T(8,128)} %get-tuple-element.316), channel_id=1, source_target_pairs={{0,24},{4,28},{8,25},{12,29},{16,26},{20,30},{24,27},{28,31}} | collective-permute-start | bytes 3145736 | tf_op jit(solution)/shard_map/ppermute | solution.py:136
  296.0 441.5 %all-gather.8.cloned.1.call-start = ((), (), s32[]{:S(2)}) async-start(), calls=%async_computation.2 | async-start | bytes 9437184 | tf_op jit(solution)/shard_map/all_gather | solution.py:138
  296.5 119.6 %collective-permute-start.4 = (f32[2048,512]{1,0:T(8,128)}, f32[2048,512]{1,0:T(8,128)}, u32[]{:S(2)}, u32[]{:S(2)}) collective-permute-start(f32[2048,512]{1,0:T(8,128)} %copy-done.6), channel_id=1, source_target_pairs={{0,1},{4,5},{8,9},{12,13},{16,17},{20,21},{24,25},{28,29}} | collective-permute-start | bytes 12582920 | tf_op jit(solution)/shard_map/ppermute | solution.py:30
  298.0 118.0 %collective-permute-start.3 = (f32[2048,512]{1,0:T(8,128)}, f32[2048,512]{1,0:T(8,128)}, u32[]{:S(2)}, u32[]{:S(2)}) collective-permute-start(f32[2048,512]{1,0:T(8,128)} %copy-done.6), channel_id=1, source_target_pairs={{0,2},{4,6},{8,10},{12,14},{16,18},{20,22},{24,26},{28,30}} | collective-permute-start | bytes 12582920 | tf_op jit(solution)/shard_map/ppermute | solution.py:30
  300.6 115.5 %collective-permute-start.2 = (f32[2048,512]{1,0:T(8,128)}, f32[2048,512]{1,0:T(8,128)}, u32[]{:S(2)}, u32[]{:S(2)}) collective-permute-start(f32[2048,512]{1,0:T(8,128)} %copy-done.6), channel_id=1, source_target_pairs={{0,3},{4,7},{8,11},{12,15},{16,19},{20,23},{24,27},{28,31}} | collective-permute-start | bytes 12582920 | tf_op jit(solution)/shard_map/ppermute | solution.py:30
  402.4 18.4 %copy-start.17 = (f32[512,512]{1,0:T(8,128)}, f32[512,512]{1,0:T(8,128)S(1)}, u32[]{:S(2)}) copy-start(f32[512,512]{1,0:T(8,128)S(1)} %get-tuple-element.330) | copy-start | bytes 3145732
  412.6 15.2 %copy-start.28 = (f32[128,128]{1,0:T(8,128)}, f32[128,128]{1,0:T(8,128)S(1)}, u32[]{:S(2)}) copy-start(f32[128,128]{1,0:T(8,128)S(1)} %copy.88) | copy-start | bytes 196612
  440.2 58.7 %copy-start.22 = (f32[256,256]{1,0:T(8,128)S(1)}, f32[256,256]{1,0:T(8,128)}, u32[]{:S(2)}) copy-start(f32[256,256]{1,0:T(8,128)} %copy-done.21) | copy-start | bytes 786436
  440.2 58.7 %copy-start.25 = (f32[128,128]{1,0:T(8,128)S(1)}, f32[128,128]{1,0:T(8,128)}, u32[]{:S(2)}) copy-start(f32[128,128]{1,0:T(8,128)} %copy-done.24) | copy-start | bytes 196612
  440.2 58.7 %copy-start.27 = (f32[128,128]{1,0:T(8,128)S(1)}, f32[128,128]{1,0:T(8,128)}, u32[]{:S(2)}) copy-start(f32[128,128]{1,0:T(8,128)} %copy-done.26) | copy-start | bytes 196612
  440.3 13.5 %collective-permute-start.15 = (f32[512,512]{1,0:T(8,128)}, f32[512,512]{1,0:T(8,128)S(1)}, u32[]{:S(2)}, u32[]{:S(2)}) collective-permute-start(f32[512,512]{1,0:T(8,128)} %get-tuple-element.317), channel_id=1, source_target_pairs={{1,0},{5,4},{9,1},{13,5},{17,2},{21,6},{25,3},{29,7}} | collective-permute-start | bytes 3145736 | tf_op jit(solution)/shard_map/ppermute | solution.py:136
  441.7 23.3 %collective-permute-start.14 = (f32[512,512]{1,0:T(8,128)}, f32[512,512]{1,0:T(8,128)}, u32[]{:S(2)}, u32[]{:S(2)}) collective-permute-start(f32[512,512]{1,0:T(8,128)} %get-tuple-element.318), channel_id=1, source_target_pairs={{1,8},{5,12},{9,9},{13,13},{17,10},{21,14},{25,11},{29,15}} | collective-permute-start | bytes 3145736 | tf_op jit(solution)/shard_map/ppermute | solution.py:136
  444.0 32.2 %collective-permute-start.13 = (f32[512,512]{1,0:T(8,128)}, f32[512,512]{1,0:T(8,128)}, u32[]{:S(2)}, u32[]{:S(2)}) collective-permute-start(f32[512,512]{1,0:T(8,128)} %get-tuple-element.319), channel_id=1, source_target_pairs={{1,16},{5,20},{9,17},{13,21},{17,18},{21,22},{25,19},{29,23}} | collective-permute-start | bytes 3145736 | tf_op jit(solution)/shard_map/ppermute | solution.py:136
  446.3 47.7 %collective-permute-start.12 = (f32[512,512]{1,0:T(8,128)}, f32[512,512]{1,0:T(8,128)}, u32[]{:S(2)}, u32[]{:S(2)}) collective-permute-start(f32[512,512]{1,0:T(8,128)} %get-tuple-element.320), channel_id=1, source_target_pairs={{1,24},{5,28},{9,25},{13,29},{17,26},{21,30},{25,27},{29,31}} | collective-permute-start | bytes 3145736 | tf_op jit(solution)/shard_map/ppermute | solution.py:136
  583.1 56.7 %collective-permute-start.11 = (f32[2048,512]{1,0:T(8,128)}, f32[2048,512]{1,0:T(8,128)}, u32[]{:S(2)}, u32[]{:S(2)}) collective-permute-start(f32[2048,512]{1,0:T(8,128)} %copy-done), channel_id=1, source_target_pairs={{1,0},{5,4},{9,8},{13,12},{17,16},{21,20},{25,24},{29,28}} | collective-permute-start | bytes 12582920 | tf_op jit(solution)/shard_map/ppermute | solution.py:30
  586.4 53.4 %collective-permute-start.10 = (f32[2048,512]{1,0:T(8,128)}, f32[2048,512]{1,0:T(8,128)}, u32[]{:S(2)}, u32[]{:S(2)}) collective-permute-start(f32[2048,512]{1,0:T(8,128)} %copy-done), channel_id=1, source_target_pairs={{1,2},{5,6},{9,10},{13,14},{17,18},{21,22},{25,26},{29,30}} | collective-permute-start | bytes 12582920 | tf_op jit(solution)/shard_map/ppermute | solution.py:30
  589.6 88.8 %collective-permute-start.9 = (f32[2048,512]{1,0:T(8,128)}, f32[2048,512]{1,0:T(8,128)}, u32[]{:S(2)}, u32[]{:S(2)}) collective-permute-start(f32[2048,512]{1,0:T(8,128)} %copy-done), channel_id=1, source_target_pairs={{1,3},{5,7},{9,11},{13,15},{17,19},{21,23},{25,27},{29,31}} | collective-permute-start | bytes 12582920 | tf_op jit(solution)/shard_map/ppermute | solution.py:30
  632.4 46.0 %copy-start.1 = (f32[2048,512]{1,0:T(8,128)S(1)}, f32[2048,512]{1,0:T(8,128)}, u32[]{:S(2)}) copy-start(f32[2048,512]{1,0:T(8,128)} %copy-done) | copy-start | bytes 12582916
  639.8 42.3 %copy-start.11 = (f32[512,512]{1,0:T(8,128)S(1)}, f32[512,512]{1,0:T(8,128)}, u32[]{:S(2)}) copy-start(f32[512,512]{1,0:T(8,128)} %copy-done.10) | copy-start | bytes 3145732
  (21 other events, 120.9 us)
Sparse Core Ops, SparseCore 0:
  9.5 72.1 all-gather.3
  296.2 121.2 all-gather.5
  497.3 121.8 all-gather.7

commit v6 on v4

--- a/solution.py
+++ b/solution.py
@@ -53,7 +53,8 @@
     colblk = colblk[: panels * NB].reshape(panels, NB, NB)
     send_a = jnp.where(col_id == 0, colblk[0], colblk[1])
     recv_a = lax.ppermute(send_a, "col", [(0, 1), (1, 2)])
-    recv_b = lax.ppermute(colblk[0:2], "col", [(0, 2)])
+    recv_b0 = lax.ppermute(colblk[0], "col", [(0, 2)])
+    recv_b1 = lax.ppermute(colblk[1], "col", [(0, 2)])
 
     def pick(options, default):
         out = default
@@ -61,8 +62,8 @@
             out = jnp.where(col_id == col, val, out)
         return out
 
-    g00 = pick([(0, colblk[0]), (1, recv_a), (2, recv_b[0])], identity)
-    g10 = pick([(1, colblk[0].T), (2, recv_b[1])], jnp.zeros_like(identity))
+    g00 = pick([(0, colblk[0]), (1, recv_a), (2, recv_b0)], identity)
+    g10 = pick([(1, colblk[0].T), (2, recv_b1)], jnp.zeros_like(identity))
     g11 = pick([(1, colblk[1]), (2, recv_a)], identity)
     g20 = pick([(2, colblk[0].T)], jnp.zeros_like(identity))
     g21 = pick([(2, colblk[1].T)], jnp.zeros_like(identity))

time: 818 us -> 817 us (level)
  transfers between devices with their start and end apart: 19 -> 20, of which waited for: 8 -> 8; matrix products, arithmetic and copies ran while one was open for 41% -> 40% of each run, Pallas kernels for 0% -> 0%
where the time goes in v6:
time: 817 us; the launch traced here: 803 us
  other arithmetic  327 us (40%)
  waiting for transfers between devices  217 us (27%)
  matrix products  169 us (21%)
  local copies, waits for them, and re-layouts  39.3 us (5%)
  starting transfers between devices  35.6 us (4%)
  between operations  15 us (2%)
    dot_general x32, matrix products, times_transposed(): lax.dot_general(left, right, (((1,), (1,)), ((), ())), precision=precisio...  155 us
    another operation x36, other arithmetic, factor(): low = jnp.linalg.cholesky(lead)  154 us
    another operation x21, other arithmetic, factor(): inv = jax.scipy.linalg.solve_triangular(low, eye_sub, lower=True)  127 us
    ppermute x8, waiting for transfers between devices, spread_columns_of(): received = lax.ppermute(pieces[piece], ('row', 'col'), route)  103 us
    all_gather x1, waiting for transfers between devices, local_body(): colblk = lax.all_gather(tile, 'row', axis=0, tiled=True)  73.2 us
    ppermute x6, waiting for transfers between devices, bcast_col(): got = lax.ppermute(value, 'col', [(owner, target)])  22.6 us
    ppermute x1, waiting for transfers between devices, local_body(): recv_a = lax.ppermute(send_a, 'col', [(0, 1), (1, 2)])  18.5 us
    ppermute x6, starting transfers between devices, bcast_col(): got = lax.ppermute(value, 'col', [(owner, target)])  17 us
  transfers between devices with their start and end apart: 20, of which 8 were waited for; matrix products, arithmetic and copies ran while one was open for 40% of the time, Pallas kernels for 0%

profile of v6, /device:TPU:25, one launch (start us, length us, event | category | flops | bytes accessed | tf_op | source)
XLA Modules:
  0.0 803.4 jit_solution(2499651957438709675)
XLA Ops:
  8.5 73.2 %all-gather.4.cloned.1.call-done = f32[2048,512]{1,0:T(8,128)} async-done(((f32[256,512]{1,0:T(8,128)}), f32[2048,512]{1,0:T(8,128)}) %all-gather.4.cloned.1.call-update) | async-done | bytes 4194320 | tf_op jit(solution)/shard_map/all_gather | solution.py:52
  94.3 18.5 %collective-permute-done.1 = f32[512,512]{0,1:T(8,128)S(1)} collective-permute-done((f32[512,512]{0,1:T(8,128)}, f32[512,512]{0,1:T(8,128)S(1)}, u32[]{:S(2)}, u32[]{:S(2)}) %collective-permute-start.1) | collective-permute-done | bytes 1048608 | tf_op jit(solution)/shard_map/ppermute | solution.py:55
  117.4 11.7 %cholesky.194 = f32[128,128]{1,0:T(8,128)S(1)} custom-call(f32[128,128]{1,0:T(8,128)S(1)} %fusion.147), custom_call_target="Cholesky" | custom-call | tf_op jit(solution)/shard_map/jit(cholesky)/cholesky | solution.py:83
  130.4 9.8 %custom-call.16 = f32[1,128,128]{1,2,0:T(8,128)S(1)} custom-call(f32[1,128,128]{2,1,0:T(8,128)S(1)} %get-tuple-element.311), custom_call_target="InvertDiagBlocksLowerTriangular" | custom-call | tf_op jit(solution)/shard_map/jit(_solve_triangular)/triangular_solve | solution.py:84
  143.9 11.8 %cholesky.205 = f32[128,128]{1,0:T(8,128)S(1)} custom-call(f32[128,128]{1,0:T(8,128)S(1)} %fusion.145), custom_call_target="Cholesky" | custom-call | tf_op jit(solution)/shard_map/jit(cholesky)/cholesky | solution.py:83
  157.0 9.8 %custom-call.17 = f32[1,128,128]{1,2,0:T(8,128)S(1)} custom-call(f32[1,128,128]{2,1,0:T(8,128)S(1)} %get-tuple-element.340), custom_call_target="InvertDiagBlocksLowerTriangular" | custom-call | tf_op jit(solution)/shard_map/jit(_solve_triangular)/triangular_solve | solution.py:84
  168.1 11.7 %cholesky.216 = f32[128,128]{1,0:T(8,128)S(1)} custom-call(f32[128,128]{1,0:T(8,128)S(1)} %fusion.143), custom_call_target="Cholesky" | custom-call | tf_op jit(solution)/shard_map/jit(cholesky)/cholesky | solution.py:83
  181.1 9.8 %custom-call.18 = f32[1,128,128]{1,2,0:T(8,128)S(1)} custom-call(f32[1,128,128]{2,1,0:T(8,128)S(1)} %get-tuple-element.337), custom_call_target="InvertDiagBlocksLowerTriangular" | custom-call | tf_op jit(solution)/shard_map/jit(_solve_triangular)/triangular_solve | solution.py:84
  191.9 11.9 %cholesky.227 = f32[128,128]{1,0:T(8,128)S(1)} custom-call(f32[128,128]{1,0:T(8,128)S(1)} %fusion.141), custom_call_target="Cholesky" | custom-call | tf_op jit(solution)/shard_map/jit(cholesky)/cholesky | solution.py:83
  206.2 9.8 %custom-call.19 = f32[1,128,128]{1,2,0:T(8,128)S(1)} custom-call(f32[1,128,128]{2,1,0:T(8,128)S(1)} %get-tuple-element.335), custom_call_target="InvertDiagBlocksLowerTriangular" | custom-call | tf_op jit(solution)/shard_map/jit(_solve_triangular)/triangular_solve | solution.py:84
  234.4 48.5 %collective-permute-done.9 = f32[512,512]{1,0:T(8,128)} collective-permute-done((f32[512,512]{1,0:T(8,128)}, f32[512,512]{1,0:T(8,128)}, u32[]{:S(2)}, u32[]{:S(2)}) %collective-permute-start.9) | collective-permute-done | bytes 1048608 | tf_op jit(solution)/shard_map/ppermute | solution.py:137
  306.0 11.7 %cholesky.238 = f32[128,128]{1,0:T(8,128)S(1)} custom-call(f32[128,128]{1,0:T(8,128)S(1)} %fusion.139), custom_call_target="Cholesky" | custom-call | tf_op jit(solution)/shard_map/jit(cholesky)/cholesky | solution.py:83
  319.0 10.0 %custom-call.20 = f32[1,128,128]{1,2,0:T(8,128)S(1)} custom-call(f32[1,128,128]{2,1,0:T(8,128)S(1)} %get-tuple-element.309), custom_call_target="InvertDiagBlocksLowerTriangular" | custom-call | tf_op jit(solution)/shard_map/jit(_solve_triangular)/triangular_solve | solution.py:84
  332.6 11.7 %cholesky.249 = f32[128,128]{1,0:T(8,128)S(1)} custom-call(f32[128,128]{1,0:T(8,128)S(1)} %fusion.137), custom_call_target="Cholesky" | custom-call | tf_op jit(solution)/shard_map/jit(cholesky)/cholesky | solution.py:83
  345.7 9.8 %custom-call.21 = f32[1,128,128]{1,2,0:T(8,128)S(1)} custom-call(f32[1,128,128]{2,1,0:T(8,128)S(1)} %get-tuple-element.334), custom_call_target="InvertDiagBlocksLowerTriangular" | custom-call | tf_op jit(solution)/shard_map/jit(_solve_triangular)/triangular_solve | solution.py:84
  357.4 11.9 %cholesky.260 = f32[128,128]{1,0:T(8,128)S(1)} custom-call(f32[128,128]{1,0:T(8,128)S(1)} %fusion.135), custom_call_target="Cholesky" | custom-call | tf_op jit(solution)/shard_map/jit(cholesky)/cholesky | solution.py:83
  370.6 9.8 %custom-call.22 = f32[1,128,128]{1,2,0:T(8,128)S(1)} custom-call(f32[1,128,128]{2,1,0:T(8,128)S(1)} %get-tuple-element.331), custom_call_target="InvertDiagBlocksLowerTriangular" | custom-call | tf_op jit(solution)/shard_map/jit(_solve_triangular)/triangular_solve | solution.py:84
  381.4 11.7 %cholesky.271 = f32[128,128]{1,0:T(8,128)S(1)} custom-call(f32[128,128]{1,0:T(8,128)S(1)} %fusion.133), custom_call_target="Cholesky" | custom-call | tf_op jit(solution)/shard_map/jit(cholesky)/cholesky | solution.py:83
  394.4 9.8 %custom-call.23 = f32[1,128,128]{1,2,0:T(8,128)S(1)} custom-call(f32[1,128,128]{2,1,0:T(8,128)S(1)} %get-tuple-element.329), custom_call_target="InvertDiagBlocksLowerTriangular" | custom-call | tf_op jit(solution)/shard_map/jit(_solve_triangular)/triangular_solve | solution.py:84
  442.9 11.2 %collective-permute-done.15 = f32[512,512]{1,0:T(8,128)S(1)} collective-permute-done((f32[512,512]{1,0:T(8,128)S(1)}, f32[512,512]{1,0:T(8,128)S(1)}, u32[]{:S(2)}, u32[]{:S(2)}) %collective-permute-start.15) | collective-permute-done | bytes 1048608 | tf_op jit(solution)/shard_map/ppermute | solution.py:137
  454.2 11.2 %collective-permute-done.14 = f32[512,512]{1,0:T(8,128)S(1)} collective-permute-done((f32[512,512]{1,0:T(8,128)S(1)}, f32[512,512]{1,0:T(8,128)S(1)}, u32[]{:S(2)}, u32[]{:S(2)}) %collective-permute-start.14) | collective-permute-done | bytes 1048608 | tf_op jit(solution)/shard_map/ppermute | solution.py:137
  465.4 24.7 %collective-permute-done.13 = f32[512,512]{1,0:T(8,128)S(1)} collective-permute-done((f32[512,512]{1,0:T(8,128)S(1)}, f32[512,512]{1,0:T(8,128)S(1)}, u32[]{:S(2)}, u32[]{:S(2)}) %collective-permute-start.13) | collective-permute-done | bytes 1048608 | tf_op jit(solution)/shard_map/ppermute | solution.py:137
  515.9 11.7 %cholesky.282 = f32[128,128]{1,0:T(8,128)S(1)} custom-call(f32[128,128]{1,0:T(8,128)S(1)} %fusion.131), custom_call_target="Cholesky" | custom-call | tf_op jit(solution)/shard_map/jit(cholesky)/cholesky | solution.py:83
  528.8 9.8 %custom-call.24 = f32[1,128,128]{1,2,0:T(8,128)S(1)} custom-call(f32[1,128,128]{2,1,0:T(8,128)S(1)} %get-tuple-element.307), custom_call_target="InvertDiagBlocksLowerTriangular" | custom-call | tf_op jit(solution)/shard_map/jit(_solve_triangular)/triangular_solve | solution.py:84
  544.0 11.9 %cholesky.293 = f32[128,128]{1,0:T(8,128)S(1)} custom-call(f32[128,128]{1,0:T(8,128)S(1)} %fusion.129), custom_call_target="Cholesky" | custom-call | tf_op jit(solution)/shard_map/jit(cholesky)/cholesky | solution.py:83
  573.5 13.2 %cholesky.304 = f32[128,128]{1,0:T(8,128)} custom-call(f32[128,128]{1,0:T(8,128)} %fusion.127), custom_call_target="Cholesky" | custom-call | tf_op jit(solution)/shard_map/jit(cholesky)/cholesky | solution.py:83
  602.1 11.3 %custom-call.26 = f32[1,128,128]{1,2,0:T(8,128)} custom-call(f32[1,128,128]{2,1,0:T(8,128)} %get-tuple-element.325), custom_call_target="InvertDiagBlocksLowerTriangular" | custom-call | tf_op jit(solution)/shard_map/jit(_solve_triangular)/triangular_solve | solution.py:84
  617.6 12.5 %cholesky.315 = f32[128,128]{1,0:T(8,128)S(1)} custom-call(f32[128,128]{1,0:T(8,128)} %fusion.125), custom_call_target="Cholesky" | custom-call | tf_op jit(solution)/shard_map/jit(cholesky)/cholesky | solution.py:83
  631.4 10.4 %custom-call.27 = f32[1,128,128]{1,2,0:T(8,128)} custom-call(f32[1,128,128]{2,1,0:T(8,128)S(1)} %get-tuple-element.323), custom_call_target="InvertDiagBlocksLowerTriangular" | custom-call | tf_op jit(solution)/shard_map/jit(_solve_triangular)/triangular_solve | solution.py:84
  659.5 22.6 %collective-permute-done.6 = f32[2048,512]{1,0:T(8,128)} collective-permute-done((f32[2048,512]{1,0:T(8,128)}, f32[2048,512]{1,0:T(8,128)}, u32[]{:S(2)}, u32[]{:S(2)}) %collective-permute-start.6) | collective-permute-done | bytes 4194336 | tf_op jit(solution)/shard_map/ppermute | solution.py:30
  693.2 10.2 %fusion.20 = f32[2048,512]{1,0:T(8,128)} fusion(f32[2048,512]{1,0:T(8,128)S(1)} %fusion.208, f32[2048,512]{1,0:T(8,128)S(1)} %fusion.207, f32[2048,4096]{1,0:T(8,128)} %param.54, pred[2048]{0:T(1024)(128)(4,1)S(1)} %copy-done.35, f32[256,256]{1,0:T(8,128)S(1)} %copy-done.23, f32[128,128]{1,0:T(8,128)S(1)} %copy.111, ...), kind=kOutput, calls=%fused_computation.21 | convolution fusion | flops 6447169536 | bytes 17565696 | tf_op jit(solution)/shard_map/dot_general | solution.py:17
  721.2 67.3 %subtract_select_fusion = f32[2048,4096]{1,0:T(8,128)} fusion(f32[2048,4096]{1,0:T(8,128)} %param.54, f32[4096,512]{1,0:T(8,128)} %bitcast.199, f32[4096,512]{1,0:T(8,128)} %bitcast.198, s32[4096]{0:T(1024)S(1)} %fusion.167, s32[2048]{0:T(1024)S(1)} %copy-done.36, pred[2048]{0:T(1024)(128)(4,1)S(1)} %copy-done.37, f32[2048,512]{1,0:T(8,128)} %copy-done.6, ...), kind=kOutput, calls=%fused_computation | convolution fusion | flops 51579453440 | bytes 92301312 | tf_op jit(solution)/shard_map/dot_general | solution.py:17
  (294 shorter events, 247.4 us)
Async XLA Ops:
  6.5 75.2 %all-gather.4.cloned.1.call-start = ((), (), s32[]{:S(2)}) async-start(), calls=%async_computation | async-start | bytes 4718592 | tf_op jit(solution)/shard_map/all_gather | solution.py:52
  8.4 696.9 %all-gather.6.cloned.1.call-start = ((), (), s32[]{:S(2)}) async-start(), calls=%async_computation.1 | async-start | bytes 9437184 | tf_op jit(solution)/shard_map/all_gather | solution.py:139
  87.5 25.4 %collective-permute-start.1 = (f32[512,512]{0,1:T(8,128)}, f32[512,512]{0,1:T(8,128)S(1)}, u32[]{:S(2)}, u32[]{:S(2)}) collective-permute-start(f32[512,512]{0,1:T(8,128)} %broadcast_select_fusion), channel_id=1, source_target_pairs={{0,1},{1,2},{4,5},{5,6},{8,9},{9,10},{12,13},{13,14},{16,17},{17,1... | collective-permute-start | bytes 3145736 | tf_op jit(solution)/shard_map/ppermute | solution.py:55
  91.2 21.6 %collective-permute-start = (f32[512,512]{0,1:T(8,128)S(1)}, f32[512,512]{0,1:T(8,128)}, u32[]{:S(2)}, u32[]{:S(2)}) collective-permute-start(f32[512,512]{0,1:T(8,128)S(1)} %copy.56), channel_id=1, source_target_pairs={{0,2},{4,6},{8,10},{12,14},{16,18},{20,22},{24,26},{28,30}} | collective-permute-start | bytes 3145736 | tf_op jit(solution)/shard_map/ppermute | solution.py:56
  205.0 20.7 %copy-start.16 = (f32[512,512]{1,0:T(8,128)}, f32[512,512]{1,0:T(8,128)S(1)}, u32[]{:S(2)}) copy-start(f32[512,512]{1,0:T(8,128)S(1)} %get-tuple-element.336) | copy-start | bytes 3145732
  205.8 89.4 %copy-start.26 = (f32[256,256]{1,0:T(8,128)}, f32[256,256]{1,0:T(8,128)S(1)}, u32[]{:S(2)}) copy-start(f32[256,256]{1,0:T(8,128)S(1)} %select_maximum_fusion.8) | copy-start | bytes 786436
  216.4 78.8 %copy-start.30 = (f32[128,128]{1,0:T(8,128)}, f32[128,128]{1,0:T(8,128)S(1)}, u32[]{:S(2)}) copy-start(f32[128,128]{1,0:T(8,128)S(1)} %copy.72) | copy-start | bytes 196612
  217.1 78.1 %copy-start.24 = (f32[256,256]{1,0:T(8,128)}, f32[256,256]{1,0:T(8,128)S(1)}, u32[]{:S(2)}) copy-start(f32[256,256]{1,0:T(8,128)S(1)} %convolution_negate_fusion.2) | copy-start | bytes 786436
  228.1 66.7 %copy-start.9 = (f32[512,512]{0,1:T(8,128)S(1)}, f32[512,512]{0,1:T(8,128)}, u32[]{:S(2)}) copy-start(f32[512,512]{0,1:T(8,128)} %copy-done.8) | copy-start | bytes 3145732
  229.0 5.4 collective-permute-start.12
  229.7 4.6 collective-permute-start.11
  231.4 3.0 collective-permute-start.10
  233.1 49.9 %collective-permute-start.9 = (f32[512,512]{1,0:T(8,128)}, f32[512,512]{1,0:T(8,128)}, u32[]{:S(2)}, u32[]{:S(2)}) collective-permute-start(f32[512,512]{1,0:T(8,128)} %get-tuple-element.316), channel_id=1, source_target_pairs={{0,24},{4,28},{8,25},{12,29},{16,26},{20,30},{24,27},{28,31}} | collective-permute-start | bytes 3145736 | tf_op jit(solution)/shard_map/ppermute | solution.py:137
  286.1 427.2 %all-gather.8.cloned.1.call-start = ((), (), s32[]{:S(2)}) async-start(), calls=%async_computation.2 | async-start | bytes 9437184 | tf_op jit(solution)/shard_map/all_gather | solution.py:139
  286.2 9.0 %collective-permute-start.5 = (f32[512,512]{0,1:T(8,128)}, f32[512,512]{0,1:T(8,128)}, u32[]{:S(2)}, u32[]{:S(2)}) collective-permute-start(f32[512,512]{0,1:T(8,128)} %copy.58), channel_id=1, source_target_pairs={{0,2},{4,6},{8,10},{12,14},{16,18},{20,22},{24,26},{28,30}} | collective-permute-start | bytes 3145736 | tf_op jit(solution)/shard_map/ppermute | solution.py:57
  287.8 120.2 %collective-permute-start.4 = (f32[2048,512]{1,0:T(8,128)}, f32[2048,512]{1,0:T(8,128)}, u32[]{:S(2)}, u32[]{:S(2)}) collective-permute-start(f32[2048,512]{1,0:T(8,128)} %copy-done.5), channel_id=1, source_target_pairs={{0,1},{4,5},{8,9},{12,13},{16,17},{20,21},{24,25},{28,29}} | collective-permute-start | bytes 12582920 | tf_op jit(solution)/shard_map/ppermute | solution.py:30
  289.1 118.9 %collective-permute-start.3 = (f32[2048,512]{1,0:T(8,128)}, f32[2048,512]{1,0:T(8,128)}, u32[]{:S(2)}, u32[]{:S(2)}) collective-permute-start(f32[2048,512]{1,0:T(8,128)} %copy-done.5), channel_id=1, source_target_pairs={{0,2},{4,6},{8,10},{12,14},{16,18},{20,22},{24,26},{28,30}} | collective-permute-start | bytes 12582920 | tf_op jit(solution)/shard_map/ppermute | solution.py:30
  291.8 116.3 %collective-permute-start.2 = (f32[2048,512]{1,0:T(8,128)}, f32[2048,512]{1,0:T(8,128)}, u32[]{:S(2)}, u32[]{:S(2)}) collective-permute-start(f32[2048,512]{1,0:T(8,128)} %copy-done.5), channel_id=1, source_target_pairs={{0,3},{4,7},{8,11},{12,15},{16,19},{20,23},{24,27},{28,31}} | collective-permute-start | bytes 12582920 | tf_op jit(solution)/shard_map/ppermute | solution.py:30
  429.1 61.0 %copy-start = (f32[2048,512]{1,0:T(8,128)}, f32[2048,512]{1,0:T(8,128)S(1)}, u32[]{:S(2)}) copy-start(f32[2048,512]{1,0:T(8,128)S(1)} %fusion.17) | copy-start | bytes 12582916
  429.7 64.6 %copy-start.25 = (f32[256,256]{1,0:T(8,128)S(1)}, f32[256,256]{1,0:T(8,128)}, u32[]{:S(2)}) copy-start(f32[256,256]{1,0:T(8,128)} %copy-done.24) | copy-start | bytes 786436
  429.7 64.6 %copy-start.27 = (f32[256,256]{1,0:T(8,128)S(1)}, f32[256,256]{1,0:T(8,128)}, u32[]{:S(2)}) copy-start(f32[256,256]{1,0:T(8,128)} %copy-done.26) | copy-start | bytes 786436
  429.7 64.6 %copy-start.31 = (f32[128,128]{1,0:T(8,128)S(1)}, f32[128,128]{1,0:T(8,128)}, u32[]{:S(2)}) copy-start(f32[128,128]{1,0:T(8,128)} %copy-done.30) | copy-start | bytes 196612
  429.7 13.2 %collective-permute-start.16 = (f32[512,512]{1,0:T(8,128)S(1)}, f32[512,512]{1,0:T(8,128)S(1)}, u32[]{:S(2)}, u32[]{:S(2)}) collective-permute-start(f32[512,512]{1,0:T(8,128)S(1)} %get-tuple-element.317), channel_id=1, source_target_pairs={{1,0},{5,4},{9,1},{13,5},{17,2},{21,6},{25,3},{29,7}} | collective-permute-start | bytes 3145736 | tf_op jit(solution)/shard_map/ppermute | solution.py:137
  431.2 22.9 %collective-permute-start.15 = (f32[512,512]{1,0:T(8,128)S(1)}, f32[512,512]{1,0:T(8,128)S(1)}, u32[]{:S(2)}, u32[]{:S(2)}) collective-permute-start(f32[512,512]{1,0:T(8,128)S(1)} %get-tuple-element.318), channel_id=1, source_target_pairs={{1,8},{5,12},{9,9},{13,13},{17,10},{21,14},{25,11},{29,15}} | collective-permute-start | bytes 3145736 | tf_op jit(solution)/shard_map/ppermute | solution.py:137
  432.6 32.8 %collective-permute-start.14 = (f32[512,512]{1,0:T(8,128)S(1)}, f32[512,512]{1,0:T(8,128)S(1)}, u32[]{:S(2)}, u32[]{:S(2)}) collective-permute-start(f32[512,512]{1,0:T(8,128)S(1)} %get-tuple-element.319), channel_id=1, source_target_pairs={{1,16},{5,20},{9,17},{13,21},{17,18},{21,22},{25,19},{29,23}} | collective-permute-start | bytes 3145736 | tf_op jit(solution)/shard_map/ppermute | solution.py:137
  434.0 56.2 %collective-permute-start.13 = (f32[512,512]{1,0:T(8,128)S(1)}, f32[512,512]{1,0:T(8,128)S(1)}, u32[]{:S(2)}, u32[]{:S(2)}) collective-permute-start(f32[512,512]{1,0:T(8,128)S(1)} %get-tuple-element.320), channel_id=1, source_target_pairs={{1,24},{5,28},{9,25},{13,29},{17,26},{21,30},{25,27},{29,31}} | collective-permute-start | bytes 3145736 | tf_op jit(solution)/shard_map/ppermute | solution.py:137
  569.8 43.6 %copy-start.28 = (f32[256,256]{0,1:T(8,128)}, f32[256,256]{0,1:T(8,128)S(1)}, u32[]{:S(2)}) copy-start(f32[256,256]{0,1:T(8,128)S(1)} %convolution_subtract_fusion.5) | copy-start | bytes 786436
  586.7 72.8 %collective-permute-start.8 = (f32[2048,512]{1,0:T(8,128)}, f32[2048,512]{1,0:T(8,128)}, u32[]{:S(2)}, u32[]{:S(2)}) collective-permute-start(f32[2048,512]{1,0:T(8,128)} %copy-done), channel_id=1, source_target_pairs={{1,0},{5,4},{9,8},{13,12},{17,16},{21,20},{25,24},{29,28}} | collective-permute-start | bytes 12582920 | tf_op jit(solution)/shard_map/ppermute | solution.py:30
  590.0 69.4 %collective-permute-start.7 = (f32[2048,512]{1,0:T(8,128)}, f32[2048,512]{1,0:T(8,128)}, u32[]{:S(2)}, u32[]{:S(2)}) collective-permute-start(f32[2048,512]{1,0:T(8,128)} %copy-done), channel_id=1, source_target_pairs={{1,2},{5,6},{9,10},{13,14},{17,18},{21,22},{25,26},{29,30}} | collective-permute-start | bytes 12582920 | tf_op jit(solution)/shard_map/ppermute | solution.py:30
  593.3 88.7 %collective-permute-start.6 = (f32[2048,512]{1,0:T(8,128)}, f32[2048,512]{1,0:T(8,128)}, u32[]{:S(2)}, u32[]{:S(2)}) collective-permute-start(f32[2048,512]{1,0:T(8,128)} %copy-done), channel_id=1, source_target_pairs={{1,3},{5,7},{9,11},{13,15},{17,19},{21,23},{25,27},{29,31}} | collective-permute-start | bytes 12582920 | tf_op jit(solution)/shard_map/ppermute | solution.py:30
  631.4 28.0 %copy-start.14 = (f32[512,512]{1,0:T(8,128)}, f32[512,512]{1,0:T(8,128)S(1)}, u32[]{:S(2)}) copy-start(f32[512,512]{1,0:T(8,128)S(1)} %get-tuple-element.324) | copy-start | bytes 3145732
  652.0 30.0 %copy-start.1 = (f32[2048,512]{1,0:T(8,128)S(1)}, f32[2048,512]{1,0:T(8,128)}, u32[]{:S(2)}) copy-start(f32[2048,512]{1,0:T(8,128)} %copy-done) | copy-start | bytes 12582916
  (26 other events, 180.7 us)
Sparse Core Ops, SparseCore 0:
  9.5 72.1 all-gather.3
  286.2 121.2 all-gather.5
  491.9 121.2 all-gather.7

commit v7 on v6

--- a/solution.py
+++ b/solution.py
@@ -51,8 +51,8 @@
     tile = gram[0:rblock, 0:NB]
     colblk = lax.all_gather(tile, "row", axis=0, tiled=True)
     colblk = colblk[: panels * NB].reshape(panels, NB, NB)
-    send_a = jnp.where(col_id == 0, colblk[0], colblk[1])
-    recv_a = lax.ppermute(send_a, "col", [(0, 1), (1, 2)])
+    recv_a = lax.ppermute(colblk[0], "col", [(0, 1)])
+    recv_c = lax.ppermute(colblk[1], "col", [(1, 2)])
     recv_b0 = lax.ppermute(colblk[0], "col", [(0, 2)])
     recv_b1 = lax.ppermute(colblk[1], "col", [(0, 2)])
 
@@ -64,7 +64,7 @@
 
     g00 = pick([(0, colblk[0]), (1, recv_a), (2, recv_b0)], identity)
     g10 = pick([(1, colblk[0].T), (2, recv_b1)], jnp.zeros_like(identity))
-    g11 = pick([(1, colblk[1]), (2, recv_a)], identity)
+    g11 = pick([(1, colblk[1]), (2, recv_c)], identity)
     g20 = pick([(2, colblk[0].T)], jnp.zeros_like(identity))
     g21 = pick([(2, colblk[1].T)], jnp.zeros_like(identity))
     g22 = pick([(2, colblk[2])], identity)

time: 817 us -> 817 us (level)
    ppermute x8, waiting for transfers between devices: 103 us -> 119 us  [spread_columns_of(): received = lax.ppermute(pieces[piece], ('row', 'col'), route)]
    ppermute x1 -> x2, waiting for transfers between devices: 18.5 us -> 3.44 us  [the longest x1 3.14 us: local_body(): recv_c = lax.ppermute(colblk[1], 'col', [(1, 2)])]
  transfers between devices with their start and end apart: 20 -> 21, of which waited for: 8 -> 9; matrix products, arithmetic and copies ran while one was open for 40% -> 40% of each run, Pallas kernels for 0% -> 0%
where the time goes in v7:
time: 817 us; the launch traced here: 804 us
  other arithmetic  326 us (40%)
  waiting for transfers between devices  218 us (27%)
  matrix products  171 us (21%)
  local copies, waits for them, and re-layouts  38.7 us (5%)
  starting transfers between devices  35.3 us (4%)
  between operations  14.9 us (2%)
    dot_general x32, matrix products, times_transposed(): lax.dot_general(left, right, (((1,), (1,)), ((), ())), precision=precisio...  156 us
    another operation x36, other arithmetic, factor(): low = jnp.linalg.cholesky(lead)  154 us
    another operation x21, other arithmetic, factor(): inv = jax.scipy.linalg.solve_triangular(low, eye_sub, lower=True)  127 us
    ppermute x8, waiting for transfers between devices, spread_columns_of(): received = lax.ppermute(pieces[piece], ('row', 'col'), route)  119 us
    all_gather x1, waiting for transfers between devices, local_body(): colblk = lax.all_gather(tile, 'row', axis=0, tiled=True)  73.2 us
    ppermute x6, waiting for transfers between devices, bcast_col(): got = lax.ppermute(value, 'col', [(owner, target)])  22.3 us
    ppermute x6, starting transfers between devices, bcast_col(): got = lax.ppermute(value, 'col', [(owner, target)])  16.9 us
  transfers between devices with their start and end apart: 21, of which 9 were waited for; matrix products, arithmetic and copies ran while one was open for 40% of the time, Pallas kernels for 0%

profile of v7, /device:TPU:25, one launch (start us, length us, event | category | flops | bytes accessed | tf_op | source)
XLA Modules:
  0.0 804.1 jit_solution(3686432577291371469)
XLA Ops:
  8.5 73.2 %all-gather.4.cloned.1.call-done = f32[2048,512]{1,0:T(8,128)} async-done(((f32[256,512]{1,0:T(8,128)}), f32[2048,512]{1,0:T(8,128)}) %all-gather.4.cloned.1.call-update) | async-done | bytes 4194320 | tf_op jit(solution)/shard_map/all_gather | solution.py:52
  93.0 11.7 %cholesky.194 = f32[128,128]{1,0:T(8,128)S(1)} custom-call(f32[128,128]{1,0:T(8,128)S(1)} %fusion.147), custom_call_target="Cholesky" | custom-call | tf_op jit(solution)/shard_map/jit(cholesky)/cholesky | solution.py:83
  106.0 9.8 %custom-call.16 = f32[1,128,128]{1,2,0:T(8,128)S(1)} custom-call(f32[1,128,128]{2,1,0:T(8,128)S(1)} %get-tuple-element.311), custom_call_target="InvertDiagBlocksLowerTriangular" | custom-call | tf_op jit(solution)/shard_map/jit(_solve_triangular)/triangular_solve | solution.py:84
  119.5 11.8 %cholesky.205 = f32[128,128]{1,0:T(8,128)S(1)} custom-call(f32[128,128]{1,0:T(8,128)S(1)} %fusion.145), custom_call_target="Cholesky" | custom-call | tf_op jit(solution)/shard_map/jit(cholesky)/cholesky | solution.py:83
  132.7 9.8 %custom-call.17 = f32[1,128,128]{1,2,0:T(8,128)S(1)} custom-call(f32[1,128,128]{2,1,0:T(8,128)S(1)} %get-tuple-element.340), custom_call_target="InvertDiagBlocksLowerTriangular" | custom-call | tf_op jit(solution)/shard_map/jit(_solve_triangular)/triangular_solve | solution.py:84
  144.4 11.7 %cholesky.216 = f32[128,128]{1,0:T(8,128)S(1)} custom-call(f32[128,128]{1,0:T(8,128)S(1)} %fusion.143), custom_call_target="Cholesky" | custom-call | tf_op jit(solution)/shard_map/jit(cholesky)/cholesky | solution.py:83
  157.5 9.8 %custom-call.18 = f32[1,128,128]{1,2,0:T(8,128)S(1)} custom-call(f32[1,128,128]{2,1,0:T(8,128)S(1)} %get-tuple-element.337), custom_call_target="InvertDiagBlocksLowerTriangular" | custom-call | tf_op jit(solution)/shard_map/jit(_solve_triangular)/triangular_solve | solution.py:84
  168.3 11.9 %cholesky.227 = f32[128,128]{1,0:T(8,128)S(1)} custom-call(f32[128,128]{1,0:T(8,128)S(1)} %fusion.141), custom_call_target="Cholesky" | custom-call | tf_op jit(solution)/shard_map/jit(cholesky)/cholesky | solution.py:83
  184.5 9.8 %custom-call.19 = f32[1,128,128]{1,2,0:T(8,128)S(1)} custom-call(f32[1,128,128]{2,1,0:T(8,128)S(1)} %get-tuple-element.335), custom_call_target="InvertDiagBlocksLowerTriangular" | custom-call | tf_op jit(solution)/shard_map/jit(_solve_triangular)/triangular_solve | solution.py:84
  212.7 58.9 %collective-permute-done.10 = f32[512,512]{1,0:T(8,128)} collective-permute-done((f32[512,512]{1,0:T(8,128)}, f32[512,512]{1,0:T(8,128)}, u32[]{:S(2)}, u32[]{:S(2)}) %collective-permute-start.10) | collective-permute-done | bytes 1048608 | tf_op jit(solution)/shard_map/ppermute | solution.py:137
  299.5 11.7 %cholesky.238 = f32[128,128]{1,0:T(8,128)S(1)} custom-call(f32[128,128]{1,0:T(8,128)S(1)} %fusion.139), custom_call_target="Cholesky" | custom-call | tf_op jit(solution)/shard_map/jit(cholesky)/cholesky | solution.py:83
  312.6 9.8 %custom-call.20 = f32[1,128,128]{1,2,0:T(8,128)S(1)} custom-call(f32[1,128,128]{2,1,0:T(8,128)S(1)} %get-tuple-element.309), custom_call_target="InvertDiagBlocksLowerTriangular" | custom-call | tf_op jit(solution)/shard_map/jit(_solve_triangular)/triangular_solve | solution.py:84
  326.4 11.7 %cholesky.249 = f32[128,128]{1,0:T(8,128)S(1)} custom-call(f32[128,128]{1,0:T(8,128)S(1)} %fusion.137), custom_call_target="Cholesky" | custom-call | tf_op jit(solution)/shard_map/jit(cholesky)/cholesky | solution.py:83
  339.4 9.8 %custom-call.21 = f32[1,128,128]{1,2,0:T(8,128)S(1)} custom-call(f32[1,128,128]{2,1,0:T(8,128)S(1)} %get-tuple-element.334), custom_call_target="InvertDiagBlocksLowerTriangular" | custom-call | tf_op jit(solution)/shard_map/jit(_solve_triangular)/triangular_solve | solution.py:84
  351.1 11.7 %cholesky.260 = f32[128,128]{1,0:T(8,128)S(1)} custom-call(f32[128,128]{1,0:T(8,128)S(1)} %fusion.135), custom_call_target="Cholesky" | custom-call | tf_op jit(solution)/shard_map/jit(cholesky)/cholesky | solution.py:83
  364.2 10.0 %custom-call.22 = f32[1,128,128]{1,2,0:T(8,128)S(1)} custom-call(f32[1,128,128]{2,1,0:T(8,128)S(1)} %get-tuple-element.331), custom_call_target="InvertDiagBlocksLowerTriangular" | custom-call | tf_op jit(solution)/shard_map/jit(_solve_triangular)/triangular_solve | solution.py:84
  375.2 11.7 %cholesky.271 = f32[128,128]{1,0:T(8,128)S(1)} custom-call(f32[128,128]{1,0:T(8,128)S(1)} %fusion.133), custom_call_target="Cholesky" | custom-call | tf_op jit(solution)/shard_map/jit(cholesky)/cholesky | solution.py:83
  388.3 9.8 %custom-call.23 = f32[1,128,128]{1,2,0:T(8,128)S(1)} custom-call(f32[1,128,128]{2,1,0:T(8,128)S(1)} %get-tuple-element.329), custom_call_target="InvertDiagBlocksLowerTriangular" | custom-call | tf_op jit(solution)/shard_map/jit(_solve_triangular)/triangular_solve | solution.py:84
  436.9 11.2 %collective-permute-done.16 = f32[512,512]{1,0:T(8,128)S(1)} collective-permute-done((f32[512,512]{1,0:T(8,128)S(1)}, f32[512,512]{1,0:T(8,128)S(1)}, u32[]{:S(2)}, u32[]{:S(2)}) %collective-permute-start.16) | collective-permute-done | bytes 1048608 | tf_op jit(solution)/shard_map/ppermute | solution.py:137
  448.1 11.3 %collective-permute-done.15 = f32[512,512]{1,0:T(8,128)S(1)} collective-permute-done((f32[512,512]{1,0:T(8,128)S(1)}, f32[512,512]{1,0:T(8,128)S(1)}, u32[]{:S(2)}, u32[]{:S(2)}) %collective-permute-start.15) | collective-permute-done | bytes 1048608 | tf_op jit(solution)/shard_map/ppermute | solution.py:137
  459.4 30.7 %collective-permute-done.14 = f32[512,512]{1,0:T(8,128)S(1)} collective-permute-done((f32[512,512]{1,0:T(8,128)S(1)}, f32[512,512]{1,0:T(8,128)S(1)}, u32[]{:S(2)}, u32[]{:S(2)}) %collective-permute-start.14) | collective-permute-done | bytes 1048608 | tf_op jit(solution)/shard_map/ppermute | solution.py:137
  515.7 11.7 %cholesky.282 = f32[128,128]{1,0:T(8,128)S(1)} custom-call(f32[128,128]{1,0:T(8,128)S(1)} %fusion.131), custom_call_target="Cholesky" | custom-call | tf_op jit(solution)/shard_map/jit(cholesky)/cholesky | solution.py:83
  528.9 9.8 %custom-call.24 = f32[1,128,128]{1,2,0:T(8,128)S(1)} custom-call(f32[1,128,128]{2,1,0:T(8,128)S(1)} %get-tuple-element.307), custom_call_target="InvertDiagBlocksLowerTriangular" | custom-call | tf_op jit(solution)/shard_map/jit(_solve_triangular)/triangular_solve | solution.py:84
  544.0 12.1 %cholesky.293 = f32[128,128]{1,0:T(8,128)S(1)} custom-call(f32[128,128]{1,0:T(8,128)S(1)} %fusion.129), custom_call_target="Cholesky" | custom-call | tf_op jit(solution)/shard_map/jit(cholesky)/cholesky | solution.py:83
  557.6 9.8 %custom-call.25 = f32[1,128,128]{1,2,0:T(8,128)S(1)} custom-call(f32[1,128,128]{2,1,0:T(8,128)S(1)} %get-tuple-element.328), custom_call_target="InvertDiagBlocksLowerTriangular" | custom-call | tf_op jit(solution)/shard_map/jit(_solve_triangular)/triangular_solve | solution.py:84
  574.0 13.2 %cholesky.304 = f32[128,128]{1,0:T(8,128)} custom-call(f32[128,128]{1,0:T(8,128)} %fusion.127), custom_call_target="Cholesky" | custom-call | tf_op jit(solution)/shard_map/jit(cholesky)/cholesky | solution.py:83
  602.8 11.3 %custom-call.26 = f32[1,128,128]{1,2,0:T(8,128)} custom-call(f32[1,128,128]{2,1,0:T(8,128)} %get-tuple-element.325), custom_call_target="InvertDiagBlocksLowerTriangular" | custom-call | tf_op jit(solution)/shard_map/jit(_solve_triangular)/triangular_solve | solution.py:84
  618.2 12.5 %cholesky.315 = f32[128,128]{1,0:T(8,128)S(1)} custom-call(f32[128,128]{1,0:T(8,128)} %fusion.125), custom_call_target="Cholesky" | custom-call | tf_op jit(solution)/shard_map/jit(cholesky)/cholesky | solution.py:83
  632.3 10.4 %custom-call.27 = f32[1,128,128]{1,2,0:T(8,128)} custom-call(f32[1,128,128]{2,1,0:T(8,128)S(1)} %get-tuple-element.323), custom_call_target="InvertDiagBlocksLowerTriangular" | custom-call | tf_op jit(solution)/shard_map/jit(_solve_triangular)/triangular_solve | solution.py:84
  660.3 22.3 %collective-permute-done.7 = f32[2048,512]{1,0:T(8,128)} collective-permute-done((f32[2048,512]{1,0:T(8,128)}, f32[2048,512]{1,0:T(8,128)}, u32[]{:S(2)}, u32[]{:S(2)}) %collective-permute-start.7) | collective-permute-done | bytes 4194336 | tf_op jit(solution)/shard_map/ppermute | solution.py:30
  693.7 10.2 %fusion.20 = f32[2048,512]{1,0:T(8,128)} fusion(f32[2048,512]{1,0:T(8,128)S(1)} %fusion.207, f32[2048,512]{1,0:T(8,128)S(1)} %fusion.206, f32[2048,4096]{1,0:T(8,128)} %param.54, pred[2048]{0:T(1024)(128)(4,1)S(1)} %copy-done.33, f32[256,256]{1,0:T(8,128)S(1)} %copy-done.21, f32[128,128]{1,0:T(8,128)S(1)} %copy.107, ...), kind=kOutput, calls=%fused_computation.21 | convolution fusion | flops 6447169536 | bytes 17565696 | tf_op jit(solution)/shard_map/dot_general | solution.py:17
  721.7 67.3 %subtract_select_fusion = f32[2048,4096]{1,0:T(8,128)} fusion(f32[2048,4096]{1,0:T(8,128)} %param.54, f32[4096,512]{1,0:T(8,128)} %bitcast.199, f32[4096,512]{1,0:T(8,128)} %bitcast.198, s32[4096]{0:T(1024)S(1)} %fusion.167, s32[2048]{0:T(1024)S(1)} %copy-done.34, pred[2048]{0:T(1024)(128)(4,1)S(1)} %copy-done.35, f32[2048,512]{1,0:T(8,128)} %copy-done.6, ...), kind=kOutput, calls=%fused_computation | convolution fusion | flops 51579453440 | bytes 92301312 | tf_op jit(solution)/shard_map/dot_general | solution.py:17
  (289 shorter events, 240.6 us)
Async XLA Ops:
  6.5 75.2 %all-gather.4.cloned.1.call-start = ((), (), s32[]{:S(2)}) async-start(), calls=%async_computation | async-start | bytes 4718592 | tf_op jit(solution)/shard_map/all_gather | solution.py:52
  8.4 697.4 %all-gather.6.cloned.1.call-start = ((), (), s32[]{:S(2)}) async-start(), calls=%async_computation.1 | async-start | bytes 9437184 | tf_op jit(solution)/shard_map/all_gather | solution.py:139
  83.7 4.7 collective-permute-start.1
  85.0 3.4 collective-permute-start
  181.6 22.5 %copy-start.14 = (f32[512,512]{1,0:T(8,128)}, f32[512,512]{1,0:T(8,128)S(1)}, u32[]{:S(2)}) copy-start(f32[512,512]{1,0:T(8,128)S(1)} %get-tuple-element.336) | copy-start | bytes 3145732
  183.2 102.9 %copy-start.24 = (f32[256,256]{1,0:T(8,128)}, f32[256,256]{1,0:T(8,128)S(1)}, u32[]{:S(2)}) copy-start(f32[256,256]{1,0:T(8,128)S(1)} %select_maximum_fusion.8) | copy-start | bytes 786436
  194.7 91.4 %copy-start.28 = (f32[128,128]{1,0:T(8,128)}, f32[128,128]{1,0:T(8,128)S(1)}, u32[]{:S(2)}) copy-start(f32[128,128]{1,0:T(8,128)S(1)} %copy.69) | copy-start | bytes 196612
  195.4 90.7 %copy-start.22 = (f32[256,256]{1,0:T(8,128)}, f32[256,256]{1,0:T(8,128)S(1)}, u32[]{:S(2)}) copy-start(f32[256,256]{1,0:T(8,128)S(1)} %convolution_negate_fusion.2) | copy-start | bytes 786436
  207.3 5.3 collective-permute-start.13
  208.1 4.6 collective-permute-start.12
  209.7 3.0 collective-permute-start.11
  211.4 60.2 %collective-permute-start.10 = (f32[512,512]{1,0:T(8,128)}, f32[512,512]{1,0:T(8,128)}, u32[]{:S(2)}, u32[]{:S(2)}) collective-permute-start(f32[512,512]{1,0:T(8,128)} %get-tuple-element.316), channel_id=1, source_target_pairs={{0,24},{4,28},{8,25},{12,29},{16,26},{20,30},{24,27},{28,31}} | collective-permute-start | bytes 3145736 | tf_op jit(solution)/shard_map/ppermute | solution.py:137
  274.8 439.0 %all-gather.8.cloned.1.call-start = ((), (), s32[]{:S(2)}) async-start(), calls=%async_computation.2 | async-start | bytes 9437184 | tf_op jit(solution)/shard_map/all_gather | solution.py:139
  275.2 10.9 %collective-permute-start.5 = (f32[512,512]{0,1:T(8,128)S(1)}, f32[512,512]{0,1:T(8,128)}, u32[]{:S(2)}, u32[]{:S(2)}) collective-permute-start(f32[512,512]{0,1:T(8,128)S(1)} %copy.72), channel_id=1, source_target_pairs={{0,2},{4,6},{8,10},{12,14},{16,18},{20,22},{24,26},{28,30}} | collective-permute-start | bytes 3145736 | tf_op jit(solution)/shard_map/ppermute | solution.py:57
  276.8 17.2 %collective-permute-start.6 = (f32[512,512]{1,0:T(8,128)S(1)}, f32[512,512]{1,0:T(8,128)}, u32[]{:S(2)}, u32[]{:S(2)}) collective-permute-start(f32[512,512]{1,0:T(8,128)S(1)} %get-tuple-element.321), channel_id=1, source_target_pairs={{1,2},{5,6},{9,10},{13,14},{17,18},{21,22},{25,26},{29,30}} | collective-permute-start | bytes 3145736 | tf_op jit(solution)/shard_map/ppermute | solution.py:55
  279.1 122.9 %collective-permute-start.4 = (f32[2048,512]{1,0:T(8,128)}, f32[2048,512]{1,0:T(8,128)}, u32[]{:S(2)}, u32[]{:S(2)}) collective-permute-start(f32[2048,512]{1,0:T(8,128)} %copy-done.5), channel_id=1, source_target_pairs={{0,1},{4,5},{8,9},{12,13},{16,17},{20,21},{24,25},{28,29}} | collective-permute-start | bytes 12582920 | tf_op jit(solution)/shard_map/ppermute | solution.py:30
  280.4 121.6 %collective-permute-start.3 = (f32[2048,512]{1,0:T(8,128)}, f32[2048,512]{1,0:T(8,128)}, u32[]{:S(2)}, u32[]{:S(2)}) collective-permute-start(f32[2048,512]{1,0:T(8,128)} %copy-done.5), channel_id=1, source_target_pairs={{0,2},{4,6},{8,10},{12,14},{16,18},{20,22},{24,26},{28,30}} | collective-permute-start | bytes 12582920 | tf_op jit(solution)/shard_map/ppermute | solution.py:30
  283.0 119.0 %collective-permute-start.2 = (f32[2048,512]{1,0:T(8,128)}, f32[2048,512]{1,0:T(8,128)}, u32[]{:S(2)}, u32[]{:S(2)}) collective-permute-start(f32[2048,512]{1,0:T(8,128)} %copy-done.5), channel_id=1, source_target_pairs={{0,3},{4,7},{8,11},{12,15},{16,19},{20,23},{24,27},{28,31}} | collective-permute-start | bytes 12582920 | tf_op jit(solution)/shard_map/ppermute | solution.py:30
  423.1 67.0 %copy-start = (f32[2048,512]{1,0:T(8,128)}, f32[2048,512]{1,0:T(8,128)S(1)}, u32[]{:S(2)}) copy-start(f32[2048,512]{1,0:T(8,128)S(1)} %fusion.17) | copy-start | bytes 12582916
  423.6 70.7 %copy-start.23 = (f32[256,256]{1,0:T(8,128)S(1)}, f32[256,256]{1,0:T(8,128)}, u32[]{:S(2)}) copy-start(f32[256,256]{1,0:T(8,128)} %copy-done.22) | copy-start | bytes 786436
  423.6 70.7 %copy-start.25 = (f32[256,256]{1,0:T(8,128)S(1)}, f32[256,256]{1,0:T(8,128)}, u32[]{:S(2)}) copy-start(f32[256,256]{1,0:T(8,128)} %copy-done.24) | copy-start | bytes 786436
  423.6 70.7 %copy-start.29 = (f32[128,128]{1,0:T(8,128)S(1)}, f32[128,128]{1,0:T(8,128)}, u32[]{:S(2)}) copy-start(f32[128,128]{1,0:T(8,128)} %copy-done.28) | copy-start | bytes 196612
  423.7 13.2 %collective-permute-start.17 = (f32[512,512]{1,0:T(8,128)S(1)}, f32[512,512]{1,0:T(8,128)S(1)}, u32[]{:S(2)}, u32[]{:S(2)}) collective-permute-start(f32[512,512]{1,0:T(8,128)S(1)} %get-tuple-element.317), channel_id=1, source_target_pairs={{1,0},{5,4},{9,1},{13,5},{17,2},{21,6},{25,3},{29,7}} | collective-permute-start | bytes 3145736 | tf_op jit(solution)/shard_map/ppermute | solution.py:137
  425.1 23.0 %collective-permute-start.16 = (f32[512,512]{1,0:T(8,128)S(1)}, f32[512,512]{1,0:T(8,128)S(1)}, u32[]{:S(2)}, u32[]{:S(2)}) collective-permute-start(f32[512,512]{1,0:T(8,128)S(1)} %get-tuple-element.318), channel_id=1, source_target_pairs={{1,8},{5,12},{9,9},{13,13},{17,10},{21,14},{25,11},{29,15}} | collective-permute-start | bytes 3145736 | tf_op jit(solution)/shard_map/ppermute | solution.py:137
  426.5 32.9 %collective-permute-start.15 = (f32[512,512]{1,0:T(8,128)S(1)}, f32[512,512]{1,0:T(8,128)S(1)}, u32[]{:S(2)}, u32[]{:S(2)}) collective-permute-start(f32[512,512]{1,0:T(8,128)S(1)} %get-tuple-element.319), channel_id=1, source_target_pairs={{1,16},{5,20},{9,17},{13,21},{17,18},{21,22},{25,19},{29,23}} | collective-permute-start | bytes 3145736 | tf_op jit(solution)/shard_map/ppermute | solution.py:137
  427.9 62.2 %collective-permute-start.14 = (f32[512,512]{1,0:T(8,128)S(1)}, f32[512,512]{1,0:T(8,128)S(1)}, u32[]{:S(2)}, u32[]{:S(2)}) collective-permute-start(f32[512,512]{1,0:T(8,128)S(1)} %get-tuple-element.320), channel_id=1, source_target_pairs={{1,24},{5,28},{9,25},{13,29},{17,26},{21,30},{25,27},{29,31}} | collective-permute-start | bytes 3145736 | tf_op jit(solution)/shard_map/ppermute | solution.py:137
  570.3 43.8 %copy-start.26 = (f32[256,256]{0,1:T(8,128)}, f32[256,256]{0,1:T(8,128)S(1)}, u32[]{:S(2)}) copy-start(f32[256,256]{0,1:T(8,128)S(1)} %convolution_subtract_fusion.5) | copy-start | bytes 786436
  587.2 73.0 %collective-permute-start.9 = (f32[2048,512]{1,0:T(8,128)}, f32[2048,512]{1,0:T(8,128)}, u32[]{:S(2)}, u32[]{:S(2)}) collective-permute-start(f32[2048,512]{1,0:T(8,128)} %copy-done), channel_id=1, source_target_pairs={{1,0},{5,4},{9,8},{13,12},{17,16},{21,20},{25,24},{29,28}} | collective-permute-start | bytes 12582920 | tf_op jit(solution)/shard_map/ppermute | solution.py:30
  590.6 69.7 %collective-permute-start.8 = (f32[2048,512]{1,0:T(8,128)}, f32[2048,512]{1,0:T(8,128)}, u32[]{:S(2)}, u32[]{:S(2)}) collective-permute-start(f32[2048,512]{1,0:T(8,128)} %copy-done), channel_id=1, source_target_pairs={{1,2},{5,6},{9,10},{13,14},{17,18},{21,22},{25,26},{29,30}} | collective-permute-start | bytes 12582920 | tf_op jit(solution)/shard_map/ppermute | solution.py:30
  593.8 88.7 %collective-permute-start.7 = (f32[2048,512]{1,0:T(8,128)}, f32[2048,512]{1,0:T(8,128)}, u32[]{:S(2)}, u32[]{:S(2)}) collective-permute-start(f32[2048,512]{1,0:T(8,128)} %copy-done), channel_id=1, source_target_pairs={{1,3},{5,7},{9,11},{13,15},{17,19},{21,23},{25,27},{29,31}} | collective-permute-start | bytes 12582920 | tf_op jit(solution)/shard_map/ppermute | solution.py:30
  632.2 28.0 %copy-start.12 = (f32[512,512]{1,0:T(8,128)}, f32[512,512]{1,0:T(8,128)S(1)}, u32[]{:S(2)}) copy-start(f32[512,512]{1,0:T(8,128)S(1)} %get-tuple-element.324) | copy-start | bytes 3145732
  652.9 29.7 %copy-start.1 = (f32[2048,512]{1,0:T(8,128)S(1)}, f32[2048,512]{1,0:T(8,128)}, u32[]{:S(2)}) copy-start(f32[2048,512]{1,0:T(8,128)} %copy-done) | copy-start | bytes 12582916
  (25 other events, 178.1 us)
Sparse Core Ops, SparseCore 0:
  9.5 72.1 all-gather.3
  274.9 120.8 all-gather.5
  491.9 121.5 all-gather.7
